TPU v7x, 768 devices: a whole 4x8x12 slice. The times are simulated.
768 devices in a mesh: ctx: 96 (over x, z, y_hi), grp: 8 (over y_lo, core).
Axes of the slice: x: 4, y: 8 (y_hi: 2, y_lo: 4; y = y_hi * 4 + y_lo), z: 12, core: 2. Of those that a mesh axis runs over, the one named last changes fastest.
Arguments:
- queries: bfloat16 [122880, 4096], P(('ctx', 'grp')), may hold values from -27 to 27
- keys: bfloat16 [122880, 512], P(('ctx', 'grp')), may hold values from -4.5 to 4.5
- values: bfloat16 [122880, 512], P(('ctx', 'grp')), may hold values from -6 to 6
- lengths: int32 [384], replicated, may hold values from 1 to 640, 122880 in all
- ssmax_scale: float32 [32], replicated, may hold values from 0.3 to 0.9
Outputs:
- attended: bfloat16 [122880, 4096], P(('ctx', 'grp'))
Inputs may be any that keep to these rules, and one draw needn't show every extreme that they name: Every document has 1 to 640 tokens and one has exactly 640; the lengths sum to 122880.
All inputs are finite; a program needn't handle non-finite values.
Results may differ from a plain program's by a relative error of at most 0.0047.
Values may be sent and summed in bfloat16 or wider, within the bound.
No kernel may reach another device: no remote copies, remote signals or barrier semaphores. Data moves between devices by JAX's collectives and lax.ppermute only.
A program may use at most 32 MiB of HBM per device.

v0:
```python
import jax
import jax.numpy as jnp
from jax import lax
from jax.sharding import PartitionSpec as P

HQ = 32
HK = 4
HD = 128
WIN_DEV = 4


def from_behind(x, axis, by):
    count = lax.axis_size(axis)
    pairs = [(i, i + by) for i in range(count) if 0 <= i + by < count]
    return lax.ppermute(x, axis, pairs)


def body(queries, keys, values, lengths, ssmax_scale):
    tok_rows = queries.shape[0]
    slab_rows = tok_rows * lax.axis_size("grp")
    doc_most = WIN_DEV * tok_rows
    win_width = doc_most + tok_rows
    per_group = HQ // HK
    grp_index = lax.axis_index("grp")
    ctx_index = lax.axis_index("ctx")
    q_start = ctx_index * slab_rows + grp_index * tok_rows
    q_pos = q_start + jnp.arange(tok_rows, dtype=jnp.int32)
    own_keys, own_values = (
        lax.all_gather(keys, "grp", axis=0, tiled=True),
        lax.all_gather(values, "grp", axis=0, tiled=True),
    )
    prior_keys, prior_values = from_behind((own_keys, own_values), "ctx", 1)
    joined_keys = jnp.concatenate([prior_keys, own_keys], axis=0)
    joined_values = jnp.concatenate([prior_values, own_values], axis=0)
    win_begin = slab_rows + grp_index * tok_rows - doc_most
    k_window = lax.dynamic_slice_in_dim(joined_keys, win_begin, win_width, 0)
    v_window = lax.dynamic_slice_in_dim(joined_values, win_begin, win_width, 0)
    k_pos = ctx_index * slab_rows - slab_rows + win_begin + jnp.arange(win_width, dtype=jnp.int32)
    totals = jnp.cumsum(lengths, dtype=jnp.int32)
    before = totals[None, :] <= q_pos[:, None]
    doc_start = jnp.sum(jnp.where(before, lengths[None, :], 0), axis=1, dtype=jnp.int32)
    visible = (q_pos - doc_start + 1).astype(jnp.float32)
    score_coef = ssmax_scale[None, :] * jnp.log(visible)[:, None] / jnp.sqrt(jnp.float32(HD))
    live_mask = (k_pos[None, :] >= doc_start[:, None]) & (k_pos[None, :] <= q_pos[:, None])
    pieces = []
    for kv_head in range(HK):
        q_heads = queries[:, kv_head * per_group * HD : (kv_head + 1) * per_group * HD].reshape(
            tok_rows, per_group, HD
        )
        k_head = k_window[:, kv_head * HD : (kv_head + 1) * HD]
        v_head = v_window[:, kv_head * HD : (kv_head + 1) * HD]
        head_coef = score_coef[:, kv_head * per_group : (kv_head + 1) * per_group].T[:, :, None]
        scores = (
            jnp.einsum("igd,jd->gij", q_heads, k_head, preferred_element_type=jnp.float32)
            * head_coef
        )
        scores = jnp.where(live_mask[None], scores, -jnp.inf)
        top_score = jnp.max(scores, axis=-1, keepdims=True)
        probs = jnp.exp(scores - top_score)
        weights = (probs / jnp.sum(probs, axis=-1, keepdims=True)).astype(jnp.bfloat16)
        mixed = jnp.einsum("gij,jd->igd", weights, v_head, preferred_element_type=jnp.float32)
        pieces.append(mixed.reshape(tok_rows, per_group * HD))
    return jnp.concatenate(pieces, axis=1).astype(jnp.bfloat16)


def solution(mesh):
    return jax.shard_map(
        body,
        mesh=mesh,
        in_specs=(
            P(("ctx", "grp"), None),
            P(("ctx", "grp"), None),
            P(("ctx", "grp"), None),
            P(),
            P(),
        ),
        out_specs=P(("ctx", "grp"), None),
        check_vma=False,
    )
```

profile of v0, /device:TPU:118, one launch (start us, length us, event | category | flops | bytes accessed | tf_op | source)
XLA Modules:
  0.0 297.3 jit_solution(2767582242512016206)
XLA Ops:
  6.5 0.7 all-gather.3.cloned.1.call-update
  7.3 0.0 all-gather.5.cloned.1.call-start
  7.3 0.7 all-gather.5.cloned.1.call-update
  8.0 1.0 reduce-window.9
  9.0 0.1 slice.56
  9.1 0.1 slice_reduce_fusion
  9.2 0.1 add_bitcast_fusion
  9.3 42.6 %all-gather.3.cloned.1.call-done = bf16[1280,512]{1,0:T(8,128)(2,1)} async-done(((bf16[160,512]{1,0:T(8,128)(2,1)}), bf16[1280,512]{1,0:T(8,128)(2,1)}) %all-gather.3.cloned.1.call-update) | async-done | bytes 1310736 | tf_op jit(solution)/shard_map/all_gather | solution.py:30
  51.9 6.1 %collective-permute-start = (bf16[1280,512]{1,0:T(8,128)(2,1)}, bf16[1280,512]{1,0:T(8,128)(2,1)S(1)}, u32[]{:S(2)}, u32[]{:S(2)}) collective-permute-start(bf16[1280,512]{1,0:T(8,128)(2,1)} %all-gather.3.cloned.1.call-done), channel_id=1, source_target_pairs={{0,8},{8,16},{16,24},{24,32},{32,40},{40,48},{48,56},{56,64},{64,7... | collective-permute-start | bytes 3932168 | tf_op jit(solution)/shard_map/ppermute | solution.py:15
  58.0 133.1 %all-gather.5.cloned.1.call-done = bf16[1280,512]{1,0:T(8,128)(2,1)} async-done(((bf16[160,512]{1,0:T(8,128)(2,1)}), bf16[1280,512]{1,0:T(8,128)(2,1)}) %all-gather.5.cloned.1.call-update) | async-done | bytes 1310736 | tf_op jit(solution)/shard_map/all_gather | solution.py:29
  191.1 1.9 collective-permute-start.1
  193.0 0.9 select_reduce_fusion
  193.9 0.7 multiply_multiply_fusion
  194.7 0.9 compare_and_fusion
  195.5 2.4 slice_bitcast_fusion.3
  197.9 0.0 collective-permute-done
  197.9 58.5 %collective-permute-done.1 = bf16[1280,512]{1,0:T(8,128)(2,1)S(1)} collective-permute-done((bf16[1280,512]{1,0:T(8,128)(2,1)}, bf16[1280,512]{1,0:T(8,128)(2,1)S(1)}, u32[]{:S(2)}, u32[]{:S(2)}) %collective-permute-start.1) | collective-permute-done | bytes 1310752 | tf_op jit(solution)/shard_map/ppermute | solution.py:15
  256.4 3.5 %fusion.48 = (bf16[800,512]{1,0:T(8,128)(2,1)}, bf16[800,512]{1,0:T(8,128)(2,1)S(1)}) fusion(s32[]{:T(128)S(6)} %select_n.21, bf16[1280,512]{1,0:T(8,128)(2,1)S(1)} %collective-permute-done.1, bf16[1280,512]{1,0:T(8,128)(2,1)} %all-gather.5.cloned.1.call-done, bf16[1280,512]{1,0:T(8,128)(2,1)} %all-gather.3.cloned.1.call-done, ...), kind=kLoop, calls=%fused_computation.53 | loop fusion | flops 3276800 | bytes 6881284 | tf_op jit(solution)/shard_map/concatenate | solution.py:33
  260.0 4.9 %fusion.121 = (f32[8,160]{1,0:T(8,128)S(1)}, f32[8,160,800]{2,1,0:T(8,128)}) fusion(f32[8,160]{1,0:T(8,128)S(1)} %get-tuple-element.9, pred[160,800]{1,0:T(8,128)(4,1)} %compare_and_fusion, bf16[20,8,8,128]{3,2,1,0:T(8,128)(2,1)} %get-tuple-element.5, bf16[800,512]{1,0:T(8,128)(2,1)} %get-tuple-element.21), kind=kOutput, calls=%fused_computation.114 | convolution fusion | flops 266240800 | bytes 4782080 | tf_op jit(solution)/shard_map/sub | solution.py:59
  264.9 3.2 %fusion.44 = bf16[8,20,8,128]{3,2,1,0:T(8,128)(2,1)S(1)} fusion(f32[8,160,800]{2,1,0:T(8,128)} %get-tuple-element.20, f32[8,160]{1,0:T(8,128)S(1)} %get-tuple-element.19, bf16[800,512]{1,0:T(8,128)(2,1)S(1)} %get-tuple-element.22), kind=kOutput, calls=%fused_computation.49 | convolution fusion | flops 264355840 | bytes 4636672 | tf_op jit(solution)/shard_map/gij,jd->igd/dot_general | solution.py:61
  268.1 0.1 copy.101
  268.2 3.8 %fusion.116 = (f32[8,160]{1,0:T(8,128)S(1)}, f32[8,160,800]{2,1,0:T(8,128)}) fusion(f32[8,160]{1,0:T(8,128)S(1)} %get-tuple-element.12, pred[160,800]{1,0:T(8,128)(4,1)S(1)} %copy-done.4, bf16[20,8,8,128]{3,2,1,0:T(8,128)(2,1)S(1)} %copy-done.3, bf16[800,512]{1,0:T(8,128)(2,1)S(1)} %copy-done), kind=kOutput, calls=%fused_computation.113 | convolution fusion | flops 266240800 | bytes 4785152 | tf_op jit(solution)/shard_map/sub | solution.py:59
  272.0 3.2 %fusion.45 = bf16[8,20,8,128]{3,2,1,0:T(8,128)(2,1)S(1)} fusion(f32[8,160,800]{2,1,0:T(8,128)} %get-tuple-element.18, f32[8,160]{1,0:T(8,128)S(1)} %get-tuple-element.17, bf16[800,512]{1,0:T(8,128)(2,1)S(1)} %get-tuple-element.22), kind=kOutput, calls=%fused_computation.50 | convolution fusion | flops 264355840 | bytes 4636672 | tf_op jit(solution)/shard_map/gij,jd->igd/dot_general | solution.py:61
  275.2 0.1 copy.100
  275.2 0.0 copy-done.2
  275.3 3.8 %fusion.111 = (f32[8,160]{1,0:T(8,128)S(1)}, f32[8,160,800]{2,1,0:T(8,128)}) fusion(f32[8,160]{1,0:T(8,128)S(1)} %get-tuple-element.11, pred[160,800]{1,0:T(8,128)(4,1)S(1)} %copy-done.4, bf16[20,8,8,128]{3,2,1,0:T(8,128)(2,1)S(1)} %copy-done.2, bf16[800,512]{1,0:T(8,128)(2,1)S(1)} %copy-done), kind=kOutput, calls=%fused_computation.112 | convolution fusion | flops 266240800 | bytes 4785152 | tf_op jit(solution)/shard_map/sub | solution.py:59
  279.1 3.2 %fusion.46 = bf16[8,20,8,128]{3,2,1,0:T(8,128)(2,1)S(1)} fusion(f32[8,160,800]{2,1,0:T(8,128)} %get-tuple-element.16, f32[8,160]{1,0:T(8,128)S(1)} %get-tuple-element.15, bf16[800,512]{1,0:T(8,128)(2,1)S(1)} %get-tuple-element.22), kind=kOutput, calls=%fused_computation.51 | convolution fusion | flops 264355840 | bytes 4636672 | tf_op jit(solution)/shard_map/gij,jd->igd/dot_general | solution.py:61
  282.2 0.1 copy.99
  282.3 3.8 %fusion.106 = (f32[8,160]{1,0:T(8,128)S(1)}, f32[8,160,800]{2,1,0:T(8,128)}) fusion(f32[8,160]{1,0:T(8,128)S(1)} %get-tuple-element.10, pred[160,800]{1,0:T(8,128)(4,1)S(1)} %copy-done.4, bf16[20,8,8,128]{3,2,1,0:T(8,128)(2,1)S(1)} %copy-done.1, bf16[800,512]{1,0:T(8,128)(2,1)S(1)} %copy-done), kind=kOutput, calls=%fused_computation.111 | convolution fusion | flops 266240800 | bytes 4785152 | tf_op jit(solution)/shard_map/sub | solution.py:59
  286.1 3.1 %fusion.47 = bf16[8,20,8,128]{3,2,1,0:T(8,128)(2,1)S(1)} fusion(f32[8,160,800]{2,1,0:T(8,128)} %get-tuple-element.14, f32[8,160]{1,0:T(8,128)S(1)} %get-tuple-element.13, bf16[800,512]{1,0:T(8,128)(2,1)S(1)} %get-tuple-element.22), kind=kOutput, calls=%fused_computation.52 | convolution fusion | flops 264355840 | bytes 4636672 | tf_op jit(solution)/shard_map/gij,jd->igd/dot_general | solution.py:61
  289.2 0.1 copy.98
  289.3 1.2 pad_maximum_fusion
  (15 shorter events, 0.1 us)
Async XLA Ops:
  6.5 45.4 %all-gather.3.cloned.1.call-start = ((), (), s32[]{:S(2)}) async-start(), calls=%async_computation | async-start | bytes 1474560 | tf_op jit(solution)/shard_map/all_gather | solution.py:30
  7.3 183.8 %all-gather.5.cloned.1.call-start = ((), (), s32[]{:S(2)}) async-start(), calls=%async_computation.1 | async-start | bytes 1474560 | tf_op jit(solution)/shard_map/all_gather | solution.py:29
  51.9 146.0 %collective-permute-start = (bf16[1280,512]{1,0:T(8,128)(2,1)}, bf16[1280,512]{1,0:T(8,128)(2,1)S(1)}, u32[]{:S(2)}, u32[]{:S(2)}) collective-permute-start(bf16[1280,512]{1,0:T(8,128)(2,1)} %all-gather.3.cloned.1.call-done), channel_id=1, source_target_pairs={{0,8},{8,16},{16,24},{24,32},{32,40},{40,48},{48,56},{56,64},{64,7... | collective-permute-start | bytes 3932168 | tf_op jit(solution)/shard_map/ppermute | solution.py:15
  191.1 65.3 %collective-permute-start.1 = (bf16[1280,512]{1,0:T(8,128)(2,1)}, bf16[1280,512]{1,0:T(8,128)(2,1)S(1)}, u32[]{:S(2)}, u32[]{:S(2)}) collective-permute-start(bf16[1280,512]{1,0:T(8,128)(2,1)} %all-gather.5.cloned.1.call-done), channel_id=1, source_target_pairs={{0,8},{8,16},{16,24},{24,32},{32,40},{40,48},{48,56},{56,64},{64,7... | collective-permute-start | bytes 3932168 | tf_op jit(solution)/shard_map/ppermute | solution.py:15
  264.9 3.3 %copy-start = (bf16[800,512]{1,0:T(8,128)(2,1)S(1)}, bf16[800,512]{1,0:T(8,128)(2,1)}, u32[]{:S(2)}) copy-start(bf16[800,512]{1,0:T(8,128)(2,1)} %get-tuple-element.21) | copy-start | bytes 2457604
  264.9 3.3 %copy-start.3 = (bf16[20,8,8,128]{3,2,1,0:T(8,128)(2,1)S(1)}, bf16[20,8,8,128]{3,2,1,0:T(8,128)(2,1)}, u32[]{:S(2)}) copy-start(bf16[20,8,8,128]{3,2,1,0:T(8,128)(2,1)} %get-tuple-element.6) | copy-start | bytes 983044
  264.9 3.3 %copy-start.4 = (pred[160,800]{1,0:T(8,128)(4,1)S(1)}, pred[160,800]{1,0:T(8,128)(4,1)}, u32[]{:S(2)}) copy-start(pred[160,800]{1,0:T(8,128)(4,1)} %compare_and_fusion) | copy-start | bytes 384004
  272.0 3.3 %copy-start.2 = (bf16[20,8,8,128]{3,2,1,0:T(8,128)(2,1)S(1)}, bf16[20,8,8,128]{3,2,1,0:T(8,128)(2,1)}, u32[]{:S(2)}) copy-start(bf16[20,8,8,128]{3,2,1,0:T(8,128)(2,1)} %get-tuple-element.8) | copy-start | bytes 983044
  279.0 3.3 %copy-start.1 = (bf16[20,8,8,128]{3,2,1,0:T(8,128)(2,1)S(1)}, bf16[20,8,8,128]{3,2,1,0:T(8,128)(2,1)}, u32[]{:S(2)}) copy-start(bf16[20,8,8,128]{3,2,1,0:T(8,128)(2,1)} %get-tuple-element.7) | copy-start | bytes 983044
Sparse Core Ops, SparseCore 0:
  9.7 42.1 all-gather.2
  54.3 136.7 all-gather.4
where the time goes:
time: 298 us; the launch traced here: 297 us
  waiting for transfers between devices  236 us (79%)
  matrix products  28.9 us (10%)
  between operations  13.6 us (5%)
  other arithmetic  8.27 us (3%)
  starting transfers between devices  8.02 us (3%)
    all_gather x1, waiting for transfers between devices, body(): lax.all_gather(keys, 'grp', axis=0, tiled=True)  133 us
    ppermute x2, waiting for transfers between devices, from_behind(): return lax.ppermute(x, axis, pairs)  58.5 us
    all_gather x1, waiting for transfers between devices, body(): lax.all_gather(values, 'grp', axis=0, tiled=True)  42.6 us
    sub x4, matrix products, body(): probs = jnp.exp(scores - top_score)  16.3 us
    dot_general x4, matrix products, body(): jnp.einsum('gij,jd->igd', weights, v_head, preferred_element_type=jnp.flo...  12.6 us
    ppermute x2, starting transfers between devices, from_behind(): return lax.ppermute(x, axis, pairs)  7.98 us
  transfers between devices with their start and end apart: 4, of which 3 were waited for; matrix products, arithmetic and copies ran while one was open for 2% of the time, Pallas kernels for 0%

commit v1 on v0

--- a/solution.py
+++ b/solution.py
@@ -7,12 +7,28 @@
 HK = 4
 HD = 128
 WIN_DEV = 4
+AXES = ("ctx", "grp")
 
 
-def from_behind(x, axis, by):
-    count = lax.axis_size(axis)
-    pairs = [(i, i + by) for i in range(count) if 0 <= i + by < count]
-    return lax.ppermute(x, axis, pairs)
+def send(x, pairs):
+    return lax.ppermute(x, AXES, pairs)
+
+
+def window_blocks(own):
+    count = lax.axis_size("ctx") * lax.axis_size("grp")
+    ahead2 = [(i, i + 2) for i in range(count - 2)]
+    to_odd = [(i, i + 1) for i in range(0, count - 1, 2)]
+    to_even = [(i, i - 1) for i in range(1, count, 2)]
+    swap = to_odd + to_even
+    back2 = send(own, ahead2)
+    from_even_own = send(own, to_odd)
+    back4 = send(back2, ahead2)
+    swapped2 = send(back2, swap)
+    from_odd4 = send(back4, to_even)
+    even = lax.axis_index("grp") % 2 == 0
+    back1 = jnp.where(even, swapped2, from_even_own)
+    back3 = jnp.where(even, from_odd4, swapped2)
+    return [back4, back3, back2, back1, own]
 
 
 def body(queries, keys, values, lengths, ssmax_scale):
@@ -25,17 +41,11 @@
     ctx_index = lax.axis_index("ctx")
     q_start = ctx_index * slab_rows + grp_index * tok_rows
     q_pos = q_start + jnp.arange(tok_rows, dtype=jnp.int32)
-    own_keys, own_values = (
-        lax.all_gather(keys, "grp", axis=0, tiled=True),
-        lax.all_gather(values, "grp", axis=0, tiled=True),
-    )
-    prior_keys, prior_values = from_behind((own_keys, own_values), "ctx", 1)
-    joined_keys = jnp.concatenate([prior_keys, own_keys], axis=0)
-    joined_values = jnp.concatenate([prior_values, own_values], axis=0)
-    win_begin = slab_rows + grp_index * tok_rows - doc_most
-    k_window = lax.dynamic_slice_in_dim(joined_keys, win_begin, win_width, 0)
-    v_window = lax.dynamic_slice_in_dim(joined_values, win_begin, win_width, 0)
-    k_pos = ctx_index * slab_rows - slab_rows + win_begin + jnp.arange(win_width, dtype=jnp.int32)
+    own = jnp.concatenate([keys, values], axis=1)
+    window = jnp.concatenate(window_blocks(own), axis=0)
+    k_window = window[:, : HK * HD]
+    v_window = window[:, HK * HD :]
+    k_pos = q_start - doc_most + jnp.arange(win_width, dtype=jnp.int32)
     totals = jnp.cumsum(lengths, dtype=jnp.int32)
     before = totals[None, :] <= q_pos[:, None]
     doc_start = jnp.sum(jnp.where(before, lengths[None, :], 0), axis=1, dtype=jnp.int32)
@@ -68,12 +78,12 @@
         body,
         mesh=mesh,
         in_specs=(
-            P(("ctx", "grp"), None),
-            P(("ctx", "grp"), None),
-            P(("ctx", "grp"), None),
+            P(AXES, None),
+            P(AXES, None),
+            P(AXES, None),
             P(),
             P(),
         ),
-        out_specs=P(("ctx", "grp"), None),
+        out_specs=P(AXES, None),
         check_vma=False,
     )

time: 298 us -> 80.1 us (0.27)
  the two profiles are of different devices: /device:TPU:118 before, /device:TPU:7 now
where the time goes in v1:
time: 80.1 us; the launch traced here: 79.6 us
  matrix products  29.8 us (37%)
  waiting for transfers between devices  25.7 us (32%)
  starting transfers between devices  14.7 us (18%)
  local copies, waits for them, and re-layouts  4.9 us (6%)
  other arithmetic  4.25 us (5%)
    ppermute x5, waiting for transfers between devices, send(): return lax.ppermute(x, AXES, pairs)  25.7 us
    sub x4, matrix products, body(): probs = jnp.exp(scores - top_score)  17 us
    ppermute x5, starting transfers between devices, send(): return lax.ppermute(x, AXES, pairs)  14.7 us
    dot_general x4, matrix products, body(): jnp.einsum('gij,jd->igd', weights, v_head, preferred_element_type=jnp.flo...  12.8 us
    unnamed x13, local copies, waits for them, and re-layouts  3.61 us
  transfers between devices with their start and end apart: 5, of which 3 were waited for; matrix products, arithmetic and copies ran while one was open for 6% of the time, Pallas kernels for 0%

profile of v1, /device:TPU:7, one launch (start us, length us, event | category | flops | bytes accessed | tf_op | source)
XLA Modules:
  0.0 79.6 jit_solution(17855390008709516551)
XLA Ops:
  0.0 0.9 %constant_dynamic-update-slice_fusion.1 = bf16[160,1024]{1,0:T(8,128)(2,1)S(1)} fusion(bf16[160,512]{1,0:T(8,128)(2,1)} %param.6), kind=kLoop, calls=%fused_computation.95 | loop fusion | bytes 327680
  0.9 0.9 %constant_dynamic-update-slice_fusion = bf16[160,1024]{1,0:T(8,128)(2,1)S(1)} fusion(bf16[160,1024]{1,0:T(8,128)(2,1)S(1)} %constant_dynamic-update-slice_fusion.1, bf16[160,512]{1,0:T(8,128)(2,1)} %param.7), kind=kLoop, calls=%fused_computation.94 | loop fusion | bytes 327680 | tf_op jit(solution)/shard_map/concatenate | solution.py:44
  1.9 1.3 %collective-permute-start.4 = (bf16[160,1024]{1,0:T(8,128)(2,1)S(1)}, bf16[160,1024]{1,0:T(8,128)(2,1)S(1)}, u32[]{:S(2)}, u32[]{:S(2)}) collective-permute-start(bf16[160,1024]{1,0:T(8,128)(2,1)S(1)} %constant_dynamic-update-slice_fusion), channel_id=1, source_target_pairs={{0,1},{2,3},{4,5},{6,7},{8,9},{10,11},{12,13},{14,15},{16,17},{18,... | collective-permute-start | bytes 983048 | tf_op jit(solution)/shard_map/ppermute | solution.py:14
  3.2 3.2 %collective-permute-start = (bf16[160,1024]{1,0:T(8,128)(2,1)S(1)}, bf16[160,1024]{1,0:T(8,128)(2,1)S(1)}, u32[]{:S(2)}, u32[]{:S(2)}) collective-permute-start(bf16[160,1024]{1,0:T(8,128)(2,1)S(1)} %constant_dynamic-update-slice_fusion), channel_id=1, source_target_pairs={{0,2},{1,3},{2,4},{3,5},{4,6},{5,7},{6,8},{7,9},{8,10},{9,11},{10,... | collective-permute-start | bytes 983048 | tf_op jit(solution)/shard_map/ppermute | solution.py:14
  6.4 1.0 %reduce-window.9 = s32[3,128]{1,0:T(4,128)S(1)} reduce-window(s32[3,128]{1,0:T(4,128)} %bitcast.195, s32[]{:T(128)} %constant.16.clone.1), window={size=1x128 pad=0_0x127_0}, to_apply=%region_0.1 | reduce-window | flops 48768 | bytes 3076 | tf_op jit(solution)/shard_map/reduce-window
  7.4 0.1 slice.66
  7.5 0.1 slice_reduce_fusion
  7.6 0.1 add_bitcast_fusion
  7.7 0.9 %select_reduce_fusion = s32[160]{0:T(256)S(1)} fusion(s32[384]{0:T(512)} %param.8, s32[384]{0:T(512)S(1)} %add_bitcast_fusion, s32[160]{0:T(256)S(1)} %iota_add_fusion.1), kind=kLoop, calls=%fused_computation.84 | loop fusion | flops 184160 | bytes 4352 | tf_op jit(solution)/shard_map/reduce_sum | solution.py:51
  8.6 0.2 compare_and_fusion
  8.8 18.8 %collective-permute-done = bf16[160,1024]{1,0:T(8,128)(2,1)S(1)} collective-permute-done((bf16[160,1024]{1,0:T(8,128)(2,1)S(1)}, bf16[160,1024]{1,0:T(8,128)(2,1)S(1)}, u32[]{:S(2)}, u32[]{:S(2)}) %collective-permute-start) | collective-permute-done | bytes 327712 | tf_op jit(solution)/shard_map/ppermute | solution.py:14
  27.5 1.9 %collective-permute-start.1 = (bf16[160,1024]{1,0:T(8,128)(2,1)S(1)}, bf16[160,1024]{1,0:T(8,128)(2,1)S(1)}, u32[]{:S(2)}, u32[]{:S(2)}) collective-permute-start(bf16[160,1024]{1,0:T(8,128)(2,1)S(1)} %collective-permute-done), channel_id=1, source_target_pairs={{0,2},{1,3},{2,4},{3,5},{4,6},{5,7},{6,8},{7,9},{8,10},{9,11},{10,... | collective-permute-start | bytes 983048 | tf_op jit(solution)/shard_map/ppermute | solution.py:14
  29.5 0.7 multiply_multiply_fusion
  30.2 1.4 %slice_bitcast_fusion.3 = (bf16[20,8,8,128]{3,2,1,0:T(8,128)(2,1)S(1)}, bf16[20,8,8,128]{3,2,1,0:T(8,128)(2,1)S(1)}, bf16[20,8,8,128]{3,2,1,0:T(8,128)(2,1)S(1)}, bf16[20,8,8,128]{3,2,1,0:T(8,128)(2,1)S(1)}) fusion(bf16[160,4096]{1,0:T(8,128)(2,1)} %param.5), kind=kLoop, calls=%fused_computation.73 | loop fusion | bytes 2621440
  31.6 3.7 %collective-permute-start.3 = (bf16[160,1024]{1,0:T(8,128)(2,1)S(1)}, bf16[160,1024]{1,0:T(8,128)(2,1)S(1)}, u32[]{:S(2)}, u32[]{:S(2)}) collective-permute-start(bf16[160,1024]{1,0:T(8,128)(2,1)S(1)} %collective-permute-done), channel_id=1, source_target_pairs={{0,1},{2,3},{4,5},{6,7},{8,9},{10,11},{12,13},{14,15},{16,17},{18,... | collective-permute-start | bytes 983048 | tf_op jit(solution)/shard_map/ppermute | solution.py:14
  35.3 5.8 %collective-permute-done.1 = bf16[160,1024]{1,0:T(8,128)(2,1)S(1)} collective-permute-done((bf16[160,1024]{1,0:T(8,128)(2,1)S(1)}, bf16[160,1024]{1,0:T(8,128)(2,1)S(1)}, u32[]{:S(2)}, u32[]{:S(2)}) %collective-permute-start.1) | collective-permute-done | bytes 327712 | tf_op jit(solution)/shard_map/ppermute | solution.py:14
  41.1 4.6 %collective-permute-start.2 = (bf16[160,1024]{1,0:T(8,128)(2,1)S(1)}, bf16[160,1024]{1,0:T(8,128)(2,1)S(1)}, u32[]{:S(2)}, u32[]{:S(2)}) collective-permute-start(bf16[160,1024]{1,0:T(8,128)(2,1)S(1)} %collective-permute-done.1), channel_id=1, source_target_pairs={{1,0},{3,2},{5,4},{7,6},{9,8},{11,10},{13,12},{15,14},{17,16},{19,... | collective-permute-start | bytes 983048 | tf_op jit(solution)/shard_map/ppermute | solution.py:14
  45.7 1.2 %collective-permute-done.2 = bf16[160,1024]{1,0:T(8,128)(2,1)S(1)} collective-permute-done((bf16[160,1024]{1,0:T(8,128)(2,1)S(1)}, bf16[160,1024]{1,0:T(8,128)(2,1)S(1)}, u32[]{:S(2)}, u32[]{:S(2)}) %collective-permute-start.2) | collective-permute-done | bytes 327712 | tf_op jit(solution)/shard_map/ppermute | solution.py:14
  46.9 0.1 select_dynamic-update-slice_fusion.1
  47.0 0.1 select_dynamic-update-slice_fusion
  47.2 1.2 %copy-done.2 = bf16[800,1024]{1,0:T(8,128)(2,1)} copy-done((bf16[800,1024]{1,0:T(8,128)(2,1)}, bf16[800,1024]{1,0:T(8,128)(2,1)S(1)}, u32[]{:S(2)}) %copy-start.2) | copy-done | bytes 1638424
  48.4 4.7 %fusion.104 = (f32[8,160]{1,0:T(8,128)S(1)}, f32[8,160,800]{2,1,0:T(8,128)}) fusion(f32[8,160]{1,0:T(8,128)S(1)} %get-tuple-element.10, pred[160,800]{1,0:T(8,128)(4,1)S(1)} %compare_and_fusion, bf16[20,8,8,128]{3,2,1,0:T(8,128)(2,1)S(1)} %get-tuple-element.7, bf16[800,1024]{1,0:T(8,128)(2,1)} %copy-done.2), kind=kOutput, calls=%fused_computation.113 | convolution fusion | flops 266240800 | bytes 4766720 | tf_op jit(solution)/shard_map/sub | solution.py:69
  53.1 3.2 %fusion.47 = bf16[8,20,8,128]{3,2,1,0:T(8,128)(2,1)S(1)} fusion(f32[8,160,800]{2,1,0:T(8,128)} %get-tuple-element.14, f32[8,160]{1,0:T(8,128)S(1)} %get-tuple-element.13, bf16[800,1024]{1,0:T(8,128)(2,1)} %copy-done.2), kind=kOutput, calls=%fused_computation.48 | convolution fusion | flops 264355840 | bytes 5125120 | tf_op jit(solution)/shard_map/gij,jd->igd/dot_general | solution.py:71
  56.4 4.7 %fusion.109 = (f32[8,160]{1,0:T(8,128)S(1)}, f32[8,160,800]{2,1,0:T(8,128)}) fusion(f32[8,160]{1,0:T(8,128)S(1)} %get-tuple-element.11, pred[160,800]{1,0:T(8,128)(4,1)S(1)} %compare_and_fusion, bf16[20,8,8,128]{3,2,1,0:T(8,128)(2,1)S(1)} %get-tuple-element.8, bf16[800,1024]{1,0:T(8,128)(2,1)} %copy-done.2), kind=kOutput, calls=%fused_computation.114 | convolution fusion | flops 266240800 | bytes 4766720 | tf_op jit(solution)/shard_map/sub | solution.py:69
  61.1 3.3 %fusion.46 = bf16[8,20,8,128]{3,2,1,0:T(8,128)(2,1)S(1)} fusion(f32[8,160,800]{2,1,0:T(8,128)} %get-tuple-element.16, f32[8,160]{1,0:T(8,128)S(1)} %get-tuple-element.15, bf16[800,1024]{1,0:T(8,128)(2,1)} %copy-done.2), kind=kOutput, calls=%fused_computation.47 | convolution fusion | flops 264355840 | bytes 5125120 | tf_op jit(solution)/shard_map/gij,jd->igd/dot_general | solution.py:71
  64.5 0.1 copy_bitcast_fusion
  64.6 3.8 %fusion.114 = (f32[8,160]{1,0:T(8,128)S(1)}, f32[8,160,800]{2,1,0:T(8,128)}) fusion(f32[8,160]{1,0:T(8,128)S(1)} %get-tuple-element.12, pred[160,800]{1,0:T(8,128)(4,1)S(1)} %compare_and_fusion, bf16[20,8,8,128]{3,2,1,0:T(8,128)(2,1)S(1)} %get-tuple-element.6, bf16[800,1024]{1,0:T(8,128)(2,1)S(1)} %copy-done.3), kind=kOutput, calls=%fused_computation.115 | convolution fusion | flops 266240800 | bytes 4785152 | tf_op jit(solution)/shard_map/sub | solution.py:69
  68.3 3.1 %fusion.45 = bf16[8,20,8,128]{3,2,1,0:T(8,128)(2,1)S(1)} fusion(f32[8,160,800]{2,1,0:T(8,128)} %get-tuple-element.18, f32[8,160]{1,0:T(8,128)S(1)} %get-tuple-element.17, bf16[800,1024]{1,0:T(8,128)(2,1)S(1)} %copy-done.3), kind=kOutput, calls=%fused_computation.46 | convolution fusion | flops 264355840 | bytes 4636672 | tf_op jit(solution)/shard_map/gij,jd->igd/dot_general | solution.py:71
  71.5 3.8 %fusion.119 = (f32[8,160]{1,0:T(8,128)S(1)}, f32[8,160,800]{2,1,0:T(8,128)}) fusion(f32[8,160]{1,0:T(8,128)S(1)} %get-tuple-element.9, pred[160,800]{1,0:T(8,128)(4,1)S(1)} %compare_and_fusion, bf16[20,8,8,128]{3,2,1,0:T(8,128)(2,1)S(1)} %get-tuple-element.5, bf16[800,1024]{1,0:T(8,128)(2,1)S(1)} %copy-done.3), kind=kOutput, calls=%fused_computation.116 | convolution fusion | flops 266240800 | bytes 4785152 | tf_op jit(solution)/shard_map/sub | solution.py:69
  75.3 3.1 %fusion.44 = bf16[8,20,8,128]{3,2,1,0:T(8,128)(2,1)S(1)} fusion(f32[8,160,800]{2,1,0:T(8,128)} %get-tuple-element.20, f32[8,160]{1,0:T(8,128)S(1)} %get-tuple-element.19, bf16[800,1024]{1,0:T(8,128)(2,1)S(1)} %copy-done.3), kind=kOutput, calls=%fused_computation.45 | convolution fusion | flops 264355840 | bytes 4636672 | tf_op jit(solution)/shard_map/gij,jd->igd/dot_general | solution.py:71
  78.4 0.1 copy_bitcast_fusion.2
  78.5 1.2 %pad_maximum_fusion = bf16[160,4096]{1,0:T(8,128)(2,1)} fusion(bf16[160,1024]{1,0:T(8,128)(2,1)S(1)} %get-tuple-element.21, bf16[160,1024]{1,0:T(8,128)(2,1)S(1)} %get-tuple-element.22, bf16[160,1024]{1,0:T(8,128)(2,1)S(1)} %get-tuple-element.23, bf16[160,1024]{1,0:T(8,128)(2,1)S(1)} %get-tuple-element.24), kind=kLoop, calls=%fused_computation.40 | loop fusion | flops 5242880 | bytes 2621440 | tf_op jit(solution)/shard_map/concatenate | solution.py:73
  (18 shorter events, 0.2 us)
Async XLA Ops:
  1.9 45.2 %collective-permute-start.4 = (bf16[160,1024]{1,0:T(8,128)(2,1)S(1)}, bf16[160,1024]{1,0:T(8,128)(2,1)S(1)}, u32[]{:S(2)}, u32[]{:S(2)}) collective-permute-start(bf16[160,1024]{1,0:T(8,128)(2,1)S(1)} %constant_dynamic-update-slice_fusion), channel_id=1, source_target_pairs={{0,1},{2,3},{4,5},{6,7},{8,9},{10,11},{12,13},{14,15},{16,17},{18,... | collective-permute-start | bytes 983048 | tf_op jit(solution)/shard_map/ppermute | solution.py:14
  3.2 24.4 %collective-permute-start = (bf16[160,1024]{1,0:T(8,128)(2,1)S(1)}, bf16[160,1024]{1,0:T(8,128)(2,1)S(1)}, u32[]{:S(2)}, u32[]{:S(2)}) collective-permute-start(bf16[160,1024]{1,0:T(8,128)(2,1)S(1)} %constant_dynamic-update-slice_fusion), channel_id=1, source_target_pairs={{0,2},{1,3},{2,4},{3,5},{4,6},{5,7},{6,8},{7,9},{8,10},{9,11},{10,... | collective-permute-start | bytes 983048 | tf_op jit(solution)/shard_map/ppermute | solution.py:14
  27.5 13.5 %collective-permute-start.1 = (bf16[160,1024]{1,0:T(8,128)(2,1)S(1)}, bf16[160,1024]{1,0:T(8,128)(2,1)S(1)}, u32[]{:S(2)}, u32[]{:S(2)}) collective-permute-start(bf16[160,1024]{1,0:T(8,128)(2,1)S(1)} %collective-permute-done), channel_id=1, source_target_pairs={{0,2},{1,3},{2,4},{3,5},{4,6},{5,7},{6,8},{7,9},{8,10},{9,11},{10,... | collective-permute-start | bytes 983048 | tf_op jit(solution)/shard_map/ppermute | solution.py:14
  30.2 17.0 %copy-start = (bf16[160,512]{1,0:T(8,128)(2,1)S(1)}, bf16[160,512]{1,0:T(8,128)(2,1)}, u32[]{:S(2)}) copy-start(bf16[160,512]{1,0:T(8,128)(2,1)} %param.6) | copy-start | bytes 491524
  30.2 17.0 %copy-start.1 = (bf16[160,512]{1,0:T(8,128)(2,1)S(1)}, bf16[160,512]{1,0:T(8,128)(2,1)}, u32[]{:S(2)}) copy-start(bf16[160,512]{1,0:T(8,128)(2,1)} %param.7) | copy-start | bytes 491524
  31.6 14.1 %collective-permute-start.3 = (bf16[160,1024]{1,0:T(8,128)(2,1)S(1)}, bf16[160,1024]{1,0:T(8,128)(2,1)S(1)}, u32[]{:S(2)}, u32[]{:S(2)}) collective-permute-start(bf16[160,1024]{1,0:T(8,128)(2,1)S(1)} %collective-permute-done), channel_id=1, source_target_pairs={{0,1},{2,3},{4,5},{6,7},{8,9},{10,11},{12,13},{14,15},{16,17},{18,... | collective-permute-start | bytes 983048 | tf_op jit(solution)/shard_map/ppermute | solution.py:14
  41.1 5.8 %collective-permute-start.2 = (bf16[160,1024]{1,0:T(8,128)(2,1)S(1)}, bf16[160,1024]{1,0:T(8,128)(2,1)S(1)}, u32[]{:S(2)}, u32[]{:S(2)}) collective-permute-start(bf16[160,1024]{1,0:T(8,128)(2,1)S(1)} %collective-permute-done.1), channel_id=1, source_target_pairs={{1,0},{3,2},{5,4},{7,6},{9,8},{11,10},{13,12},{15,14},{17,16},{19,... | collective-permute-start | bytes 983048 | tf_op jit(solution)/shard_map/ppermute | solution.py:14
  47.2 1.2 %copy-start.2 = (bf16[800,1024]{1,0:T(8,128)(2,1)}, bf16[800,1024]{1,0:T(8,128)(2,1)S(1)}, u32[]{:S(2)}) copy-start(bf16[800,1024]{1,0:T(8,128)(2,1)S(1)} %constant_dynamic-update-slice_fusion.5) | copy-start | bytes 4915204
  61.1 3.4 %copy-start.3 = (bf16[800,1024]{1,0:T(8,128)(2,1)S(1)}, bf16[800,1024]{1,0:T(8,128)(2,1)}, u32[]{:S(2)}) copy-start(bf16[800,1024]{1,0:T(8,128)(2,1)} %copy-done.2) | copy-start | bytes 4915204

commit v2 on v1

v2 whole, which is shorter than its diff:
```python
import jax
import jax.numpy as jnp
from jax import lax
from jax.experimental import pallas as pl
from jax.experimental.pallas import tpu as pltpu
from jax.sharding import PartitionSpec as P

HQ = 32
HK = 4
HD = 128
WIN_DEV = 4
AXES = ("ctx", "grp")


def send(x, pairs):
    return lax.ppermute(x, AXES, pairs)


def window_blocks(own):
    count = lax.axis_size("ctx") * lax.axis_size("grp")
    ahead2 = [(i, i + 2) for i in range(count - 2)]
    to_odd = [(i, i + 1) for i in range(0, count - 1, 2)]
    to_even = [(i, i - 1) for i in range(1, count, 2)]
    swap = to_odd + to_even
    back2 = send(own, ahead2)
    from_even_own = send(own, to_odd)
    back4 = send(back2, ahead2)
    swapped2 = send(back2, swap)
    from_odd4 = send(back4, to_even)
    even = lax.axis_index("grp") % 2 == 0
    back1 = jnp.where(even, swapped2, from_even_own)
    back3 = jnp.where(even, from_odd4, swapped2)
    return [back4, back3, back2, back1, own]


def attend_kernel(coef_ref, lo_ref, q_ref, k_ref, v_ref, o_ref):
    rows, width = q_ref.shape[0], k_ref.shape[0]
    doc_most = width - rows
    col = lax.broadcasted_iota(jnp.int32, (rows, width), 1)
    row = lax.broadcasted_iota(jnp.int32, (rows, width), 0)
    live = (col >= lo_ref[...]) & (col <= row + doc_most)
    k = k_ref[...]
    v = v_ref[...]
    for g in range(HQ // HK):
        q = q_ref[:, g * HD : (g + 1) * HD]
        s = lax.dot_general(q, k, (((1,), (1,)), ((), ())), preferred_element_type=jnp.float32)
        s = jnp.where(live, s * coef_ref[g], -jnp.inf)
        m = jnp.max(s, axis=1, keepdims=True)
        p = jnp.exp(s - m)
        l = jnp.sum(p, axis=1, keepdims=True)
        w = (p / l).astype(jnp.bfloat16)
        o = jnp.dot(w, v, preferred_element_type=jnp.float32)
        o_ref[:, g * HD : (g + 1) * HD] = o.astype(o_ref.dtype)


def attend(queries, window, coef, lo, interpret=False):
    rows = queries.shape[0]
    width = window.shape[0]
    per_group = HQ // HK
    flops = 4 * HQ * rows * width * HD
    return pl.pallas_call(
        attend_kernel,
        grid=(HK,),
        in_specs=[
            pl.BlockSpec((per_group, rows, 1), lambda h: (h, 0, 0)),
            pl.BlockSpec((rows, 1), lambda h: (0, 0)),
            pl.BlockSpec((rows, per_group * HD), lambda h: (0, h)),
            pl.BlockSpec((width, HD), lambda h: (0, h)),
            pl.BlockSpec((width, HD), lambda h: (0, h + HK)),
        ],
        out_specs=pl.BlockSpec((rows, per_group * HD), lambda h: (0, h)),
        out_shape=jax.ShapeDtypeStruct((rows, HQ * HD), jnp.bfloat16),
        cost_estimate=pl.CostEstimate(
            flops=flops,
            transcendentals=HQ * rows * width,
            bytes_accessed=2 * (2 * rows * HQ * HD + width * 2 * HK * HD),
        ),
        interpret=interpret,
    )(coef, lo, queries, window, window)


def body(queries, keys, values, lengths, ssmax_scale):
    tok_rows = queries.shape[0]
    slab_rows = tok_rows * lax.axis_size("grp")
    doc_most = WIN_DEV * tok_rows
    grp_index = lax.axis_index("grp")
    ctx_index = lax.axis_index("ctx")
    q_start = ctx_index * slab_rows + grp_index * tok_rows
    q_pos = q_start + jnp.arange(tok_rows, dtype=jnp.int32)
    own = jnp.concatenate([keys, values], axis=1)
    window = jnp.concatenate(window_blocks(own), axis=0)
    totals = jnp.cumsum(lengths, dtype=jnp.int32)
    before = totals[None, :] <= q_pos[:, None]
    doc_start = jnp.sum(jnp.where(before, lengths[None, :], 0), axis=1, dtype=jnp.int32)
    visible = (q_pos - doc_start + 1).astype(jnp.float32)
    score_coef = ssmax_scale[None, :] * jnp.log(visible)[:, None] / jnp.sqrt(jnp.float32(HD))
    lo = (doc_start - (q_start - doc_most))[:, None]
    return attend(queries, window, score_coef.T[:, :, None], lo)


def solution(mesh):
    return jax.shard_map(
        body,
        mesh=mesh,
        in_specs=(
            P(AXES, None),
            P(AXES, None),
            P(AXES, None),
            P(),
            P(),
        ),
        out_specs=P(AXES, None),
        check_vma=False,
    )
```

time: 80.1 us -> 69.1 us (0.86)
  matrix products: 29.8 us -> 0 us
  Pallas kernels: 0 us -> 18.3 us
    pallas_call x0 -> x1, Pallas kernels: none -> 18.3 us  [attend(): pl.pallas_call(attend_kernel, grid=(HK,), in_specs=[pl.BlockSpec((per_gro...]
    sub x4 -> x0, matrix products: 17 us -> none  [body(): probs = jnp.exp(scores - top_score)]
    dot_general x4 -> x0, matrix products: 12.8 us -> none  [body(): jnp.einsum('gij,jd->igd', weights, v_head, preferred_element_type=jnp.flo...]
    div x1, other arithmetic: 0.73 us -> 2.63 us  [body(): ssmax_scale[None, :] * jnp.log(visible)[:, None] / jnp.sqrt(jnp.float32(HD))]
    concatenate x1 -> x0, other arithmetic: 1.16 us -> none  [body(): return jnp.concatenate(pieces, axis=1).astype(jnp.bfloat16)]
    unnamed x13 -> x10, local copies, waits for them, and re-layouts: 3.61 us -> 2.83 us
  transfers between devices with their start and end apart: 5 -> 5, of which waited for: 3 -> 2; matrix products, arithmetic and copies ran while one was open for 6% -> 8% of each run, Pallas kernels for 0% -> 0%
where the time goes in v2:
time: 69.1 us; the launch traced here: 68.8 us
  waiting for transfers between devices  26.2 us (38%)
  Pallas kernels  18.3 us (26%)
  starting transfers between devices  14.7 us (21%)
  other arithmetic  4.81 us (7%)
  local copies, waits for them, and re-layouts  4.71 us (7%)
    ppermute x5, waiting for transfers between devices, send(): return lax.ppermute(x, AXES, pairs)  26.2 us
    pallas_call x1, Pallas kernels, attend(): pl.pallas_call(attend_kernel, grid=(HK,), in_specs=[pl.BlockSpec((per_gro...  18.3 us
    ppermute x5, starting transfers between devices, send(): return lax.ppermute(x, AXES, pairs)  14.7 us
    unnamed x10, local copies, waits for them, and re-layouts  2.83 us
    div x1, other arithmetic, body(): ssmax_scale[None, :] * jnp.log(visible)[:, None] / jnp.sqrt(jnp.float32(HD))  2.63 us
  transfers between devices with their start and end apart: 5, of which 2 were waited for; matrix products, arithmetic and copies ran while one was open for 8% of the time, Pallas kernels for 0%

profile of v2, /device:TPU:7, one launch (start us, length us, event | category | flops | bytes accessed | tf_op | source)
XLA Modules:
  0.0 68.8 jit_solution(9016562779732782165)
XLA Ops:
  0.0 0.9 %constant_dynamic-update-slice_fusion.1 = bf16[160,1024]{1,0:T(8,128)(2,1)S(1)} fusion(bf16[160,512]{1,0:T(8,128)(2,1)} %param.6), kind=kLoop, calls=%fused_computation.5 | loop fusion | bytes 327680
  0.9 0.9 %constant_dynamic-update-slice_fusion = bf16[160,1024]{1,0:T(8,128)(2,1)S(1)} fusion(bf16[160,1024]{1,0:T(8,128)(2,1)S(1)} %constant_dynamic-update-slice_fusion.1, bf16[160,512]{1,0:T(8,128)(2,1)} %param.7), kind=kLoop, calls=%fused_computation.4 | loop fusion | bytes 327680 | tf_op jit(solution)/shard_map/concatenate | solution.py:90
  1.9 1.3 %collective-permute-start.4 = (bf16[160,1024]{1,0:T(8,128)(2,1)S(1)}, bf16[160,1024]{1,0:T(8,128)(2,1)S(1)}, u32[]{:S(2)}, u32[]{:S(2)}) collective-permute-start(bf16[160,1024]{1,0:T(8,128)(2,1)S(1)} %constant_dynamic-update-slice_fusion), channel_id=1, source_target_pairs={{0,1},{2,3},{4,5},{6,7},{8,9},{10,11},{12,13},{14,15},{16,17},{18,... | collective-permute-start | bytes 983048 | tf_op jit(solution)/shard_map/ppermute | solution.py:16
  3.2 3.2 %collective-permute-start = (bf16[160,1024]{1,0:T(8,128)(2,1)S(1)}, bf16[160,1024]{1,0:T(8,128)(2,1)S(1)}, u32[]{:S(2)}, u32[]{:S(2)}) collective-permute-start(bf16[160,1024]{1,0:T(8,128)(2,1)S(1)} %constant_dynamic-update-slice_fusion), channel_id=1, source_target_pairs={{0,2},{1,3},{2,4},{3,5},{4,6},{5,7},{6,8},{7,9},{8,10},{9,11},{10,... | collective-permute-start | bytes 983048 | tf_op jit(solution)/shard_map/ppermute | solution.py:16
  6.4 1.0 %reduce-window.9 = s32[3,128]{1,0:T(4,128)S(1)} reduce-window(s32[3,128]{1,0:T(4,128)} %bitcast.4, s32[]{:T(128)} %constant.31.clone.1), window={size=1x128 pad=0_0x127_0}, to_apply=%region_0.1 | reduce-window | flops 48768 | bytes 3076 | tf_op jit(solution)/shard_map/reduce-window
  7.4 0.1 slice.7
  7.5 0.1 slice_reduce_fusion
  7.6 0.1 add_bitcast_fusion
  7.7 0.9 %select_reduce_fusion = s32[160]{0:T(256)S(1)} fusion(s32[384]{0:T(512)} %param.8, s32[384]{0:T(512)S(1)} %add_bitcast_fusion, s32[160]{0:T(256)S(1)} %iota_add_fusion), kind=kLoop, calls=%fused_computation.3 | loop fusion | flops 184160 | bytes 4352 | tf_op jit(solution)/shard_map/reduce_sum | solution.py:94
  8.6 19.0 %collective-permute-done = bf16[160,1024]{1,0:T(8,128)(2,1)S(1)} collective-permute-done((bf16[160,1024]{1,0:T(8,128)(2,1)S(1)}, bf16[160,1024]{1,0:T(8,128)(2,1)S(1)}, u32[]{:S(2)}, u32[]{:S(2)}) %collective-permute-start) | collective-permute-done | bytes 327712 | tf_op jit(solution)/shard_map/ppermute | solution.py:16
  27.5 1.9 %collective-permute-start.1 = (bf16[160,1024]{1,0:T(8,128)(2,1)S(1)}, bf16[160,1024]{1,0:T(8,128)(2,1)S(1)}, u32[]{:S(2)}, u32[]{:S(2)}) collective-permute-start(bf16[160,1024]{1,0:T(8,128)(2,1)S(1)} %collective-permute-done), channel_id=1, source_target_pairs={{0,2},{1,3},{2,4},{3,5},{4,6},{5,7},{6,8},{7,9},{8,10},{9,11},{10,... | collective-permute-start | bytes 983048 | tf_op jit(solution)/shard_map/ppermute | solution.py:16
  29.5 0.7 %copy.9.lo_ref = s32[160,1]{1,0:T(8,128)} copy(s32[160,1]{0,1:T(1,128)S(1)} %bitcast.5) | data formatting | bytes 1280 | tf_op jit(solution)/shard_map/sub | solution.py:97
  30.2 3.7 %collective-permute-start.3 = (bf16[160,1024]{1,0:T(8,128)(2,1)S(1)}, bf16[160,1024]{1,0:T(8,128)(2,1)S(1)}, u32[]{:S(2)}, u32[]{:S(2)}) collective-permute-start(bf16[160,1024]{1,0:T(8,128)(2,1)S(1)} %collective-permute-done), channel_id=1, source_target_pairs={{0,1},{2,3},{4,5},{6,7},{8,9},{10,11},{12,13},{14,15},{16,17},{18,... | collective-permute-start | bytes 983048 | tf_op jit(solution)/shard_map/ppermute | solution.py:16
  33.9 7.2 %collective-permute-done.1 = bf16[160,1024]{1,0:T(8,128)(2,1)S(1)} collective-permute-done((bf16[160,1024]{1,0:T(8,128)(2,1)S(1)}, bf16[160,1024]{1,0:T(8,128)(2,1)S(1)}, u32[]{:S(2)}, u32[]{:S(2)}) %collective-permute-start.1) | collective-permute-done | bytes 327712 | tf_op jit(solution)/shard_map/ppermute | solution.py:16
  41.1 4.6 %collective-permute-start.2 = (bf16[160,1024]{1,0:T(8,128)(2,1)S(1)}, bf16[160,1024]{1,0:T(8,128)(2,1)S(1)}, u32[]{:S(2)}, u32[]{:S(2)}) collective-permute-start(bf16[160,1024]{1,0:T(8,128)(2,1)S(1)} %collective-permute-done.1), channel_id=1, source_target_pairs={{1,0},{3,2},{5,4},{7,6},{9,8},{11,10},{13,12},{15,14},{17,16},{19,... | collective-permute-start | bytes 983048 | tf_op jit(solution)/shard_map/ppermute | solution.py:16
  45.7 2.6 %multiply_multiply_fusion.coef_ref = f32[32,160,1]{2,1,0:T(8,128)} fusion(f32[32]{0:T(128)} %param.9, f32[160]{0:T(256)S(1)} %convert_log_fusion), kind=kLoop, calls=%fused_computation | loop fusion | flops 10240 | bytes 21248 | tf_op jit(solution)/shard_map/div | solution.py:96
  48.3 0.0 copy-start.1
  48.3 0.0 copy-start.2
  48.4 0.0 collective-permute-done.3
  48.4 0.0 collective-permute-done.2
  48.4 0.1 select_dynamic-update-slice_fusion.1
  48.5 0.0 collective-permute-done.4
  48.5 0.1 select_dynamic-update-slice_fusion
  48.6 0.6 copy-done.1
  49.3 0.1 copy-done.2
  49.3 0.0 copy-start
  49.3 1.2 %copy-done = bf16[800,1024]{1,0:T(8,128)(2,1)} copy-done((bf16[800,1024]{1,0:T(8,128)(2,1)}, bf16[800,1024]{1,0:T(8,128)(2,1)S(1)}, u32[]{:S(2)}) %copy-start) | copy-done | bytes 1638424
  50.5 18.3 %shard_map.55 = bf16[160,4096]{1,0:T(8,128)(2,1)} custom-call(f32[32,160,1]{2,1,0:T(8,128)} %multiply_multiply_fusion.coef_ref, s32[160,1]{1,0:T(8,128)} %copy.9.lo_ref, bf16[160,4096]{1,0:T(8,128)(2,1)} %q_ref.1, bf16[800,1024]{1,0:T(8,128)(2,1)} %copy-done, bf16[800,1024]{1,0:T(8,128)(2,1)} %copy-done), custom_call_target="tpu_custom_call" | custom-call | flops 2097152000 | bytes 4259840 | tf_op jit(solution)/shard_map/pallas_call | solution.py:61
  (8 shorter events, 0.1 us)
Async XLA Ops:
  1.9 46.7 %collective-permute-start.4 = (bf16[160,1024]{1,0:T(8,128)(2,1)S(1)}, bf16[160,1024]{1,0:T(8,128)(2,1)S(1)}, u32[]{:S(2)}, u32[]{:S(2)}) collective-permute-start(bf16[160,1024]{1,0:T(8,128)(2,1)S(1)} %constant_dynamic-update-slice_fusion), channel_id=1, source_target_pairs={{0,1},{2,3},{4,5},{6,7},{8,9},{10,11},{12,13},{14,15},{16,17},{18,... | collective-permute-start | bytes 983048 | tf_op jit(solution)/shard_map/ppermute | solution.py:16
  3.2 24.4 %collective-permute-start = (bf16[160,1024]{1,0:T(8,128)(2,1)S(1)}, bf16[160,1024]{1,0:T(8,128)(2,1)S(1)}, u32[]{:S(2)}, u32[]{:S(2)}) collective-permute-start(bf16[160,1024]{1,0:T(8,128)(2,1)S(1)} %constant_dynamic-update-slice_fusion), channel_id=1, source_target_pairs={{0,2},{1,3},{2,4},{3,5},{4,6},{5,7},{6,8},{7,9},{8,10},{9,11},{10,... | collective-permute-start | bytes 983048 | tf_op jit(solution)/shard_map/ppermute | solution.py:16
  27.5 13.5 %collective-permute-start.1 = (bf16[160,1024]{1,0:T(8,128)(2,1)S(1)}, bf16[160,1024]{1,0:T(8,128)(2,1)S(1)}, u32[]{:S(2)}, u32[]{:S(2)}) collective-permute-start(bf16[160,1024]{1,0:T(8,128)(2,1)S(1)} %collective-permute-done), channel_id=1, source_target_pairs={{0,2},{1,3},{2,4},{3,5},{4,6},{5,7},{6,8},{7,9},{8,10},{9,11},{10,... | collective-permute-start | bytes 983048 | tf_op jit(solution)/shard_map/ppermute | solution.py:16
  30.2 18.1 %collective-permute-start.3 = (bf16[160,1024]{1,0:T(8,128)(2,1)S(1)}, bf16[160,1024]{1,0:T(8,128)(2,1)S(1)}, u32[]{:S(2)}, u32[]{:S(2)}) collective-permute-start(bf16[160,1024]{1,0:T(8,128)(2,1)S(1)} %collective-permute-done), channel_id=1, source_target_pairs={{0,1},{2,3},{4,5},{6,7},{8,9},{10,11},{12,13},{14,15},{16,17},{18,... | collective-permute-start | bytes 983048 | tf_op jit(solution)/shard_map/ppermute | solution.py:16
  41.1 7.3 %collective-permute-start.2 = (bf16[160,1024]{1,0:T(8,128)(2,1)S(1)}, bf16[160,1024]{1,0:T(8,128)(2,1)S(1)}, u32[]{:S(2)}, u32[]{:S(2)}) collective-permute-start(bf16[160,1024]{1,0:T(8,128)(2,1)S(1)} %collective-permute-done.1), channel_id=1, source_target_pairs={{1,0},{3,2},{5,4},{7,6},{9,8},{11,10},{13,12},{15,14},{17,16},{19,... | collective-permute-start | bytes 983048 | tf_op jit(solution)/shard_map/ppermute | solution.py:16
  48.3 0.9 %copy-start.1 = (bf16[160,512]{1,0:T(8,128)(2,1)S(1)}, bf16[160,512]{1,0:T(8,128)(2,1)}, u32[]{:S(2)}) copy-start(bf16[160,512]{1,0:T(8,128)(2,1)} %param.6) | copy-start | bytes 491524
  48.3 1.0 %copy-start.2 = (bf16[160,512]{1,0:T(8,128)(2,1)S(1)}, bf16[160,512]{1,0:T(8,128)(2,1)}, u32[]{:S(2)}) copy-start(bf16[160,512]{1,0:T(8,128)(2,1)} %param.7) | copy-start | bytes 491524
  49.3 1.2 %copy-start = (bf16[800,1024]{1,0:T(8,128)(2,1)}, bf16[800,1024]{1,0:T(8,128)(2,1)S(1)}, u32[]{:S(2)}) copy-start(bf16[800,1024]{1,0:T(8,128)(2,1)S(1)} %constant_dynamic-update-slice_fusion.5.k_ref.v_ref) | copy-start | bytes 4915204

commit v3 on v2

--- a/solution.py
+++ b/solution.py
@@ -33,41 +33,52 @@
     return [back4, back3, back2, back1, own]
 
 
-def attend_kernel(coef_ref, lo_ref, q_ref, k_ref, v_ref, o_ref):
-    rows, width = q_ref.shape[0], k_ref.shape[0]
+def attend_kernel(scale_ref, logv_ref, lo_ref, q_ref, *refs):
+    kv_refs, o_ref = refs[:-1], refs[-1]
+    blocks = len(kv_refs) // 2
+    rows = q_ref.shape[0]
+    width = rows * blocks
     doc_most = width - rows
+    head = pl.program_id(0)
     col = lax.broadcasted_iota(jnp.int32, (rows, width), 1)
     row = lax.broadcasted_iota(jnp.int32, (rows, width), 0)
     live = (col >= lo_ref[...]) & (col <= row + doc_most)
-    k = k_ref[...]
-    v = v_ref[...]
-    for g in range(HQ // HK):
+    k = jnp.concatenate([r[...] for r in kv_refs[:blocks]], axis=0)
+    v = jnp.concatenate([r[...] for r in kv_refs[blocks:]], axis=0)
+    logv = logv_ref[...]
+    per_group = HQ // HK
+    for g in range(per_group):
+        coef = scale_ref[head * per_group + g] * logv / jnp.sqrt(jnp.float32(HD))
         q = q_ref[:, g * HD : (g + 1) * HD]
         s = lax.dot_general(q, k, (((1,), (1,)), ((), ())), preferred_element_type=jnp.float32)
-        s = jnp.where(live, s * coef_ref[g], -jnp.inf)
+        s = jnp.where(live, s * coef, -jnp.inf)
         m = jnp.max(s, axis=1, keepdims=True)
         p = jnp.exp(s - m)
         l = jnp.sum(p, axis=1, keepdims=True)
-        w = (p / l).astype(jnp.bfloat16)
+        w = (p * (1.0 / l)).astype(jnp.bfloat16)
         o = jnp.dot(w, v, preferred_element_type=jnp.float32)
         o_ref[:, g * HD : (g + 1) * HD] = o.astype(o_ref.dtype)
 
 
-def attend(queries, window, coef, lo, interpret=False):
+def attend(queries, blocks, scale, logv, lo, interpret=False):
     rows = queries.shape[0]
-    width = window.shape[0]
+    width = rows * len(blocks)
     per_group = HQ // HK
     flops = 4 * HQ * rows * width * HD
+    small = pl.BlockSpec((rows, 1), lambda h: (0, 0))
+    k_specs = [pl.BlockSpec((rows, HD), lambda h: (0, h)) for _ in blocks]
+    v_specs = [pl.BlockSpec((rows, HD), lambda h: (0, h + HK)) for _ in blocks]
     return pl.pallas_call(
         attend_kernel,
         grid=(HK,),
         in_specs=[
-            pl.BlockSpec((per_group, rows, 1), lambda h: (h, 0, 0)),
-            pl.BlockSpec((rows, 1), lambda h: (0, 0)),
+            pl.BlockSpec(memory_space=pltpu.SMEM),
+            small,
+            small,
             pl.BlockSpec((rows, per_group * HD), lambda h: (0, h)),
-            pl.BlockSpec((width, HD), lambda h: (0, h)),
-            pl.BlockSpec((width, HD), lambda h: (0, h + HK)),
-        ],
+        ]
+        + k_specs
+        + v_specs,
         out_specs=pl.BlockSpec((rows, per_group * HD), lambda h: (0, h)),
         out_shape=jax.ShapeDtypeStruct((rows, HQ * HD), jnp.bfloat16),
         cost_estimate=pl.CostEstimate(
@@ -76,7 +87,7 @@
             bytes_accessed=2 * (2 * rows * HQ * HD + width * 2 * HK * HD),
         ),
         interpret=interpret,
-    )(coef, lo, queries, window, window)
+    )(scale, logv, lo, queries, *blocks, *blocks)
 
 
 def body(queries, keys, values, lengths, ssmax_scale):
@@ -88,14 +99,13 @@
     q_start = ctx_index * slab_rows + grp_index * tok_rows
     q_pos = q_start + jnp.arange(tok_rows, dtype=jnp.int32)
     own = jnp.concatenate([keys, values], axis=1)
-    window = jnp.concatenate(window_blocks(own), axis=0)
+    blocks = window_blocks(own)
     totals = jnp.cumsum(lengths, dtype=jnp.int32)
     before = totals[None, :] <= q_pos[:, None]
     doc_start = jnp.sum(jnp.where(before, lengths[None, :], 0), axis=1, dtype=jnp.int32)
     visible = (q_pos - doc_start + 1).astype(jnp.float32)
-    score_coef = ssmax_scale[None, :] * jnp.log(visible)[:, None] / jnp.sqrt(jnp.float32(HD))
     lo = (doc_start - (q_start - doc_most))[:, None]
-    return attend(queries, window, score_coef.T[:, :, None], lo)
+    return attend(queries, blocks, ssmax_scale, jnp.log(visible)[:, None], lo)
 
 
 def solution(mesh):

time: 69.1 us -> 65.8 us (0.952)
  local copies, waits for them, and re-layouts: 4.71 us -> 2.18 us
  starting transfers between devices: 14.7 us -> 13.6 us
  waiting for transfers between devices: 26.2 us -> 27.1 us
    div x1 -> x0, other arithmetic: 2.63 us -> none  [body(): ssmax_scale[None, :] * jnp.log(visible)[:, None] / jnp.sqrt(jnp.float32(HD))]
    unnamed x10 -> x7, local copies, waits for them, and re-layouts: 2.83 us -> 0.94 us
    ppermute x5, starting transfers between devices: 14.7 us -> 13.6 us  [send(): return lax.ppermute(x, AXES, pairs)]
    ppermute x5, waiting for transfers between devices: 26.2 us -> 27.1 us  [send(): return lax.ppermute(x, AXES, pairs)]
    select_n x0 -> x1, other arithmetic: none -> 0.91 us  [window_blocks(): back1 = jnp.where(even, swapped2, from_even_own)]
    sub x1 -> x0, local copies, waits for them, and re-layouts: 0.74 us -> none  [body(): lo = (doc_start - (q_start - doc_most))[:, None]]
  transfers between devices with their start and end apart: 5 -> 5, of which waited for: 2 -> 2; matrix products, arithmetic and copies ran while one was open for 8% -> 5% of each run, Pallas kernels for 0% -> 0%
where the time goes in v3:
time: 65.8 us; the launch traced here: 65.5 us
  waiting for transfers between devices  27.1 us (41%)
  Pallas kernels  18.3 us (28%)
  starting transfers between devices  13.6 us (21%)
  other arithmetic  4.17 us (6%)
  local copies, waits for them, and re-layouts  2.18 us (3%)
    ppermute x5, waiting for transfers between devices, send(): return lax.ppermute(x, AXES, pairs)  27.1 us
    pallas_call x1, Pallas kernels, attend(): pl.pallas_call(attend_kernel, grid=(HK,), in_specs=[pl.BlockSpec(memory_s...  18.3 us
    ppermute x5, starting transfers between devices, send(): return lax.ppermute(x, AXES, pairs)  13.6 us
  transfers between devices with their start and end apart: 5, of which 2 were waited for; matrix products, arithmetic and copies ran while one was open for 5% of the time, Pallas kernels for 0%

profile of v3, /device:TPU:7, one launch (start us, length us, event | category | flops | bytes accessed | tf_op | source)
XLA Modules:
  0.0 65.5 jit_solution(1970338624485179451)
XLA Ops:
  0.0 0.9 %constant_dynamic-update-slice_fusion.1 = bf16[160,1024]{1,0:T(8,128)(2,1)S(1)} fusion(bf16[160,512]{1,0:T(8,128)(2,1)} %param.6), kind=kLoop, calls=%fused_computation.6 | loop fusion | bytes 327680
  0.9 0.9 %constant_dynamic-update-slice_fusion.refs_4_.refs_9_ = bf16[160,1024]{1,0:T(8,128)(2,1)S(1)} fusion(bf16[160,1024]{1,0:T(8,128)(2,1)S(1)} %constant_dynamic-update-slice_fusion.1, bf16[160,512]{1,0:T(8,128)(2,1)} %param.7), kind=kLoop, calls=%fused_computation.5 | loop fusion | bytes 327680 | tf_op jit(solution)/shard_map/concatenate | solution.py:101
  1.9 0.0 copy-start
  1.9 3.2 %collective-permute-start = (bf16[160,1024]{1,0:T(8,128)(2,1)S(1)}, bf16[160,1024]{1,0:T(8,128)(2,1)S(1)}, u32[]{:S(2)}, u32[]{:S(2)}) collective-permute-start(bf16[160,1024]{1,0:T(8,128)(2,1)S(1)} %constant_dynamic-update-slice_fusion.refs_4_.refs_9_), channel_id=1, source_target_pairs={{0,2},{1,3},{2,4},{3,5},{4,6},{5,7},{6,8},{7,9},{8,10},{9,11},{10,... | collective-permute-start | bytes 983048 | tf_op jit(solution)/shard_map/ppermute | solution.py:16
  5.1 1.3 %collective-permute-start.4 = (bf16[160,1024]{1,0:T(8,128)(2,1)S(1)}, bf16[160,1024]{1,0:T(8,128)(2,1)S(1)}, u32[]{:S(2)}, u32[]{:S(2)}) collective-permute-start(bf16[160,1024]{1,0:T(8,128)(2,1)S(1)} %constant_dynamic-update-slice_fusion.refs_4_.refs_9_), channel_id=1, source_target_pairs={{0,1},{2,3},{4,5},{6,7},{8,9},{10,11},{12,13},{14,15},{16,17},{18,... | collective-permute-start | bytes 983048 | tf_op jit(solution)/shard_map/ppermute | solution.py:16
  6.4 1.0 %reduce-window.9 = s32[3,128]{1,0:T(4,128)S(1)} reduce-window(s32[3,128]{1,0:T(4,128)} %bitcast.4, s32[]{:T(128)} %constant.29.clone.1), window={size=1x128 pad=0_0x127_0}, to_apply=%region_0.1 | reduce-window | flops 48768 | bytes 3076 | tf_op jit(solution)/shard_map/reduce-window
  7.4 0.1 slice.7
  7.5 0.1 slice_reduce_fusion
  7.6 19.2 %collective-permute-done.refs_2_.refs_7_ = bf16[160,1024]{1,0:T(8,128)(2,1)S(1)} collective-permute-done((bf16[160,1024]{1,0:T(8,128)(2,1)S(1)}, bf16[160,1024]{1,0:T(8,128)(2,1)S(1)}, u32[]{:S(2)}, u32[]{:S(2)}) %collective-permute-start) | collective-permute-done | bytes 327712 | tf_op jit(solution)/shard_map/ppermute | solution.py:16
  26.8 0.0 copy-start.1
  26.8 1.9 %collective-permute-start.1 = (bf16[160,1024]{1,0:T(8,128)(2,1)S(1)}, bf16[160,1024]{1,0:T(8,128)(2,1)S(1)}, u32[]{:S(2)}, u32[]{:S(2)}) collective-permute-start(bf16[160,1024]{1,0:T(8,128)(2,1)S(1)} %collective-permute-done.refs_2_.refs_7_), channel_id=1, source_target_pairs={{0,2},{1,3},{2,4},{3,5},{4,6},{5,7},{6,8},{7,9},{8,10},{9,11},{10,... | collective-permute-start | bytes 983048 | tf_op jit(solution)/shard_map/ppermute | solution.py:16
  28.7 0.1 add_bitcast_fusion
  28.8 0.9 %select_reduce_fusion = s32[160]{0:T(256)S(1)} fusion(s32[384]{0:T(512)} %param.8, s32[384]{0:T(512)S(1)} %add_bitcast_fusion, s32[160]{0:T(256)S(1)} %iota_add_fusion), kind=kLoop, calls=%fused_computation.2 | loop fusion | flops 184160 | bytes 4352 | tf_op jit(solution)/shard_map/reduce_sum | solution.py:105
  29.6 0.1 copy.11
  29.8 3.1 %collective-permute-start.3 = (bf16[160,1024]{1,0:T(8,128)(2,1)S(1)}, bf16[160,1024]{1,0:T(8,128)(2,1)S(1)}, u32[]{:S(2)}, u32[]{:S(2)}) collective-permute-start(bf16[160,1024]{1,0:T(8,128)(2,1)S(1)} %collective-permute-done.refs_2_.refs_7_), channel_id=1, source_target_pairs={{0,1},{2,3},{4,5},{6,7},{8,9},{10,11},{12,13},{14,15},{16,17},{18,... | collective-permute-start | bytes 983048 | tf_op jit(solution)/shard_map/ppermute | solution.py:16
  32.9 7.9 %collective-permute-done.1.refs_0_.refs_5_ = bf16[160,1024]{1,0:T(8,128)(2,1)S(1)} collective-permute-done((bf16[160,1024]{1,0:T(8,128)(2,1)S(1)}, bf16[160,1024]{1,0:T(8,128)(2,1)S(1)}, u32[]{:S(2)}, u32[]{:S(2)}) %collective-permute-start.1) | collective-permute-done | bytes 327712 | tf_op jit(solution)/shard_map/ppermute | solution.py:16
  40.9 0.0 copy-start.2
  40.9 4.1 %collective-permute-start.2 = (bf16[160,1024]{1,0:T(8,128)(2,1)S(1)}, bf16[160,1024]{1,0:T(8,128)(2,1)S(1)}, u32[]{:S(2)}, u32[]{:S(2)}) collective-permute-start(bf16[160,1024]{1,0:T(8,128)(2,1)S(1)} %collective-permute-done.1.refs_0_.refs_5_), channel_id=1, source_target_pairs={{1,0},{3,2},{5,4},{7,6},{9,8},{11,10},{13,12},{15,14},{17,16},{19,... | collective-permute-start | bytes 983048 | tf_op jit(solution)/shard_map/ppermute | solution.py:16
  44.9 0.7 %convert_log_fusion.logv_ref = f32[160,1]{1,0:T(8,128)} fusion(s32[160,1]{1,0:T(8,128)S(1)} %copy.11, s32[]{:T(128)S(6)} %add.41), kind=kLoop, calls=%fused_computation.3 | loop fusion | flops 640 | bytes 1284 | tf_op jit(solution)/shard_map/log | solution.py:108
  45.6 0.6 broadcast_subtract_fusion.lo_ref
  46.2 0.0 collective-permute-done.4
  46.2 0.0 collective-permute-done.3
  46.2 0.0 collective-permute-done.2
  46.2 0.9 %broadcast_select_fusion = (bf16[160,1024]{1,0:T(8,128)(2,1)}, bf16[160,1024]{1,0:T(8,128)(2,1)}) fusion(bf16[160,1024]{1,0:T(8,128)(2,1)S(1)} %collective-permute-done.3, bf16[160,1024]{1,0:T(8,128)(2,1)S(1)} %collective-permute-done.4, pred[]{:T(512)S(6)} %eq.5, bf16[160,1024]{1,0:T(8,128)(2,1)S(1)} %collective-permute-done.2), kind=kLoop, calls=%fused_computation | loop fusion | flops 327680 | bytes 1638401 | tf_op jit(solution)/shard_map/jit(_where)/select_n | solution.py:31
  47.2 0.0 copy-done
  47.2 0.0 copy-done.1
  47.2 0.0 copy-done.2
  47.2 18.3 %shard_map.55 = bf16[160,4096]{1,0:T(8,128)(2,1)} custom-call(f32[32]{0:T(128)} %scale_ref.1, f32[160,1]{1,0:T(8,128)} %convert_log_fusion.logv_ref, s32[160,1]{1,0:T(8,128)} %broadcast_subtract_fusion.lo_ref, bf16[160,4096]{1,0:T(8,128)(2,1)} %q_ref.1, bf16[160,1024]{1,0:T(8,128)(2,1)} %copy-done.2, bf16[160,1024]{1,0:T(8,128)(2,1)} %get-tuple-element.6.refs_1_.refs_6_, ...), custom_call_target="tpu_custom_call" | custom-call | flops 2097152000 | bytes 4259840 | tf_op jit(solution)/shard_map/pallas_call | solution.py:71
  (2 shorter events, 0.0 us)
Async XLA Ops:
  1.9 45.3 %copy-start = (bf16[160,1024]{1,0:T(8,128)(2,1)}, bf16[160,1024]{1,0:T(8,128)(2,1)S(1)}, u32[]{:S(2)}) copy-start(bf16[160,1024]{1,0:T(8,128)(2,1)S(1)} %constant_dynamic-update-slice_fusion.refs_4_.refs_9_) | copy-start | bytes 983044
  1.9 24.9 %collective-permute-start = (bf16[160,1024]{1,0:T(8,128)(2,1)S(1)}, bf16[160,1024]{1,0:T(8,128)(2,1)S(1)}, u32[]{:S(2)}, u32[]{:S(2)}) collective-permute-start(bf16[160,1024]{1,0:T(8,128)(2,1)S(1)} %constant_dynamic-update-slice_fusion.refs_4_.refs_9_), channel_id=1, source_target_pairs={{0,2},{1,3},{2,4},{3,5},{4,6},{5,7},{6,8},{7,9},{8,10},{9,11},{10,... | collective-permute-start | bytes 983048 | tf_op jit(solution)/shard_map/ppermute | solution.py:16
  5.1 41.1 %collective-permute-start.4 = (bf16[160,1024]{1,0:T(8,128)(2,1)S(1)}, bf16[160,1024]{1,0:T(8,128)(2,1)S(1)}, u32[]{:S(2)}, u32[]{:S(2)}) collective-permute-start(bf16[160,1024]{1,0:T(8,128)(2,1)S(1)} %constant_dynamic-update-slice_fusion.refs_4_.refs_9_), channel_id=1, source_target_pairs={{0,1},{2,3},{4,5},{6,7},{8,9},{10,11},{12,13},{14,15},{16,17},{18,... | collective-permute-start | bytes 983048 | tf_op jit(solution)/shard_map/ppermute | solution.py:16
  26.8 20.4 %copy-start.1 = (bf16[160,1024]{1,0:T(8,128)(2,1)}, bf16[160,1024]{1,0:T(8,128)(2,1)S(1)}, u32[]{:S(2)}) copy-start(bf16[160,1024]{1,0:T(8,128)(2,1)S(1)} %collective-permute-done.refs_2_.refs_7_) | copy-start | bytes 983044
  26.8 14.1 %collective-permute-start.1 = (bf16[160,1024]{1,0:T(8,128)(2,1)S(1)}, bf16[160,1024]{1,0:T(8,128)(2,1)S(1)}, u32[]{:S(2)}, u32[]{:S(2)}) collective-permute-start(bf16[160,1024]{1,0:T(8,128)(2,1)S(1)} %collective-permute-done.refs_2_.refs_7_), channel_id=1, source_target_pairs={{0,2},{1,3},{2,4},{3,5},{4,6},{5,7},{6,8},{7,9},{8,10},{9,11},{10,... | collective-permute-start | bytes 983048 | tf_op jit(solution)/shard_map/ppermute | solution.py:16
  29.8 16.5 %collective-permute-start.3 = (bf16[160,1024]{1,0:T(8,128)(2,1)S(1)}, bf16[160,1024]{1,0:T(8,128)(2,1)S(1)}, u32[]{:S(2)}, u32[]{:S(2)}) collective-permute-start(bf16[160,1024]{1,0:T(8,128)(2,1)S(1)} %collective-permute-done.refs_2_.refs_7_), channel_id=1, source_target_pairs={{0,1},{2,3},{4,5},{6,7},{8,9},{10,11},{12,13},{14,15},{16,17},{18,... | collective-permute-start | bytes 983048 | tf_op jit(solution)/shard_map/ppermute | solution.py:16
  40.9 6.3 %copy-start.2 = (bf16[160,1024]{1,0:T(8,128)(2,1)}, bf16[160,1024]{1,0:T(8,128)(2,1)S(1)}, u32[]{:S(2)}) copy-start(bf16[160,1024]{1,0:T(8,128)(2,1)S(1)} %collective-permute-done.1.refs_0_.refs_5_) | copy-start | bytes 983044
  40.9 5.4 %collective-permute-start.2 = (bf16[160,1024]{1,0:T(8,128)(2,1)S(1)}, bf16[160,1024]{1,0:T(8,128)(2,1)S(1)}, u32[]{:S(2)}, u32[]{:S(2)}) collective-permute-start(bf16[160,1024]{1,0:T(8,128)(2,1)S(1)} %collective-permute-done.1.refs_0_.refs_5_), channel_id=1, source_target_pairs={{1,0},{3,2},{5,4},{7,6},{9,8},{11,10},{13,12},{15,14},{17,16},{19,... | collective-permute-start | bytes 983048 | tf_op jit(solution)/shard_map/ppermute | solution.py:16

commit v4 on v3

--- a/solution.py
+++ b/solution.py
@@ -47,18 +47,19 @@
     v = jnp.concatenate([r[...] for r in kv_refs[blocks:]], axis=0)
     logv = logv_ref[...]
     per_group = HQ // HK
+    coef = jnp.stack(
+        [scale_ref[head * per_group + g] * logv / jnp.sqrt(jnp.float32(HD)) for g in range(per_group)]
+    )
+    q = jnp.concatenate([q_ref[:, g * HD : (g + 1) * HD] for g in range(per_group)], axis=0)
+    s = lax.dot_general(q, k, (((1,), (1,)), ((), ())), preferred_element_type=jnp.float32)
+    s = jnp.where(live[None], s.reshape(per_group, rows, width) * coef, -jnp.inf)
+    m = jnp.max(s, axis=2, keepdims=True)
+    p = jnp.exp(s - m)
+    l = jnp.sum(p, axis=2, keepdims=True)
+    w = (p * (1.0 / l)).astype(jnp.bfloat16).reshape(per_group * rows, width)
+    o = jnp.dot(w, v, preferred_element_type=jnp.float32)
     for g in range(per_group):
-        coef = scale_ref[head * per_group + g] * logv / jnp.sqrt(jnp.float32(HD))
-        q = q_ref[:, g * HD : (g + 1) * HD]
-        s = lax.dot_general(q, k, (((1,), (1,)), ((), ())), preferred_element_type=jnp.float32)
-        s = jnp.where(live, s * coef, -jnp.inf)
-        m = jnp.max(s, axis=1, keepdims=True)
-        p = jnp.exp(s - m)
-        l = jnp.sum(p, axis=1, keepdims=True)
-        w = (p * (1.0 / l)).astype(jnp.bfloat16)
-        o = jnp.dot(w, v, preferred_element_type=jnp.float32)
-        o_ref[:, g * HD : (g + 1) * HD] = o.astype(o_ref.dtype)
-
+        o_ref[:, g * HD : (g + 1) * HD] = o[g * rows : (g + 1) * rows].astype(o_ref.dtype)
 
 def attend(queries, blocks, scale, logv, lo, interpret=False):
     rows = queries.shape[0]

time: 65.8 us -> 62 us (0.942)
  Pallas kernels: 18.3 us -> 14.5 us
    pallas_call x1, Pallas kernels: 18.3 us -> 14.5 us  [attend(): pl.pallas_call(attend_kernel, grid=(HK,), in_specs=[pl.BlockSpec(memory_s...]
  transfers between devices with their start and end apart: 5 -> 5, of which waited for: 2 -> 2; matrix products, arithmetic and copies ran while one was open for 5% -> 6% of each run, Pallas kernels for 0% -> 0%
where the time goes in v4:
time: 62 us; the launch traced here: 61.6 us
  waiting for transfers between devices  27.1 us (44%)
  Pallas kernels  14.5 us (23%)
  starting transfers between devices  13.6 us (22%)
  other arithmetic  4.17 us (7%)
  local copies, waits for them, and re-layouts  2.18 us (4%)
    ppermute x5, waiting for transfers between devices, send(): return lax.ppermute(x, AXES, pairs)  27.1 us
    pallas_call x1, Pallas kernels, attend(): pl.pallas_call(attend_kernel, grid=(HK,), in_specs=[pl.BlockSpec(memory_s...  14.5 us
    ppermute x5, starting transfers between devices, send(): return lax.ppermute(x, AXES, pairs)  13.6 us
  transfers between devices with their start and end apart: 5, of which 2 were waited for; matrix products, arithmetic and copies ran while one was open for 6% of the time, Pallas kernels for 0%

profile of v4, /device:TPU:7, one launch (start us, length us, event | category | flops | bytes accessed | tf_op | source)
XLA Modules:
  0.0 61.6 jit_solution(7492023560768370540)
XLA Ops:
  0.0 0.9 %constant_dynamic-update-slice_fusion.1 = bf16[160,1024]{1,0:T(8,128)(2,1)S(1)} fusion(bf16[160,512]{1,0:T(8,128)(2,1)} %param.6), kind=kLoop, calls=%fused_computation.6 | loop fusion | bytes 327680
  0.9 0.9 %constant_dynamic-update-slice_fusion.refs_4_.refs_9_ = bf16[160,1024]{1,0:T(8,128)(2,1)S(1)} fusion(bf16[160,1024]{1,0:T(8,128)(2,1)S(1)} %constant_dynamic-update-slice_fusion.1, bf16[160,512]{1,0:T(8,128)(2,1)} %param.7), kind=kLoop, calls=%fused_computation.5 | loop fusion | bytes 327680 | tf_op jit(solution)/shard_map/concatenate | solution.py:102
  1.9 0.0 copy-start
  1.9 3.2 %collective-permute-start = (bf16[160,1024]{1,0:T(8,128)(2,1)S(1)}, bf16[160,1024]{1,0:T(8,128)(2,1)S(1)}, u32[]{:S(2)}, u32[]{:S(2)}) collective-permute-start(bf16[160,1024]{1,0:T(8,128)(2,1)S(1)} %constant_dynamic-update-slice_fusion.refs_4_.refs_9_), channel_id=1, source_target_pairs={{0,2},{1,3},{2,4},{3,5},{4,6},{5,7},{6,8},{7,9},{8,10},{9,11},{10,... | collective-permute-start | bytes 983048 | tf_op jit(solution)/shard_map/ppermute | solution.py:16
  5.1 1.3 %collective-permute-start.4 = (bf16[160,1024]{1,0:T(8,128)(2,1)S(1)}, bf16[160,1024]{1,0:T(8,128)(2,1)S(1)}, u32[]{:S(2)}, u32[]{:S(2)}) collective-permute-start(bf16[160,1024]{1,0:T(8,128)(2,1)S(1)} %constant_dynamic-update-slice_fusion.refs_4_.refs_9_), channel_id=1, source_target_pairs={{0,1},{2,3},{4,5},{6,7},{8,9},{10,11},{12,13},{14,15},{16,17},{18,... | collective-permute-start | bytes 983048 | tf_op jit(solution)/shard_map/ppermute | solution.py:16
  6.4 1.0 %reduce-window.9 = s32[3,128]{1,0:T(4,128)S(1)} reduce-window(s32[3,128]{1,0:T(4,128)} %bitcast.4, s32[]{:T(128)} %constant.29.clone.1), window={size=1x128 pad=0_0x127_0}, to_apply=%region_0.1 | reduce-window | flops 48768 | bytes 3076 | tf_op jit(solution)/shard_map/reduce-window
  7.4 0.1 slice.7
  7.5 0.1 slice_reduce_fusion
  7.6 19.2 %collective-permute-done.refs_2_.refs_7_ = bf16[160,1024]{1,0:T(8,128)(2,1)S(1)} collective-permute-done((bf16[160,1024]{1,0:T(8,128)(2,1)S(1)}, bf16[160,1024]{1,0:T(8,128)(2,1)S(1)}, u32[]{:S(2)}, u32[]{:S(2)}) %collective-permute-start) | collective-permute-done | bytes 327712 | tf_op jit(solution)/shard_map/ppermute | solution.py:16
  26.8 0.0 copy-start.1
  26.8 1.9 %collective-permute-start.1 = (bf16[160,1024]{1,0:T(8,128)(2,1)S(1)}, bf16[160,1024]{1,0:T(8,128)(2,1)S(1)}, u32[]{:S(2)}, u32[]{:S(2)}) collective-permute-start(bf16[160,1024]{1,0:T(8,128)(2,1)S(1)} %collective-permute-done.refs_2_.refs_7_), channel_id=1, source_target_pairs={{0,2},{1,3},{2,4},{3,5},{4,6},{5,7},{6,8},{7,9},{8,10},{9,11},{10,... | collective-permute-start | bytes 983048 | tf_op jit(solution)/shard_map/ppermute | solution.py:16
  28.7 0.1 add_bitcast_fusion
  28.8 0.9 %select_reduce_fusion = s32[160]{0:T(256)S(1)} fusion(s32[384]{0:T(512)} %param.8, s32[384]{0:T(512)S(1)} %add_bitcast_fusion, s32[160]{0:T(256)S(1)} %iota_add_fusion), kind=kLoop, calls=%fused_computation.2 | loop fusion | flops 184160 | bytes 4352 | tf_op jit(solution)/shard_map/reduce_sum | solution.py:106
  29.6 0.1 copy.11
  29.8 3.1 %collective-permute-start.3 = (bf16[160,1024]{1,0:T(8,128)(2,1)S(1)}, bf16[160,1024]{1,0:T(8,128)(2,1)S(1)}, u32[]{:S(2)}, u32[]{:S(2)}) collective-permute-start(bf16[160,1024]{1,0:T(8,128)(2,1)S(1)} %collective-permute-done.refs_2_.refs_7_), channel_id=1, source_target_pairs={{0,1},{2,3},{4,5},{6,7},{8,9},{10,11},{12,13},{14,15},{16,17},{18,... | collective-permute-start | bytes 983048 | tf_op jit(solution)/shard_map/ppermute | solution.py:16
  32.9 7.9 %collective-permute-done.1.refs_0_.refs_5_ = bf16[160,1024]{1,0:T(8,128)(2,1)S(1)} collective-permute-done((bf16[160,1024]{1,0:T(8,128)(2,1)S(1)}, bf16[160,1024]{1,0:T(8,128)(2,1)S(1)}, u32[]{:S(2)}, u32[]{:S(2)}) %collective-permute-start.1) | collective-permute-done | bytes 327712 | tf_op jit(solution)/shard_map/ppermute | solution.py:16
  40.9 0.0 copy-start.2
  40.9 4.1 %collective-permute-start.2 = (bf16[160,1024]{1,0:T(8,128)(2,1)S(1)}, bf16[160,1024]{1,0:T(8,128)(2,1)S(1)}, u32[]{:S(2)}, u32[]{:S(2)}) collective-permute-start(bf16[160,1024]{1,0:T(8,128)(2,1)S(1)} %collective-permute-done.1.refs_0_.refs_5_), channel_id=1, source_target_pairs={{1,0},{3,2},{5,4},{7,6},{9,8},{11,10},{13,12},{15,14},{17,16},{19,... | collective-permute-start | bytes 983048 | tf_op jit(solution)/shard_map/ppermute | solution.py:16
  44.9 0.7 %convert_log_fusion.logv_ref = f32[160,1]{1,0:T(8,128)} fusion(s32[160,1]{1,0:T(8,128)S(1)} %copy.11, s32[]{:T(128)S(6)} %add.41), kind=kLoop, calls=%fused_computation.3 | loop fusion | flops 640 | bytes 1284 | tf_op jit(solution)/shard_map/log | solution.py:109
  45.6 0.6 %broadcast_subtract_fusion.lo_ref = s32[160,1]{1,0:T(8,128)} fusion(s32[160,1]{1,0:T(8,128)S(1)} %copy.11, s32[]{:T(128)S(6)} %sub.27), kind=kLoop, calls=%fused_computation.4 | loop fusion | flops 160 | bytes 1284 | tf_op jit(solution)/shard_map/sub | solution.py:108
  46.2 0.0 collective-permute-done.4
  46.2 0.0 collective-permute-done.3
  46.2 0.0 collective-permute-done.2
  46.2 0.9 %broadcast_select_fusion = (bf16[160,1024]{1,0:T(8,128)(2,1)}, bf16[160,1024]{1,0:T(8,128)(2,1)}) fusion(bf16[160,1024]{1,0:T(8,128)(2,1)S(1)} %collective-permute-done.3, bf16[160,1024]{1,0:T(8,128)(2,1)S(1)} %collective-permute-done.4, pred[]{:T(512)S(6)} %eq.5, bf16[160,1024]{1,0:T(8,128)(2,1)S(1)} %collective-permute-done.2), kind=kLoop, calls=%fused_computation | loop fusion | flops 327680 | bytes 1638401 | tf_op jit(solution)/shard_map/jit(_where)/select_n | solution.py:31
  47.2 0.0 copy-done
  47.2 0.0 copy-done.1
  47.2 0.0 copy-done.2
  47.2 14.5 %shard_map.55 = bf16[160,4096]{1,0:T(8,128)(2,1)} custom-call(f32[32]{0:T(128)} %scale_ref.1, f32[160,1]{1,0:T(8,128)} %convert_log_fusion.logv_ref, s32[160,1]{1,0:T(8,128)} %broadcast_subtract_fusion.lo_ref, bf16[160,4096]{1,0:T(8,128)(2,1)} %q_ref.1, bf16[160,1024]{1,0:T(8,128)(2,1)} %copy-done.2, bf16[160,1024]{1,0:T(8,128)(2,1)} %get-tuple-element.6.refs_1_.refs_6_, ...), custom_call_target="tpu_custom_call" | custom-call | flops 2097152000 | bytes 4259840 | tf_op jit(solution)/shard_map/pallas_call | solution.py:72
  (2 shorter events, 0.0 us)
Async XLA Ops:
  1.9 45.3 %copy-start = (bf16[160,1024]{1,0:T(8,128)(2,1)}, bf16[160,1024]{1,0:T(8,128)(2,1)S(1)}, u32[]{:S(2)}) copy-start(bf16[160,1024]{1,0:T(8,128)(2,1)S(1)} %constant_dynamic-update-slice_fusion.refs_4_.refs_9_) | copy-start | bytes 983044
  1.9 24.9 %collective-permute-start = (bf16[160,1024]{1,0:T(8,128)(2,1)S(1)}, bf16[160,1024]{1,0:T(8,128)(2,1)S(1)}, u32[]{:S(2)}, u32[]{:S(2)}) collective-permute-start(bf16[160,1024]{1,0:T(8,128)(2,1)S(1)} %constant_dynamic-update-slice_fusion.refs_4_.refs_9_), channel_id=1, source_target_pairs={{0,2},{1,3},{2,4},{3,5},{4,6},{5,7},{6,8},{7,9},{8,10},{9,11},{10,... | collective-permute-start | bytes 983048 | tf_op jit(solution)/shard_map/ppermute | solution.py:16
  5.1 41.1 %collective-permute-start.4 = (bf16[160,1024]{1,0:T(8,128)(2,1)S(1)}, bf16[160,1024]{1,0:T(8,128)(2,1)S(1)}, u32[]{:S(2)}, u32[]{:S(2)}) collective-permute-start(bf16[160,1024]{1,0:T(8,128)(2,1)S(1)} %constant_dynamic-update-slice_fusion.refs_4_.refs_9_), channel_id=1, source_target_pairs={{0,1},{2,3},{4,5},{6,7},{8,9},{10,11},{12,13},{14,15},{16,17},{18,... | collective-permute-start | bytes 983048 | tf_op jit(solution)/shard_map/ppermute | solution.py:16
  26.8 20.4 %copy-start.1 = (bf16[160,1024]{1,0:T(8,128)(2,1)}, bf16[160,1024]{1,0:T(8,128)(2,1)S(1)}, u32[]{:S(2)}) copy-start(bf16[160,1024]{1,0:T(8,128)(2,1)S(1)} %collective-permute-done.refs_2_.refs_7_) | copy-start | bytes 983044
  26.8 14.1 %collective-permute-start.1 = (bf16[160,1024]{1,0:T(8,128)(2,1)S(1)}, bf16[160,1024]{1,0:T(8,128)(2,1)S(1)}, u32[]{:S(2)}, u32[]{:S(2)}) collective-permute-start(bf16[160,1024]{1,0:T(8,128)(2,1)S(1)} %collective-permute-done.refs_2_.refs_7_), channel_id=1, source_target_pairs={{0,2},{1,3},{2,4},{3,5},{4,6},{5,7},{6,8},{7,9},{8,10},{9,11},{10,... | collective-permute-start | bytes 983048 | tf_op jit(solution)/shard_map/ppermute | solution.py:16
  29.8 16.5 %collective-permute-start.3 = (bf16[160,1024]{1,0:T(8,128)(2,1)S(1)}, bf16[160,1024]{1,0:T(8,128)(2,1)S(1)}, u32[]{:S(2)}, u32[]{:S(2)}) collective-permute-start(bf16[160,1024]{1,0:T(8,128)(2,1)S(1)} %collective-permute-done.refs_2_.refs_7_), channel_id=1, source_target_pairs={{0,1},{2,3},{4,5},{6,7},{8,9},{10,11},{12,13},{14,15},{16,17},{18,... | collective-permute-start | bytes 983048 | tf_op jit(solution)/shard_map/ppermute | solution.py:16
  40.9 6.3 %copy-start.2 = (bf16[160,1024]{1,0:T(8,128)(2,1)}, bf16[160,1024]{1,0:T(8,128)(2,1)S(1)}, u32[]{:S(2)}) copy-start(bf16[160,1024]{1,0:T(8,128)(2,1)S(1)} %collective-permute-done.1.refs_0_.refs_5_) | copy-start | bytes 983044
  40.9 5.4 %collective-permute-start.2 = (bf16[160,1024]{1,0:T(8,128)(2,1)S(1)}, bf16[160,1024]{1,0:T(8,128)(2,1)S(1)}, u32[]{:S(2)}, u32[]{:S(2)}) collective-permute-start(bf16[160,1024]{1,0:T(8,128)(2,1)S(1)} %collective-permute-done.1.refs_0_.refs_5_), channel_id=1, source_target_pairs={{1,0},{3,2},{5,4},{7,6},{9,8},{11,10},{13,12},{15,14},{17,16},{19,... | collective-permute-start | bytes 983048 | tf_op jit(solution)/shard_map/ppermute | solution.py:16

commit v5 on v4

--- a/solution.py
+++ b/solution.py
@@ -27,25 +27,33 @@
     back4 = send(back2, ahead2)
     swapped2 = send(back2, swap)
     from_odd4 = send(back4, to_even)
-    even = lax.axis_index("grp") % 2 == 0
-    back1 = jnp.where(even, swapped2, from_even_own)
-    back3 = jnp.where(even, from_odd4, swapped2)
-    return [back4, back3, back2, back1, own]
+    return [back4, from_odd4, swapped2, back2, from_even_own, own]
 
 
-def attend_kernel(scale_ref, logv_ref, lo_ref, q_ref, *refs):
+def attend_kernel(qs_ref, scale_ref, ds_ref, q_ref, *refs):
     kv_refs, o_ref = refs[:-1], refs[-1]
-    blocks = len(kv_refs) // 2
+    half = len(kv_refs) // 2
     rows = q_ref.shape[0]
-    width = rows * blocks
+    width = rows * (half - 1)
     doc_most = width - rows
     head = pl.program_id(0)
+    q_start = qs_ref[0]
+    even = qs_ref[1] == 0
+
+    def ordered(r):
+        back4, odd4, swap2, back2, even_own, own = [x[...] for x in r]
+        back3 = jnp.where(even, odd4, swap2)
+        back1 = jnp.where(even, swap2, even_own)
+        return jnp.concatenate([back4, back3, back2, back1, own], axis=0)
+
     col = lax.broadcasted_iota(jnp.int32, (rows, width), 1)
     row = lax.broadcasted_iota(jnp.int32, (rows, width), 0)
-    live = (col >= lo_ref[...]) & (col <= row + doc_most)
-    k = jnp.concatenate([r[...] for r in kv_refs[:blocks]], axis=0)
-    v = jnp.concatenate([r[...] for r in kv_refs[blocks:]], axis=0)
-    logv = logv_ref[...]
+    doc_start = ds_ref[...]
+    live = (col >= doc_start - (q_start - doc_most)) & (col <= row + doc_most)
+    k = ordered(kv_refs[:half])
+    v = ordered(kv_refs[half:])
+    q_pos = q_start + lax.broadcasted_iota(jnp.int32, (rows, 1), 0)
+    logv = jnp.log((q_pos - doc_start + 1).astype(jnp.float32))
     per_group = HQ // HK
     coef = jnp.stack(
         [scale_ref[head * per_group + g] * logv / jnp.sqrt(jnp.float32(HD)) for g in range(per_group)]
@@ -61,12 +69,12 @@
     for g in range(per_group):
         o_ref[:, g * HD : (g + 1) * HD] = o[g * rows : (g + 1) * rows].astype(o_ref.dtype)
 
-def attend(queries, blocks, scale, logv, lo, interpret=False):
+
+def attend(queries, blocks, where, scale, doc_start, interpret=False):
     rows = queries.shape[0]
-    width = rows * len(blocks)
+    width = rows * (len(blocks) - 1)
     per_group = HQ // HK
     flops = 4 * HQ * rows * width * HD
-    small = pl.BlockSpec((rows, 1), lambda h: (0, 0))
     k_specs = [pl.BlockSpec((rows, HD), lambda h: (0, h)) for _ in blocks]
     v_specs = [pl.BlockSpec((rows, HD), lambda h: (0, h + HK)) for _ in blocks]
     return pl.pallas_call(
@@ -74,8 +82,8 @@
         grid=(HK,),
         in_specs=[
             pl.BlockSpec(memory_space=pltpu.SMEM),
-            small,
-            small,
+            pl.BlockSpec(memory_space=pltpu.SMEM),
+            pl.BlockSpec((rows, 1), lambda h: (0, 0)),
             pl.BlockSpec((rows, per_group * HD), lambda h: (0, h)),
         ]
         + k_specs
@@ -88,7 +96,7 @@
             bytes_accessed=2 * (2 * rows * HQ * HD + width * 2 * HK * HD),
         ),
         interpret=interpret,
-    )(scale, logv, lo, queries, *blocks, *blocks)
+    )(where, scale, doc_start, queries, *blocks, *blocks)
 
 
 def body(queries, keys, values, lengths, ssmax_scale):
@@ -104,9 +112,8 @@
     totals = jnp.cumsum(lengths, dtype=jnp.int32)
     before = totals[None, :] <= q_pos[:, None]
     doc_start = jnp.sum(jnp.where(before, lengths[None, :], 0), axis=1, dtype=jnp.int32)
-    visible = (q_pos - doc_start + 1).astype(jnp.float32)
-    lo = (doc_start - (q_start - doc_most))[:, None]
-    return attend(queries, blocks, ssmax_scale, jnp.log(visible)[:, None], lo)
+    where = jnp.stack([q_start, grp_index % 2]).astype(jnp.int32)
+    return attend(queries, blocks, where, ssmax_scale, doc_start[:, None])
 
 
 def solution(mesh):

time: 62 us -> 63.5 us (1.024)
  local copies, waits for them, and re-layouts: 2.18 us -> 4.36 us
  other arithmetic: 4.17 us -> 2.52 us
  waiting for transfers between devices: 27.1 us -> 28.1 us
    unnamed x7 -> x13, local copies, waits for them, and re-layouts: 0.94 us -> 2.48 us
    ppermute x5, waiting for transfers between devices: 27.1 us -> 28.1 us  [send(): return lax.ppermute(x, AXES, pairs)]
    select_n x1 -> x0, other arithmetic: 0.91 us -> none  [window_blocks(): back1 = jnp.where(even, swapped2, from_even_own)]
    broadcast_in_dim x0 -> x1, local copies, waits for them, and re-layouts: none -> 0.76 us  [body(): return attend(queries, blocks, where, ssmax_scale, doc_start[:, None])]
    log x1 -> x0, other arithmetic: 0.66 us -> none  [body(): return attend(queries, blocks, ssmax_scale, jnp.log(visible)[:, None], lo)]
    sub x1 -> x0, other arithmetic: 0.64 us -> none  [body(): lo = (doc_start - (q_start - doc_most))[:, None]]
    another operation x3 -> x4, other arithmetic: 1.09 us -> 1.65 us
  transfers between devices with their start and end apart: 5 -> 5, of which waited for: 2 -> 2; matrix products, arithmetic and copies ran while one was open for 6% -> 5% of each run, Pallas kernels for 0% -> 0%
where the time goes in v5:
time: 63.5 us; the launch traced here: 63.2 us
  waiting for transfers between devices  28.1 us (44%)
  Pallas kernels  14.5 us (23%)
  starting transfers between devices  13.6 us (21%)
  local copies, waits for them, and re-layouts  4.36 us (7%)
  other arithmetic  2.52 us (4%)
    ppermute x5, waiting for transfers between devices, send(): return lax.ppermute(x, AXES, pairs)  28.1 us
    pallas_call x1, Pallas kernels, attend(): pl.pallas_call(attend_kernel, grid=(HK,), in_specs=[pl.BlockSpec(memory_s...  14.5 us
    ppermute x5, starting transfers between devices, send(): return lax.ppermute(x, AXES, pairs)  13.6 us
    unnamed x13, local copies, waits for them, and re-layouts  2.48 us
  transfers between devices with their start and end apart: 5, of which 2 were waited for; matrix products, arithmetic and copies ran while one was open for 5% of the time, Pallas kernels for 0%

profile of v5, /device:TPU:7, one launch (start us, length us, event | category | flops | bytes accessed | tf_op | source)
XLA Modules:
  0.0 63.2 jit_solution(4847132054554864496)
XLA Ops:
  0.0 0.9 %constant_dynamic-update-slice_fusion.1 = bf16[160,1024]{1,0:T(8,128)(2,1)S(1)} fusion(bf16[160,512]{1,0:T(8,128)(2,1)} %param.6), kind=kLoop, calls=%fused_computation.2 | loop fusion | bytes 327680
  0.9 0.9 %constant_dynamic-update-slice_fusion.refs_5_.refs_11_ = bf16[160,1024]{1,0:T(8,128)(2,1)S(1)} fusion(bf16[160,1024]{1,0:T(8,128)(2,1)S(1)} %constant_dynamic-update-slice_fusion.1, bf16[160,512]{1,0:T(8,128)(2,1)} %param.7), kind=kLoop, calls=%fused_computation.1 | loop fusion | bytes 327680 | tf_op jit(solution)/shard_map/concatenate | solution.py:110
  1.9 0.0 copy-start
  1.9 3.2 %collective-permute-start = (bf16[160,1024]{1,0:T(8,128)(2,1)S(1)}, bf16[160,1024]{1,0:T(8,128)(2,1)S(1)}, u32[]{:S(2)}, u32[]{:S(2)}) collective-permute-start(bf16[160,1024]{1,0:T(8,128)(2,1)S(1)} %constant_dynamic-update-slice_fusion.refs_5_.refs_11_), channel_id=1, source_target_pairs={{0,2},{1,3},{2,4},{3,5},{4,6},{5,7},{6,8},{7,9},{8,10},{9,11},{10,... | collective-permute-start | bytes 983048 | tf_op jit(solution)/shard_map/ppermute | solution.py:16
  5.1 1.3 %collective-permute-start.4 = (bf16[160,1024]{1,0:T(8,128)(2,1)S(1)}, bf16[160,1024]{1,0:T(8,128)(2,1)S(1)}, u32[]{:S(2)}, u32[]{:S(2)}) collective-permute-start(bf16[160,1024]{1,0:T(8,128)(2,1)S(1)} %constant_dynamic-update-slice_fusion.refs_5_.refs_11_), channel_id=1, source_target_pairs={{0,1},{2,3},{4,5},{6,7},{8,9},{10,11},{12,13},{14,15},{16,17},{18,... | collective-permute-start | bytes 983048 | tf_op jit(solution)/shard_map/ppermute | solution.py:16
  6.4 1.0 %reduce-window.9 = s32[3,128]{1,0:T(4,128)S(1)} reduce-window(s32[3,128]{1,0:T(4,128)} %bitcast.6, s32[]{:T(128)} %constant.26.clone.1), window={size=1x128 pad=0_0x127_0}, to_apply=%region_0.0 | reduce-window | flops 48768 | bytes 3076 | tf_op jit(solution)/shard_map/reduce-window
  7.4 0.1 slice.7
  7.5 19.3 %collective-permute-done.refs_3_.refs_9_ = bf16[160,1024]{1,0:T(8,128)(2,1)S(1)} collective-permute-done((bf16[160,1024]{1,0:T(8,128)(2,1)S(1)}, bf16[160,1024]{1,0:T(8,128)(2,1)S(1)}, u32[]{:S(2)}, u32[]{:S(2)}) %collective-permute-start) | collective-permute-done | bytes 327712 | tf_op jit(solution)/shard_map/ppermute | solution.py:16
  26.8 0.0 copy-start.1
  26.8 1.9 %collective-permute-start.1 = (bf16[160,1024]{1,0:T(8,128)(2,1)S(1)}, bf16[160,1024]{1,0:T(8,128)(2,1)S(1)}, u32[]{:S(2)}, u32[]{:S(2)}) collective-permute-start(bf16[160,1024]{1,0:T(8,128)(2,1)S(1)} %collective-permute-done.refs_3_.refs_9_), channel_id=1, source_target_pairs={{0,2},{1,3},{2,4},{3,5},{4,6},{5,7},{6,8},{7,9},{8,10},{9,11},{10,... | collective-permute-start | bytes 983048 | tf_op jit(solution)/shard_map/ppermute | solution.py:16
  28.7 0.1 slice_reduce_fusion
  28.8 0.1 add_bitcast_fusion
  28.9 3.1 %collective-permute-start.3 = (bf16[160,1024]{1,0:T(8,128)(2,1)S(1)}, bf16[160,1024]{1,0:T(8,128)(2,1)S(1)}, u32[]{:S(2)}, u32[]{:S(2)}) collective-permute-start(bf16[160,1024]{1,0:T(8,128)(2,1)S(1)} %collective-permute-done.refs_3_.refs_9_), channel_id=1, source_target_pairs={{0,1},{2,3},{4,5},{6,7},{8,9},{10,11},{12,13},{14,15},{16,17},{18,... | collective-permute-start | bytes 983048 | tf_op jit(solution)/shard_map/ppermute | solution.py:16
  32.0 8.8 %collective-permute-done.1.refs_0_.refs_6_ = bf16[160,1024]{1,0:T(8,128)(2,1)S(1)} collective-permute-done((bf16[160,1024]{1,0:T(8,128)(2,1)S(1)}, bf16[160,1024]{1,0:T(8,128)(2,1)S(1)}, u32[]{:S(2)}, u32[]{:S(2)}) %collective-permute-start.1) | collective-permute-done | bytes 327712 | tf_op jit(solution)/shard_map/ppermute | solution.py:16
  40.9 0.0 copy-start.3
  40.9 4.1 %collective-permute-start.2 = (bf16[160,1024]{1,0:T(8,128)(2,1)S(1)}, bf16[160,1024]{1,0:T(8,128)(2,1)S(1)}, u32[]{:S(2)}, u32[]{:S(2)}) collective-permute-start(bf16[160,1024]{1,0:T(8,128)(2,1)S(1)} %collective-permute-done.1.refs_0_.refs_6_), channel_id=1, source_target_pairs={{1,0},{3,2},{5,4},{7,6},{9,8},{11,10},{13,12},{15,14},{17,16},{19,... | collective-permute-start | bytes 983048 | tf_op jit(solution)/shard_map/ppermute | solution.py:16
  44.9 0.9 %select_reduce_fusion = s32[160]{0:T(256)S(1)} fusion(s32[384]{0:T(512)} %param.8, s32[384]{0:T(512)S(1)} %add_bitcast_fusion, s32[160]{0:T(256)S(1)} %iota_add_fusion), kind=kLoop, calls=%fused_computation | loop fusion | flops 184160 | bytes 4352 | tf_op jit(solution)/shard_map/reduce_sum | solution.py:114
  45.8 0.8 %copy.7.ds_ref = s32[160,1]{1,0:T(8,128)} copy(s32[160,1]{0,1:T(1,128)S(1)} %bitcast.7) | data formatting | bytes 1280 | tf_op jit(solution)/shard_map/broadcast_in_dim | solution.py:116
  46.6 0.6 pad_add_fusion.qs_ref
  47.1 0.0 collective-permute-done.4.refs_4_.refs_10_
  47.1 0.0 copy-start.2
  47.1 0.0 collective-permute-done.3.refs_2_.refs_8_
  47.1 0.0 copy-start.4
  47.2 0.0 collective-permute-done.2.refs_1_.refs_7_
  47.2 0.0 copy-done
  47.2 0.0 copy-done.1
  47.2 0.0 copy-done.3
  47.2 0.7 %copy-done.2 = bf16[160,1024]{1,0:T(8,128)(2,1)} copy-done((bf16[160,1024]{1,0:T(8,128)(2,1)}, bf16[160,1024]{1,0:T(8,128)(2,1)S(1)}, u32[]{:S(2)}) %copy-start.2) | copy-done | bytes 327704
  47.8 0.1 copy-done.4
  48.0 0.0 copy-start.5
  48.0 0.7 %copy-done.5 = bf16[160,1024]{1,0:T(8,128)(2,1)} copy-done((bf16[160,1024]{1,0:T(8,128)(2,1)}, bf16[160,1024]{1,0:T(8,128)(2,1)S(1)}, u32[]{:S(2)}) %copy-start.5) | copy-done | bytes 327704
  48.7 14.5 %shard_map.55 = bf16[160,4096]{1,0:T(8,128)(2,1)} custom-call(s32[2]{0:T(128)} %pad_add_fusion.qs_ref, f32[32]{0:T(128)} %scale_ref.1, s32[160,1]{1,0:T(8,128)} %copy.7.ds_ref, bf16[160,4096]{1,0:T(8,128)(2,1)} %q_ref.1, bf16[160,1024]{1,0:T(8,128)(2,1)} %copy-done.3, bf16[160,1024]{1,0:T(8,128)(2,1)} %copy-done.5, bf16[160,1024]{1,0:T(8,128)(2,1)} %copy-done.4, ...), custom_call_target="tpu_custom_call" | custom-call | flops 2097152000 | bytes 4259840 | tf_op jit(solution)/shard_map/pallas_call | solution.py:80
  (2 shorter events, 0.0 us)
Async XLA Ops:
  1.9 45.3 %copy-start = (bf16[160,1024]{1,0:T(8,128)(2,1)}, bf16[160,1024]{1,0:T(8,128)(2,1)S(1)}, u32[]{:S(2)}) copy-start(bf16[160,1024]{1,0:T(8,128)(2,1)S(1)} %constant_dynamic-update-slice_fusion.refs_5_.refs_11_) | copy-start | bytes 983044
  1.9 24.9 %collective-permute-start = (bf16[160,1024]{1,0:T(8,128)(2,1)S(1)}, bf16[160,1024]{1,0:T(8,128)(2,1)S(1)}, u32[]{:S(2)}, u32[]{:S(2)}) collective-permute-start(bf16[160,1024]{1,0:T(8,128)(2,1)S(1)} %constant_dynamic-update-slice_fusion.refs_5_.refs_11_), channel_id=1, source_target_pairs={{0,2},{1,3},{2,4},{3,5},{4,6},{5,7},{6,8},{7,9},{8,10},{9,11},{10,... | collective-permute-start | bytes 983048 | tf_op jit(solution)/shard_map/ppermute | solution.py:16
  5.1 42.0 %collective-permute-start.4 = (bf16[160,1024]{1,0:T(8,128)(2,1)S(1)}, bf16[160,1024]{1,0:T(8,128)(2,1)S(1)}, u32[]{:S(2)}, u32[]{:S(2)}) collective-permute-start(bf16[160,1024]{1,0:T(8,128)(2,1)S(1)} %constant_dynamic-update-slice_fusion.refs_5_.refs_11_), channel_id=1, source_target_pairs={{0,1},{2,3},{4,5},{6,7},{8,9},{10,11},{12,13},{14,15},{16,17},{18,... | collective-permute-start | bytes 983048 | tf_op jit(solution)/shard_map/ppermute | solution.py:16
  26.8 20.4 %copy-start.1 = (bf16[160,1024]{1,0:T(8,128)(2,1)}, bf16[160,1024]{1,0:T(8,128)(2,1)S(1)}, u32[]{:S(2)}) copy-start(bf16[160,1024]{1,0:T(8,128)(2,1)S(1)} %collective-permute-done.refs_3_.refs_9_) | copy-start | bytes 983044
  26.8 14.1 %collective-permute-start.1 = (bf16[160,1024]{1,0:T(8,128)(2,1)S(1)}, bf16[160,1024]{1,0:T(8,128)(2,1)S(1)}, u32[]{:S(2)}, u32[]{:S(2)}) collective-permute-start(bf16[160,1024]{1,0:T(8,128)(2,1)S(1)} %collective-permute-done.refs_3_.refs_9_), channel_id=1, source_target_pairs={{0,2},{1,3},{2,4},{3,5},{4,6},{5,7},{6,8},{7,9},{8,10},{9,11},{10,... | collective-permute-start | bytes 983048 | tf_op jit(solution)/shard_map/ppermute | solution.py:16
  28.9 18.2 %collective-permute-start.3 = (bf16[160,1024]{1,0:T(8,128)(2,1)S(1)}, bf16[160,1024]{1,0:T(8,128)(2,1)S(1)}, u32[]{:S(2)}, u32[]{:S(2)}) collective-permute-start(bf16[160,1024]{1,0:T(8,128)(2,1)S(1)} %collective-permute-done.refs_3_.refs_9_), channel_id=1, source_target_pairs={{0,1},{2,3},{4,5},{6,7},{8,9},{10,11},{12,13},{14,15},{16,17},{18,... | collective-permute-start | bytes 983048 | tf_op jit(solution)/shard_map/ppermute | solution.py:16
  40.9 6.3 %copy-start.3 = (bf16[160,1024]{1,0:T(8,128)(2,1)}, bf16[160,1024]{1,0:T(8,128)(2,1)S(1)}, u32[]{:S(2)}) copy-start(bf16[160,1024]{1,0:T(8,128)(2,1)S(1)} %collective-permute-done.1.refs_0_.refs_6_) | copy-start | bytes 983044
  40.9 6.3 %collective-permute-start.2 = (bf16[160,1024]{1,0:T(8,128)(2,1)S(1)}, bf16[160,1024]{1,0:T(8,128)(2,1)S(1)}, u32[]{:S(2)}, u32[]{:S(2)}) collective-permute-start(bf16[160,1024]{1,0:T(8,128)(2,1)S(1)} %collective-permute-done.1.refs_0_.refs_6_), channel_id=1, source_target_pairs={{1,0},{3,2},{5,4},{7,6},{9,8},{11,10},{13,12},{15,14},{17,16},{19,... | collective-permute-start | bytes 983048 | tf_op jit(solution)/shard_map/ppermute | solution.py:16
  47.1 0.7 %copy-start.2 = (bf16[160,1024]{1,0:T(8,128)(2,1)}, bf16[160,1024]{1,0:T(8,128)(2,1)S(1)}, u32[]{:S(2)}) copy-start(bf16[160,1024]{1,0:T(8,128)(2,1)S(1)} %collective-permute-done.4.refs_4_.refs_10_) | copy-start | bytes 983044
  47.1 0.9 %copy-start.4 = (bf16[160,1024]{1,0:T(8,128)(2,1)}, bf16[160,1024]{1,0:T(8,128)(2,1)S(1)}, u32[]{:S(2)}) copy-start(bf16[160,1024]{1,0:T(8,128)(2,1)S(1)} %collective-permute-done.3.refs_2_.refs_8_) | copy-start | bytes 983044
  48.0 0.7 %copy-start.5 = (bf16[160,1024]{1,0:T(8,128)(2,1)}, bf16[160,1024]{1,0:T(8,128)(2,1)S(1)}, u32[]{:S(2)}) copy-start(bf16[160,1024]{1,0:T(8,128)(2,1)S(1)} %collective-permute-done.2.refs_1_.refs_7_) | copy-start | bytes 983044

commit v6 on v5

--- a/solution.py
+++ b/solution.py
@@ -1,3 +1,5 @@
+import functools
+
 import jax
 import jax.numpy as jnp
 from jax import lax
@@ -16,15 +18,32 @@
     return lax.ppermute(x, AXES, pairs)
 
 
-def window_blocks(own):
+def far_receivers(mesh):
+    flat = list(mesh.devices.reshape(-1))
+    try:
+        chips = [tuple(d.coords) for d in flat]
+    except AttributeError:
+        return ()
+    sizes = [max(c[a] for c in chips) + 1 for a in range(len(chips[0]))]
+
+    def hops(a, b):
+        return sum(min(abs(p - q), n - abs(p - q)) for p, q, n in zip(a, b, sizes))
+
+    return tuple(i for i in range(4, len(flat)) if hops(chips[i - 2], chips[i]) >= 3)
+
+
+def window_blocks(own, far):
     count = lax.axis_size("ctx") * lax.axis_size("grp")
     ahead2 = [(i, i + 2) for i in range(count - 2)]
     to_odd = [(i, i + 1) for i in range(0, count - 1, 2)]
     to_even = [(i, i - 1) for i in range(1, count, 2)]
     swap = to_odd + to_even
+    far_set = set(far)
     back2 = send(own, ahead2)
     from_even_own = send(own, to_odd)
-    back4 = send(back2, ahead2)
+    direct4 = send(own, [(i - 4, i) for i in far])
+    forward2 = [(i, j) for i, j in ahead2 if j not in far_set]
+    back4 = send(back2, forward2) + direct4 if far else send(back2, forward2)
     swapped2 = send(back2, swap)
     from_odd4 = send(back4, to_even)
     return [back4, from_odd4, swapped2, back2, from_even_own, own]
@@ -99,7 +118,7 @@
     )(where, scale, doc_start, queries, *blocks, *blocks)
 
 
-def body(queries, keys, values, lengths, ssmax_scale):
+def body(queries, keys, values, lengths, ssmax_scale, far=()):
     tok_rows = queries.shape[0]
     slab_rows = tok_rows * lax.axis_size("grp")
     doc_most = WIN_DEV * tok_rows
@@ -108,7 +127,7 @@
     q_start = ctx_index * slab_rows + grp_index * tok_rows
     q_pos = q_start + jnp.arange(tok_rows, dtype=jnp.int32)
     own = jnp.concatenate([keys, values], axis=1)
-    blocks = window_blocks(own)
+    blocks = window_blocks(own, far)
     totals = jnp.cumsum(lengths, dtype=jnp.int32)
     before = totals[None, :] <= q_pos[:, None]
     doc_start = jnp.sum(jnp.where(before, lengths[None, :], 0), axis=1, dtype=jnp.int32)
@@ -118,7 +137,7 @@
 
 def solution(mesh):
     return jax.shard_map(
-        body,
+        functools.partial(body, far=far_receivers(mesh)),
         mesh=mesh,
         in_specs=(
             P(AXES, None),

time: 63.5 us -> 58.6 us (0.923)
  the two profiles are of different devices: /device:TPU:7 before, /device:TPU:15 now
where the time goes in v6:
time: 58.6 us; the launch traced here: 58.3 us
  waiting for transfers between devices  20.1 us (34%)
  starting transfers between devices  17.2 us (29%)
  Pallas kernels  14.5 us (25%)
  local copies, waits for them, and re-layouts  4.41 us (8%)
  other arithmetic  1.97 us (3%)
    ppermute x6, waiting for transfers between devices, send(): return lax.ppermute(x, AXES, pairs)  20.1 us
    ppermute x6, starting transfers between devices, send(): return lax.ppermute(x, AXES, pairs)  17.2 us
    pallas_call x1, Pallas kernels, attend(): pl.pallas_call(attend_kernel, grid=(HK,), in_specs=[pl.BlockSpec(memory_s...  14.5 us
    unnamed x15, local copies, waits for them, and re-layouts  2.52 us
  transfers between devices with their start and end apart: 6, of which 2 were waited for; matrix products, arithmetic and copies ran while one was open for 5% of the time, Pallas kernels for 0%

profile of v6, /device:TPU:15, one launch (start us, length us, event | category | flops | bytes accessed | tf_op | source)
XLA Modules:
  0.0 58.3 jit_solution(10340004240102152966)
XLA Ops:
  0.0 0.9 %constant_dynamic-update-slice_fusion.1 = bf16[160,1024]{1,0:T(8,128)(2,1)S(1)} fusion(bf16[160,512]{1,0:T(8,128)(2,1)} %param.6), kind=kLoop, calls=%fused_computation.2 | loop fusion | bytes 327680
  0.9 0.9 %constant_dynamic-update-slice_fusion.refs_5_.refs_11_ = bf16[160,1024]{1,0:T(8,128)(2,1)S(1)} fusion(bf16[160,1024]{1,0:T(8,128)(2,1)S(1)} %constant_dynamic-update-slice_fusion.1, bf16[160,512]{1,0:T(8,128)(2,1)} %param.7), kind=kLoop, calls=%fused_computation.1 | loop fusion | bytes 327680 | tf_op jit(solution)/shard_map/concatenate | solution.py:129
  1.9 0.0 copy-start.1
  1.9 3.2 %collective-permute-start = (bf16[160,1024]{1,0:T(8,128)(2,1)S(1)}, bf16[160,1024]{1,0:T(8,128)(2,1)S(1)}, u32[]{:S(2)}, u32[]{:S(2)}) collective-permute-start(bf16[160,1024]{1,0:T(8,128)(2,1)S(1)} %constant_dynamic-update-slice_fusion.refs_5_.refs_11_), channel_id=1, source_target_pairs={{0,2},{1,3},{2,4},{3,5},{4,6},{5,7},{6,8},{7,9},{8,10},{9,11},{10,... | collective-permute-start | bytes 983048 | tf_op jit(solution)/shard_map/ppermute | solution.py:18
  5.1 1.3 %collective-permute-start.5 = (bf16[160,1024]{1,0:T(8,128)(2,1)S(1)}, bf16[160,1024]{1,0:T(8,128)(2,1)S(1)}, u32[]{:S(2)}, u32[]{:S(2)}) collective-permute-start(bf16[160,1024]{1,0:T(8,128)(2,1)S(1)} %constant_dynamic-update-slice_fusion.refs_5_.refs_11_), channel_id=1, source_target_pairs={{0,1},{2,3},{4,5},{6,7},{8,9},{10,11},{12,13},{14,15},{16,17},{18,... | collective-permute-start | bytes 983048 | tf_op jit(solution)/shard_map/ppermute | solution.py:18
  6.4 0.7 %collective-permute-start.2 = (bf16[160,1024]{1,0:T(8,128)(2,1)S(1)}, bf16[160,1024]{1,0:T(8,128)(2,1)S(1)}, u32[]{:S(2)}, u32[]{:S(2)}) collective-permute-start(bf16[160,1024]{1,0:T(8,128)(2,1)S(1)} %constant_dynamic-update-slice_fusion.refs_5_.refs_11_), channel_id=1, source_target_pairs={{188,192},{189,193},{380,384},{381,385},{572,576},{573,577}} | collective-permute-start | bytes 983048 | tf_op jit(solution)/shard_map/ppermute | solution.py:18
  7.1 1.0 %reduce-window.9 = s32[3,128]{1,0:T(4,128)S(1)} reduce-window(s32[3,128]{1,0:T(4,128)} %bitcast.6, s32[]{:T(128)} %constant.26.clone.1), window={size=1x128 pad=0_0x127_0}, to_apply=%region_0.0 | reduce-window | flops 48768 | bytes 3076 | tf_op jit(solution)/shard_map/reduce-window
  8.1 0.1 slice.7
  8.2 4.2 %collective-permute-done.refs_3_.refs_9_ = bf16[160,1024]{1,0:T(8,128)(2,1)S(1)} collective-permute-done((bf16[160,1024]{1,0:T(8,128)(2,1)S(1)}, bf16[160,1024]{1,0:T(8,128)(2,1)S(1)}, u32[]{:S(2)}, u32[]{:S(2)}) %collective-permute-start) | collective-permute-done | bytes 327712 | tf_op jit(solution)/shard_map/ppermute | solution.py:18
  12.4 3.2 %collective-permute-start.1 = (bf16[160,1024]{1,0:T(8,128)(2,1)S(1)}, bf16[160,1024]{1,0:T(8,128)(2,1)S(1)}, u32[]{:S(2)}, u32[]{:S(2)}) collective-permute-start(bf16[160,1024]{1,0:T(8,128)(2,1)S(1)} %collective-permute-done.refs_3_.refs_9_), channel_id=1, source_target_pairs={{0,2},{1,3},{2,4},{3,5},{4,6},{5,7},{6,8},{7,9},{8,10},{9,11},{10,... | collective-permute-start | bytes 983048 | tf_op jit(solution)/shard_map/ppermute | solution.py:18
  15.6 0.1 slice_reduce_fusion
  15.7 0.1 add_bitcast_fusion
  15.8 3.7 %collective-permute-start.4 = (bf16[160,1024]{1,0:T(8,128)(2,1)S(1)}, bf16[160,1024]{1,0:T(8,128)(2,1)S(1)}, u32[]{:S(2)}, u32[]{:S(2)}) collective-permute-start(bf16[160,1024]{1,0:T(8,128)(2,1)S(1)} %collective-permute-done.refs_3_.refs_9_), channel_id=1, source_target_pairs={{0,1},{2,3},{4,5},{6,7},{8,9},{10,11},{12,13},{14,15},{16,17},{18,... | collective-permute-start | bytes 983048 | tf_op jit(solution)/shard_map/ppermute | solution.py:18
  19.5 0.0 collective-permute-done.2
  19.5 16.0 %collective-permute-done.1 = bf16[160,1024]{1,0:T(8,128)(2,1)S(1)} collective-permute-done((bf16[160,1024]{1,0:T(8,128)(2,1)S(1)}, bf16[160,1024]{1,0:T(8,128)(2,1)S(1)}, u32[]{:S(2)}, u32[]{:S(2)}) %collective-permute-start.1) | collective-permute-done | bytes 327712 | tf_op jit(solution)/shard_map/ppermute | solution.py:18
  35.5 0.1 add.24.refs_0_.refs_6_
  35.6 0.0 copy-start
  35.6 5.1 %collective-permute-start.3 = (bf16[160,1024]{1,0:T(8,128)(2,1)S(1)}, bf16[160,1024]{1,0:T(8,128)(2,1)S(1)}, u32[]{:S(2)}, u32[]{:S(2)}) collective-permute-start(bf16[160,1024]{1,0:T(8,128)(2,1)S(1)} %add.24.refs_0_.refs_6_), channel_id=1, source_target_pairs={{1,0},{3,2},{5,4},{7,6},{9,8},{11,10},{13,12},{15,14},{17,16},{19,... | collective-permute-start | bytes 983048 | tf_op jit(solution)/shard_map/ppermute | solution.py:18
  40.7 0.0 copy-done.2
  40.7 0.2 select_reduce_fusion
  40.9 0.8 %copy.7.ds_ref = s32[160,1]{1,0:T(8,128)} copy(s32[160,1]{0,1:T(1,128)S(1)} %bitcast.7) | data formatting | bytes 1280 | tf_op jit(solution)/shard_map/broadcast_in_dim | solution.py:135
  41.6 0.6 pad_add_fusion.qs_ref
  42.2 0.0 collective-permute-done.5.refs_4_.refs_10_
  42.2 0.0 collective-permute-done.4.refs_2_.refs_8_
  42.2 0.0 copy-start.5
  42.2 0.0 collective-permute-done.3.refs_1_.refs_7_
  42.3 0.0 copy-done.1
  42.3 0.0 copy-done.3
  42.3 0.7 %copy-done.4 = bf16[160,1024]{1,0:T(8,128)(2,1)} copy-done((bf16[160,1024]{1,0:T(8,128)(2,1)}, bf16[160,1024]{1,0:T(8,128)(2,1)S(1)}, u32[]{:S(2)}) %copy-start.4) | copy-done | bytes 327704
  42.9 0.2 copy-done.5
  43.1 0.7 %copy-done.6 = bf16[160,1024]{1,0:T(8,128)(2,1)} copy-done((bf16[160,1024]{1,0:T(8,128)(2,1)}, bf16[160,1024]{1,0:T(8,128)(2,1)S(1)}, u32[]{:S(2)}) %copy-start.6) | copy-done | bytes 327704
  43.9 14.5 %shard_map.55 = bf16[160,4096]{1,0:T(8,128)(2,1)} custom-call(s32[2]{0:T(128)} %pad_add_fusion.qs_ref, f32[32]{0:T(128)} %scale_ref.1, s32[160,1]{1,0:T(8,128)} %copy.7.ds_ref, bf16[160,4096]{1,0:T(8,128)(2,1)} %q_ref.1, bf16[160,1024]{1,0:T(8,128)(2,1)} %copy-done, bf16[160,1024]{1,0:T(8,128)(2,1)} %copy-done.6, bf16[160,1024]{1,0:T(8,128)(2,1)} %copy-done.5, ...), custom_call_target="tpu_custom_call" | custom-call | flops 2097152000 | bytes 4259840 | tf_op jit(solution)/shard_map/pallas_call | solution.py:99
  (7 shorter events, 0.1 us)
Async XLA Ops:
  0.0 40.7 %copy-start.2 = (s32[384]{0:T(512)S(1)}, s32[384]{0:T(512)}, u32[]{:S(2)}) copy-start(s32[384]{0:T(512)} %param.8) | copy-start | bytes 4612
  1.9 40.4 %copy-start.1 = (bf16[160,1024]{1,0:T(8,128)(2,1)}, bf16[160,1024]{1,0:T(8,128)(2,1)S(1)}, u32[]{:S(2)}) copy-start(bf16[160,1024]{1,0:T(8,128)(2,1)S(1)} %constant_dynamic-update-slice_fusion.refs_5_.refs_11_) | copy-start | bytes 983044
  1.9 10.5 %collective-permute-start = (bf16[160,1024]{1,0:T(8,128)(2,1)S(1)}, bf16[160,1024]{1,0:T(8,128)(2,1)S(1)}, u32[]{:S(2)}, u32[]{:S(2)}) collective-permute-start(bf16[160,1024]{1,0:T(8,128)(2,1)S(1)} %constant_dynamic-update-slice_fusion.refs_5_.refs_11_), channel_id=1, source_target_pairs={{0,2},{1,3},{2,4},{3,5},{4,6},{5,7},{6,8},{7,9},{8,10},{9,11},{10,... | collective-permute-start | bytes 983048 | tf_op jit(solution)/shard_map/ppermute | solution.py:18
  5.1 37.1 %collective-permute-start.5 = (bf16[160,1024]{1,0:T(8,128)(2,1)S(1)}, bf16[160,1024]{1,0:T(8,128)(2,1)S(1)}, u32[]{:S(2)}, u32[]{:S(2)}) collective-permute-start(bf16[160,1024]{1,0:T(8,128)(2,1)S(1)} %constant_dynamic-update-slice_fusion.refs_5_.refs_11_), channel_id=1, source_target_pairs={{0,1},{2,3},{4,5},{6,7},{8,9},{10,11},{12,13},{14,15},{16,17},{18,... | collective-permute-start | bytes 983048 | tf_op jit(solution)/shard_map/ppermute | solution.py:18
  6.4 13.1 %collective-permute-start.2 = (bf16[160,1024]{1,0:T(8,128)(2,1)S(1)}, bf16[160,1024]{1,0:T(8,128)(2,1)S(1)}, u32[]{:S(2)}, u32[]{:S(2)}) collective-permute-start(bf16[160,1024]{1,0:T(8,128)(2,1)S(1)} %constant_dynamic-update-slice_fusion.refs_5_.refs_11_), channel_id=1, source_target_pairs={{188,192},{189,193},{380,384},{381,385},{572,576},{573,577}} | collective-permute-start | bytes 983048 | tf_op jit(solution)/shard_map/ppermute | solution.py:18
  12.4 29.9 %copy-start.3 = (bf16[160,1024]{1,0:T(8,128)(2,1)}, bf16[160,1024]{1,0:T(8,128)(2,1)S(1)}, u32[]{:S(2)}) copy-start(bf16[160,1024]{1,0:T(8,128)(2,1)S(1)} %collective-permute-done.refs_3_.refs_9_) | copy-start | bytes 983044
  12.4 23.1 %collective-permute-start.1 = (bf16[160,1024]{1,0:T(8,128)(2,1)S(1)}, bf16[160,1024]{1,0:T(8,128)(2,1)S(1)}, u32[]{:S(2)}, u32[]{:S(2)}) collective-permute-start(bf16[160,1024]{1,0:T(8,128)(2,1)S(1)} %collective-permute-done.refs_3_.refs_9_), channel_id=1, source_target_pairs={{0,2},{1,3},{2,4},{3,5},{4,6},{5,7},{6,8},{7,9},{8,10},{9,11},{10,... | collective-permute-start | bytes 983048 | tf_op jit(solution)/shard_map/ppermute | solution.py:18
  15.8 26.5 %collective-permute-start.4 = (bf16[160,1024]{1,0:T(8,128)(2,1)S(1)}, bf16[160,1024]{1,0:T(8,128)(2,1)S(1)}, u32[]{:S(2)}, u32[]{:S(2)}) collective-permute-start(bf16[160,1024]{1,0:T(8,128)(2,1)S(1)} %collective-permute-done.refs_3_.refs_9_), channel_id=1, source_target_pairs={{0,1},{2,3},{4,5},{6,7},{8,9},{10,11},{12,13},{14,15},{16,17},{18,... | collective-permute-start | bytes 983048 | tf_op jit(solution)/shard_map/ppermute | solution.py:18
  35.6 6.7 %copy-start = (bf16[160,1024]{1,0:T(8,128)(2,1)}, bf16[160,1024]{1,0:T(8,128)(2,1)S(1)}, u32[]{:S(2)}) copy-start(bf16[160,1024]{1,0:T(8,128)(2,1)S(1)} %add.24.refs_0_.refs_6_) | copy-start | bytes 983044
  35.6 6.7 %collective-permute-start.3 = (bf16[160,1024]{1,0:T(8,128)(2,1)S(1)}, bf16[160,1024]{1,0:T(8,128)(2,1)S(1)}, u32[]{:S(2)}, u32[]{:S(2)}) collective-permute-start(bf16[160,1024]{1,0:T(8,128)(2,1)S(1)} %add.24.refs_0_.refs_6_), channel_id=1, source_target_pairs={{1,0},{3,2},{5,4},{7,6},{9,8},{11,10},{13,12},{15,14},{17,16},{19,... | collective-permute-start | bytes 983048 | tf_op jit(solution)/shard_map/ppermute | solution.py:18
  42.2 0.7 %copy-start.4 = (bf16[160,1024]{1,0:T(8,128)(2,1)}, bf16[160,1024]{1,0:T(8,128)(2,1)S(1)}, u32[]{:S(2)}) copy-start(bf16[160,1024]{1,0:T(8,128)(2,1)S(1)} %collective-permute-done.5.refs_4_.refs_10_) | copy-start | bytes 983044
  42.2 0.9 %copy-start.5 = (bf16[160,1024]{1,0:T(8,128)(2,1)}, bf16[160,1024]{1,0:T(8,128)(2,1)S(1)}, u32[]{:S(2)}) copy-start(bf16[160,1024]{1,0:T(8,128)(2,1)S(1)} %collective-permute-done.4.refs_2_.refs_8_) | copy-start | bytes 983044
  43.1 0.7 %copy-start.6 = (bf16[160,1024]{1,0:T(8,128)(2,1)}, bf16[160,1024]{1,0:T(8,128)(2,1)S(1)}, u32[]{:S(2)}) copy-start(bf16[160,1024]{1,0:T(8,128)(2,1)S(1)} %collective-permute-done.3.refs_1_.refs_7_) | copy-start | bytes 983044

commit v7 on v6

--- a/solution.py
+++ b/solution.py
@@ -29,7 +29,7 @@
     def hops(a, b):
         return sum(min(abs(p - q), n - abs(p - q)) for p, q, n in zip(a, b, sizes))
 
-    return tuple(i for i in range(4, len(flat)) if hops(chips[i - 2], chips[i]) >= 3)
+    return tuple(i for i in range(4, len(flat)) if hops(chips[i - 4], chips[i]) >= 3)
 
 
 def window_blocks(own, far):

time: 58.6 us -> 62 us (1.058)
  waiting for transfers between devices: 20.1 us -> 24.6 us
  starting transfers between devices: 17.2 us -> 16.1 us
    ppermute x6, waiting for transfers between devices: 20.1 us -> 24.6 us  [send(): return lax.ppermute(x, AXES, pairs)]
    ppermute x6, starting transfers between devices: 17.2 us -> 16.1 us  [send(): return lax.ppermute(x, AXES, pairs)]
where the time goes in v7:
time: 62 us; the launch traced here: 61.7 us
  waiting for transfers between devices  24.6 us (40%)
  starting transfers between devices  16.1 us (26%)
  Pallas kernels  14.5 us (23%)
  local copies, waits for them, and re-layouts  4.41 us (7%)
  other arithmetic  1.97 us (3%)
    ppermute x6, waiting for transfers between devices, send(): return lax.ppermute(x, AXES, pairs)  24.6 us
    ppermute x6, starting transfers between devices, send(): return lax.ppermute(x, AXES, pairs)  16.1 us
    pallas_call x1, Pallas kernels, attend(): pl.pallas_call(attend_kernel, grid=(HK,), in_specs=[pl.BlockSpec(memory_s...  14.5 us
    unnamed x15, local copies, waits for them, and re-layouts  2.52 us
  transfers between devices with their start and end apart: 6, of which 2 were waited for; matrix products, arithmetic and copies ran while one was open for 5% of the time, Pallas kernels for 0%

profile of v7, /device:TPU:15, one launch (start us, length us, event | category | flops | bytes accessed | tf_op | source)
XLA Modules:
  0.0 61.7 jit_solution(139008139262136850)
XLA Ops:
  0.0 0.9 %constant_dynamic-update-slice_fusion.1 = bf16[160,1024]{1,0:T(8,128)(2,1)S(1)} fusion(bf16[160,512]{1,0:T(8,128)(2,1)} %param.6), kind=kLoop, calls=%fused_computation.2 | loop fusion | bytes 327680
  0.9 0.9 %constant_dynamic-update-slice_fusion.refs_5_.refs_11_ = bf16[160,1024]{1,0:T(8,128)(2,1)S(1)} fusion(bf16[160,1024]{1,0:T(8,128)(2,1)S(1)} %constant_dynamic-update-slice_fusion.1, bf16[160,512]{1,0:T(8,128)(2,1)} %param.7), kind=kLoop, calls=%fused_computation.1 | loop fusion | bytes 327680 | tf_op jit(solution)/shard_map/concatenate | solution.py:129
  1.9 0.0 copy-start.1
  1.9 3.2 %collective-permute-start = (bf16[160,1024]{1,0:T(8,128)(2,1)S(1)}, bf16[160,1024]{1,0:T(8,128)(2,1)S(1)}, u32[]{:S(2)}, u32[]{:S(2)}) collective-permute-start(bf16[160,1024]{1,0:T(8,128)(2,1)S(1)} %constant_dynamic-update-slice_fusion.refs_5_.refs_11_), channel_id=1, source_target_pairs={{0,2},{1,3},{2,4},{3,5},{4,6},{5,7},{6,8},{7,9},{8,10},{9,11},{10,... | collective-permute-start | bytes 983048 | tf_op jit(solution)/shard_map/ppermute | solution.py:18
  5.1 1.3 %collective-permute-start.5 = (bf16[160,1024]{1,0:T(8,128)(2,1)S(1)}, bf16[160,1024]{1,0:T(8,128)(2,1)S(1)}, u32[]{:S(2)}, u32[]{:S(2)}) collective-permute-start(bf16[160,1024]{1,0:T(8,128)(2,1)S(1)} %constant_dynamic-update-slice_fusion.refs_5_.refs_11_), channel_id=1, source_target_pairs={{0,1},{2,3},{4,5},{6,7},{8,9},{10,11},{12,13},{14,15},{16,17},{18,... | collective-permute-start | bytes 983048 | tf_op jit(solution)/shard_map/ppermute | solution.py:18
  6.4 1.3 %collective-permute-start.2 = (bf16[160,1024]{1,0:T(8,128)(2,1)S(1)}, bf16[160,1024]{1,0:T(8,128)(2,1)S(1)}, u32[]{:S(2)}, u32[]{:S(2)}) collective-permute-start(bf16[160,1024]{1,0:T(8,128)(2,1)S(1)} %constant_dynamic-update-slice_fusion.refs_5_.refs_11_), channel_id=1, source_target_pairs={{12,16},{13,17},{14,18},{15,19},{28,32},{29,33},{30,34},{31,35},{4... | collective-permute-start | bytes 983048 | tf_op jit(solution)/shard_map/ppermute | solution.py:18
  7.7 1.0 %reduce-window.9 = s32[3,128]{1,0:T(4,128)S(1)} reduce-window(s32[3,128]{1,0:T(4,128)} %bitcast.6, s32[]{:T(128)} %constant.26.clone.1), window={size=1x128 pad=0_0x127_0}, to_apply=%region_0.0 | reduce-window | flops 48768 | bytes 3076 | tf_op jit(solution)/shard_map/reduce-window
  8.7 0.1 slice.7
  8.8 3.5 %collective-permute-done.refs_3_.refs_9_ = bf16[160,1024]{1,0:T(8,128)(2,1)S(1)} collective-permute-done((bf16[160,1024]{1,0:T(8,128)(2,1)S(1)}, bf16[160,1024]{1,0:T(8,128)(2,1)S(1)}, u32[]{:S(2)}, u32[]{:S(2)}) %collective-permute-start) | collective-permute-done | bytes 327712 | tf_op jit(solution)/shard_map/ppermute | solution.py:18
  12.4 3.2 %collective-permute-start.1 = (bf16[160,1024]{1,0:T(8,128)(2,1)S(1)}, bf16[160,1024]{1,0:T(8,128)(2,1)S(1)}, u32[]{:S(2)}, u32[]{:S(2)}) collective-permute-start(bf16[160,1024]{1,0:T(8,128)(2,1)S(1)} %collective-permute-done.refs_3_.refs_9_), channel_id=1, source_target_pairs={{0,2},{1,3},{2,4},{3,5},{4,6},{5,7},{6,8},{7,9},{8,10},{9,11},{10,... | collective-permute-start | bytes 983048 | tf_op jit(solution)/shard_map/ppermute | solution.py:18
  15.6 0.1 slice_reduce_fusion
  15.7 0.1 add_bitcast_fusion
  15.8 3.7 %collective-permute-start.4 = (bf16[160,1024]{1,0:T(8,128)(2,1)S(1)}, bf16[160,1024]{1,0:T(8,128)(2,1)S(1)}, u32[]{:S(2)}, u32[]{:S(2)}) collective-permute-start(bf16[160,1024]{1,0:T(8,128)(2,1)S(1)} %collective-permute-done.refs_3_.refs_9_), channel_id=1, source_target_pairs={{0,1},{2,3},{4,5},{6,7},{8,9},{10,11},{12,13},{14,15},{16,17},{18,... | collective-permute-start | bytes 983048 | tf_op jit(solution)/shard_map/ppermute | solution.py:18
  19.5 21.0 %collective-permute-done.2 = bf16[160,1024]{1,0:T(8,128)(2,1)S(1)} collective-permute-done((bf16[160,1024]{1,0:T(8,128)(2,1)S(1)}, bf16[160,1024]{1,0:T(8,128)(2,1)S(1)}, u32[]{:S(2)}, u32[]{:S(2)}) %collective-permute-start.2) | collective-permute-done | bytes 327712 | tf_op jit(solution)/shard_map/ppermute | solution.py:18
  40.5 0.0 collective-permute-done.1
  40.5 0.1 add.24.refs_0_.refs_6_
  40.6 0.0 copy-start
  40.6 3.4 %collective-permute-start.3 = (bf16[160,1024]{1,0:T(8,128)(2,1)S(1)}, bf16[160,1024]{1,0:T(8,128)(2,1)S(1)}, u32[]{:S(2)}, u32[]{:S(2)}) collective-permute-start(bf16[160,1024]{1,0:T(8,128)(2,1)S(1)} %add.24.refs_0_.refs_6_), channel_id=1, source_target_pairs={{1,0},{3,2},{5,4},{7,6},{9,8},{11,10},{13,12},{15,14},{17,16},{19,... | collective-permute-start | bytes 983048 | tf_op jit(solution)/shard_map/ppermute | solution.py:18
  44.0 0.0 copy-done.2
  44.0 0.2 select_reduce_fusion
  44.2 0.8 %copy.7.ds_ref = s32[160,1]{1,0:T(8,128)} copy(s32[160,1]{0,1:T(1,128)S(1)} %bitcast.7) | data formatting | bytes 1280 | tf_op jit(solution)/shard_map/broadcast_in_dim | solution.py:135
  45.0 0.6 pad_add_fusion.qs_ref
  45.6 0.0 collective-permute-done.5.refs_4_.refs_10_
  45.6 0.0 collective-permute-done.4.refs_2_.refs_8_
  45.6 0.0 collective-permute-done.3.refs_1_.refs_7_
  45.6 0.0 copy-done.1
  45.6 0.0 copy-done.3
  45.6 0.0 copy-done
  45.6 0.7 %copy-done.4 = bf16[160,1024]{1,0:T(8,128)(2,1)} copy-done((bf16[160,1024]{1,0:T(8,128)(2,1)}, bf16[160,1024]{1,0:T(8,128)(2,1)S(1)}, u32[]{:S(2)}) %copy-start.4) | copy-done | bytes 327704
  46.3 0.2 copy-done.5
  46.4 0.7 %copy-done.6 = bf16[160,1024]{1,0:T(8,128)(2,1)} copy-done((bf16[160,1024]{1,0:T(8,128)(2,1)}, bf16[160,1024]{1,0:T(8,128)(2,1)S(1)}, u32[]{:S(2)}) %copy-start.6) | copy-done | bytes 327704
  47.2 14.5 %shard_map.55 = bf16[160,4096]{1,0:T(8,128)(2,1)} custom-call(s32[2]{0:T(128)} %pad_add_fusion.qs_ref, f32[32]{0:T(128)} %scale_ref.1, s32[160,1]{1,0:T(8,128)} %copy.7.ds_ref, bf16[160,4096]{1,0:T(8,128)(2,1)} %q_ref.1, bf16[160,1024]{1,0:T(8,128)(2,1)} %copy-done, bf16[160,1024]{1,0:T(8,128)(2,1)} %copy-done.6, bf16[160,1024]{1,0:T(8,128)(2,1)} %copy-done.5, ...), custom_call_target="tpu_custom_call" | custom-call | flops 2097152000 | bytes 4259840 | tf_op jit(solution)/shard_map/pallas_call | solution.py:99
  (7 shorter events, 0.1 us)
Async XLA Ops:
  0.0 44.0 %copy-start.2 = (s32[384]{0:T(512)S(1)}, s32[384]{0:T(512)}, u32[]{:S(2)}) copy-start(s32[384]{0:T(512)} %param.8) | copy-start | bytes 4612
  1.9 43.7 %copy-start.1 = (bf16[160,1024]{1,0:T(8,128)(2,1)}, bf16[160,1024]{1,0:T(8,128)(2,1)S(1)}, u32[]{:S(2)}) copy-start(bf16[160,1024]{1,0:T(8,128)(2,1)S(1)} %constant_dynamic-update-slice_fusion.refs_5_.refs_11_) | copy-start | bytes 983044
  1.9 10.5 %collective-permute-start = (bf16[160,1024]{1,0:T(8,128)(2,1)S(1)}, bf16[160,1024]{1,0:T(8,128)(2,1)S(1)}, u32[]{:S(2)}, u32[]{:S(2)}) collective-permute-start(bf16[160,1024]{1,0:T(8,128)(2,1)S(1)} %constant_dynamic-update-slice_fusion.refs_5_.refs_11_), channel_id=1, source_target_pairs={{0,2},{1,3},{2,4},{3,5},{4,6},{5,7},{6,8},{7,9},{8,10},{9,11},{10,... | collective-permute-start | bytes 983048 | tf_op jit(solution)/shard_map/ppermute | solution.py:18
  5.1 40.5 %collective-permute-start.5 = (bf16[160,1024]{1,0:T(8,128)(2,1)S(1)}, bf16[160,1024]{1,0:T(8,128)(2,1)S(1)}, u32[]{:S(2)}, u32[]{:S(2)}) collective-permute-start(bf16[160,1024]{1,0:T(8,128)(2,1)S(1)} %constant_dynamic-update-slice_fusion.refs_5_.refs_11_), channel_id=1, source_target_pairs={{0,1},{2,3},{4,5},{6,7},{8,9},{10,11},{12,13},{14,15},{16,17},{18,... | collective-permute-start | bytes 983048 | tf_op jit(solution)/shard_map/ppermute | solution.py:18
  6.4 34.1 %collective-permute-start.2 = (bf16[160,1024]{1,0:T(8,128)(2,1)S(1)}, bf16[160,1024]{1,0:T(8,128)(2,1)S(1)}, u32[]{:S(2)}, u32[]{:S(2)}) collective-permute-start(bf16[160,1024]{1,0:T(8,128)(2,1)S(1)} %constant_dynamic-update-slice_fusion.refs_5_.refs_11_), channel_id=1, source_target_pairs={{12,16},{13,17},{14,18},{15,19},{28,32},{29,33},{30,34},{31,35},{4... | collective-permute-start | bytes 983048 | tf_op jit(solution)/shard_map/ppermute | solution.py:18
  12.4 33.2 %copy-start.3 = (bf16[160,1024]{1,0:T(8,128)(2,1)}, bf16[160,1024]{1,0:T(8,128)(2,1)S(1)}, u32[]{:S(2)}) copy-start(bf16[160,1024]{1,0:T(8,128)(2,1)S(1)} %collective-permute-done.refs_3_.refs_9_) | copy-start | bytes 983044
  12.4 28.1 %collective-permute-start.1 = (bf16[160,1024]{1,0:T(8,128)(2,1)S(1)}, bf16[160,1024]{1,0:T(8,128)(2,1)S(1)}, u32[]{:S(2)}, u32[]{:S(2)}) collective-permute-start(bf16[160,1024]{1,0:T(8,128)(2,1)S(1)} %collective-permute-done.refs_3_.refs_9_), channel_id=1, source_target_pairs={{0,2},{1,3},{2,4},{3,5},{4,6},{5,7},{6,8},{7,9},{8,10},{9,11},{10,... | collective-permute-start | bytes 983048 | tf_op jit(solution)/shard_map/ppermute | solution.py:18
  15.8 29.8 %collective-permute-start.4 = (bf16[160,1024]{1,0:T(8,128)(2,1)S(1)}, bf16[160,1024]{1,0:T(8,128)(2,1)S(1)}, u32[]{:S(2)}, u32[]{:S(2)}) collective-permute-start(bf16[160,1024]{1,0:T(8,128)(2,1)S(1)} %collective-permute-done.refs_3_.refs_9_), channel_id=1, source_target_pairs={{0,1},{2,3},{4,5},{6,7},{8,9},{10,11},{12,13},{14,15},{16,17},{18,... | collective-permute-start | bytes 983048 | tf_op jit(solution)/shard_map/ppermute | solution.py:18
  40.6 5.0 %copy-start = (bf16[160,1024]{1,0:T(8,128)(2,1)}, bf16[160,1024]{1,0:T(8,128)(2,1)S(1)}, u32[]{:S(2)}) copy-start(bf16[160,1024]{1,0:T(8,128)(2,1)S(1)} %add.24.refs_0_.refs_6_) | copy-start | bytes 983044
  40.6 5.0 %collective-permute-start.3 = (bf16[160,1024]{1,0:T(8,128)(2,1)S(1)}, bf16[160,1024]{1,0:T(8,128)(2,1)S(1)}, u32[]{:S(2)}, u32[]{:S(2)}) collective-permute-start(bf16[160,1024]{1,0:T(8,128)(2,1)S(1)} %add.24.refs_0_.refs_6_), channel_id=1, source_target_pairs={{1,0},{3,2},{5,4},{7,6},{9,8},{11,10},{13,12},{15,14},{17,16},{19,... | collective-permute-start | bytes 983048 | tf_op jit(solution)/shard_map/ppermute | solution.py:18
  45.6 0.7 %copy-start.4 = (bf16[160,1024]{1,0:T(8,128)(2,1)}, bf16[160,1024]{1,0:T(8,128)(2,1)S(1)}, u32[]{:S(2)}) copy-start(bf16[160,1024]{1,0:T(8,128)(2,1)S(1)} %collective-permute-done.5.refs_4_.refs_10_) | copy-start | bytes 983044
  45.6 0.9 %copy-start.5 = (bf16[160,1024]{1,0:T(8,128)(2,1)}, bf16[160,1024]{1,0:T(8,128)(2,1)S(1)}, u32[]{:S(2)}) copy-start(bf16[160,1024]{1,0:T(8,128)(2,1)S(1)} %collective-permute-done.4.refs_2_.refs_8_) | copy-start | bytes 983044
  46.4 0.7 %copy-start.6 = (bf16[160,1024]{1,0:T(8,128)(2,1)}, bf16[160,1024]{1,0:T(8,128)(2,1)S(1)}, u32[]{:S(2)}) copy-start(bf16[160,1024]{1,0:T(8,128)(2,1)S(1)} %collective-permute-done.3.refs_1_.refs_7_) | copy-start | bytes 983044

commit v8 on v6

--- a/solution.py
+++ b/solution.py
@@ -11,6 +11,7 @@
 HK = 4
 HD = 128
 WIN_DEV = 4
+CHUNK = 16
 AXES = ("ctx", "grp")
 
 
@@ -50,7 +51,8 @@
 
 
 def attend_kernel(qs_ref, scale_ref, ds_ref, q_ref, *refs):
-    kv_refs, o_ref = refs[:-1], refs[-1]
+    kv_refs, o_ref = refs[:-5], refs[-5]
+    s_ref, w_ref, coef_ref, lo_ref = refs[-4:]
     half = len(kv_refs) // 2
     rows = q_ref.shape[0]
     width = rows * (half - 1)
@@ -65,29 +67,35 @@
         back1 = jnp.where(even, swap2, even_own)
         return jnp.concatenate([back4, back3, back2, back1, own], axis=0)
 
-    col = lax.broadcasted_iota(jnp.int32, (rows, width), 1)
-    row = lax.broadcasted_iota(jnp.int32, (rows, width), 0)
     doc_start = ds_ref[...]
-    live = (col >= doc_start - (q_start - doc_most)) & (col <= row + doc_most)
     k = ordered(kv_refs[:half])
     v = ordered(kv_refs[half:])
     q_pos = q_start + lax.broadcasted_iota(jnp.int32, (rows, 1), 0)
     logv = jnp.log((q_pos - doc_start + 1).astype(jnp.float32))
     per_group = HQ // HK
-    coef = jnp.stack(
-        [scale_ref[head * per_group + g] * logv / jnp.sqrt(jnp.float32(HD)) for g in range(per_group)]
-    )
+    for g in range(per_group):
+        coef_ref[g * rows : (g + 1) * rows, :] = scale_ref[head * per_group + g] * logv / jnp.sqrt(jnp.float32(HD))
+    lo_ref[...] = doc_start - (q_start - doc_most)
     q = jnp.concatenate([q_ref[:, g * HD : (g + 1) * HD] for g in range(per_group)], axis=0)
-    s = lax.dot_general(q, k, (((1,), (1,)), ((), ())), preferred_element_type=jnp.float32)
-    s = jnp.where(live[None], s.reshape(per_group, rows, width) * coef, -jnp.inf)
-    m = jnp.max(s, axis=2, keepdims=True)
-    p = jnp.exp(s - m)
-    l = jnp.sum(p, axis=2, keepdims=True)
-    w = (p * (1.0 / l)).astype(jnp.bfloat16).reshape(per_group * rows, width)
-    o = jnp.dot(w, v, preferred_element_type=jnp.float32)
+    s_ref[...] = lax.dot_general(q, k, (((1,), (1,)), ((), ())), preferred_element_type=jnp.float32)
+
+    def chunk(c, carry):
+        r0 = pl.multiple_of(c * CHUNK, CHUNK)
+        i0 = pl.multiple_of((c % (rows // CHUNK)) * CHUNK, CHUNK)
+        col = lax.broadcasted_iota(jnp.int32, (CHUNK, width), 1)
+        row = lax.broadcasted_iota(jnp.int32, (CHUNK, width), 0) + i0
+        live = (col >= lo_ref[pl.ds(i0, CHUNK), :]) & (col <= row + doc_most)
+        x = jnp.where(live, s_ref[pl.ds(r0, CHUNK), :] * coef_ref[pl.ds(r0, CHUNK), :], -jnp.inf)
+        m = jnp.max(x, axis=1, keepdims=True)
+        p = jnp.exp(x - m)
+        l = jnp.sum(p, axis=1, keepdims=True)
+        w_ref[pl.ds(r0, CHUNK), :] = (p * (1.0 / l)).astype(jnp.bfloat16)
+        return carry
+
+    lax.fori_loop(0, per_group * rows // CHUNK, chunk, 0, unroll=2)
+    o = jnp.dot(w_ref[...], v, preferred_element_type=jnp.float32)
     for g in range(per_group):
         o_ref[:, g * HD : (g + 1) * HD] = o[g * rows : (g + 1) * rows].astype(o_ref.dtype)
-
 
 def attend(queries, blocks, where, scale, doc_start, interpret=False):
     rows = queries.shape[0]
@@ -109,6 +117,12 @@
         + v_specs,
         out_specs=pl.BlockSpec((rows, per_group * HD), lambda h: (0, h)),
         out_shape=jax.ShapeDtypeStruct((rows, HQ * HD), jnp.bfloat16),
+        scratch_shapes=[
+            pltpu.VMEM((per_group * rows, width), jnp.float32),
+            pltpu.VMEM((per_group * rows, width), jnp.bfloat16),
+            pltpu.VMEM((per_group * rows, 1), jnp.float32),
+            pltpu.VMEM((rows, 1), jnp.int32),
+        ],
         cost_estimate=pl.CostEstimate(
             flops=flops,
             transcendentals=HQ * rows * width,

time: 58.6 us -> 99.8 us (1.70)
  Pallas kernels: 14.5 us -> 55.7 us
    pallas_call x1, Pallas kernels: 14.5 us -> 55.7 us  [attend(): pl.pallas_call(attend_kernel, grid=(HK,), in_specs=[pl.BlockSpec(memory_s...]
  transfers between devices with their start and end apart: 6 -> 6, of which waited for: 2 -> 2; matrix products, arithmetic and copies ran while one was open for 5% -> 3% of each run, Pallas kernels for 0% -> 0%
where the time goes in v8:
time: 99.8 us; the launch traced here: 99.5 us
  Pallas kernels  55.7 us (56%)
  waiting for transfers between devices  20.1 us (20%)
  starting transfers between devices  17.2 us (17%)
  local copies, waits for them, and re-layouts  4.41 us (4%)
  other arithmetic  1.97 us (2%)
    pallas_call x1, Pallas kernels, attend(): pl.pallas_call(attend_kernel, grid=(HK,), in_specs=[pl.BlockSpec(memory_s...  55.7 us
    ppermute x6, waiting for transfers between devices, send(): return lax.ppermute(x, AXES, pairs)  20.1 us
    ppermute x6, starting transfers between devices, send(): return lax.ppermute(x, AXES, pairs)  17.2 us
    unnamed x15, local copies, waits for them, and re-layouts  2.52 us
  transfers between devices with their start and end apart: 6, of which 2 were waited for; matrix products, arithmetic and copies ran while one was open for 3% of the time, Pallas kernels for 0%

profile of v8, /device:TPU:15, one launch (start us, length us, event | category | flops | bytes accessed | tf_op | source)
XLA Modules:
  0.0 99.5 jit_solution(18400265744809331722)
XLA Ops:
  0.0 0.9 constant_dynamic-update-slice_fusion.1
  0.9 0.9 constant_dynamic-update-slice_fusion.refs_5_.refs_11_
  1.9 0.0 copy-start.1
  1.9 3.2 %collective-permute-start = (bf16[160,1024]{1,0:T(8,128)(2,1)S(1)}, bf16[160,1024]{1,0:T(8,128)(2,1)S(1)}, u32[]{:S(2)}, u32[]{:S(2)}) collective-permute-start(bf16[160,1024]{1,0:T(8,128)(2,1)S(1)} %constant_dynamic-update-slice_fusion.refs_5_.refs_11_), channel_id=1, source_target_pairs={{0,2},{1,3},{2,4},{3,5},{4,6},{5,7},{6,8},{7,9},{8,10},{9,11},{10,... | collective-permute-start | bytes 983048 | tf_op jit(solution)/shard_map/ppermute | solution.py:19
  5.1 1.3 %collective-permute-start.5 = (bf16[160,1024]{1,0:T(8,128)(2,1)S(1)}, bf16[160,1024]{1,0:T(8,128)(2,1)S(1)}, u32[]{:S(2)}, u32[]{:S(2)}) collective-permute-start(bf16[160,1024]{1,0:T(8,128)(2,1)S(1)} %constant_dynamic-update-slice_fusion.refs_5_.refs_11_), channel_id=1, source_target_pairs={{0,1},{2,3},{4,5},{6,7},{8,9},{10,11},{12,13},{14,15},{16,17},{18,... | collective-permute-start | bytes 983048 | tf_op jit(solution)/shard_map/ppermute | solution.py:19
  6.4 0.7 collective-permute-start.2
  7.1 1.0 reduce-window.9
  8.1 0.1 slice.7
  8.2 4.2 %collective-permute-done.refs_3_.refs_9_ = bf16[160,1024]{1,0:T(8,128)(2,1)S(1)} collective-permute-done((bf16[160,1024]{1,0:T(8,128)(2,1)S(1)}, bf16[160,1024]{1,0:T(8,128)(2,1)S(1)}, u32[]{:S(2)}, u32[]{:S(2)}) %collective-permute-start) | collective-permute-done | bytes 327712 | tf_op jit(solution)/shard_map/ppermute | solution.py:19
  12.4 3.2 %collective-permute-start.1 = (bf16[160,1024]{1,0:T(8,128)(2,1)S(1)}, bf16[160,1024]{1,0:T(8,128)(2,1)S(1)}, u32[]{:S(2)}, u32[]{:S(2)}) collective-permute-start(bf16[160,1024]{1,0:T(8,128)(2,1)S(1)} %collective-permute-done.refs_3_.refs_9_), channel_id=1, source_target_pairs={{0,2},{1,3},{2,4},{3,5},{4,6},{5,7},{6,8},{7,9},{8,10},{9,11},{10,... | collective-permute-start | bytes 983048 | tf_op jit(solution)/shard_map/ppermute | solution.py:19
  15.6 0.1 slice_reduce_fusion
  15.7 0.1 add_bitcast_fusion
  15.8 3.7 %collective-permute-start.4 = (bf16[160,1024]{1,0:T(8,128)(2,1)S(1)}, bf16[160,1024]{1,0:T(8,128)(2,1)S(1)}, u32[]{:S(2)}, u32[]{:S(2)}) collective-permute-start(bf16[160,1024]{1,0:T(8,128)(2,1)S(1)} %collective-permute-done.refs_3_.refs_9_), channel_id=1, source_target_pairs={{0,1},{2,3},{4,5},{6,7},{8,9},{10,11},{12,13},{14,15},{16,17},{18,... | collective-permute-start | bytes 983048 | tf_op jit(solution)/shard_map/ppermute | solution.py:19
  19.5 0.0 collective-permute-done.2
  19.5 16.0 %collective-permute-done.1 = bf16[160,1024]{1,0:T(8,128)(2,1)S(1)} collective-permute-done((bf16[160,1024]{1,0:T(8,128)(2,1)S(1)}, bf16[160,1024]{1,0:T(8,128)(2,1)S(1)}, u32[]{:S(2)}, u32[]{:S(2)}) %collective-permute-start.1) | collective-permute-done | bytes 327712 | tf_op jit(solution)/shard_map/ppermute | solution.py:19
  35.5 0.1 add.24.refs_0_.refs_6_
  35.6 0.0 copy-start
  35.6 5.1 %collective-permute-start.3 = (bf16[160,1024]{1,0:T(8,128)(2,1)S(1)}, bf16[160,1024]{1,0:T(8,128)(2,1)S(1)}, u32[]{:S(2)}, u32[]{:S(2)}) collective-permute-start(bf16[160,1024]{1,0:T(8,128)(2,1)S(1)} %add.24.refs_0_.refs_6_), channel_id=1, source_target_pairs={{1,0},{3,2},{5,4},{7,6},{9,8},{11,10},{13,12},{15,14},{17,16},{19,... | collective-permute-start | bytes 983048 | tf_op jit(solution)/shard_map/ppermute | solution.py:19
  40.7 0.0 copy-done.2
  40.7 0.2 select_reduce_fusion
  40.9 0.8 copy.7.ds_ref
  41.6 0.6 pad_add_fusion.qs_ref
  42.2 0.0 collective-permute-done.5.refs_4_.refs_10_
  42.2 0.0 collective-permute-done.4.refs_2_.refs_8_
  42.2 0.0 copy-start.5
  42.2 0.0 collective-permute-done.3.refs_1_.refs_7_
  42.3 0.0 copy-done.1
  42.3 0.0 copy-done.3
  42.3 0.7 copy-done.4
  42.9 0.2 copy-done.5
  43.1 0.7 copy-done.6
  43.9 55.7 %shard_map.55 = bf16[160,4096]{1,0:T(8,128)(2,1)} custom-call(s32[2]{0:T(128)} %pad_add_fusion.qs_ref, f32[32]{0:T(128)} %scale_ref.1, s32[160,1]{1,0:T(8,128)} %copy.7.ds_ref, bf16[160,4096]{1,0:T(8,128)(2,1)} %q_ref.1, bf16[160,1024]{1,0:T(8,128)(2,1)} %copy-done, bf16[160,1024]{1,0:T(8,128)(2,1)} %copy-done.6, bf16[160,1024]{1,0:T(8,128)(2,1)} %copy-done.5, ...), custom_call_target="tpu_custom_call" | custom-call | flops 2097152000 | bytes 4259840 | tf_op jit(solution)/shard_map/pallas_call | solution.py:107
  (7 shorter events, 0.1 us)
Async XLA Ops:
  0.0 40.7 %copy-start.2 = (s32[384]{0:T(512)S(1)}, s32[384]{0:T(512)}, u32[]{:S(2)}) copy-start(s32[384]{0:T(512)} %param.8) | copy-start | bytes 4612
  1.9 40.4 %copy-start.1 = (bf16[160,1024]{1,0:T(8,128)(2,1)}, bf16[160,1024]{1,0:T(8,128)(2,1)S(1)}, u32[]{:S(2)}) copy-start(bf16[160,1024]{1,0:T(8,128)(2,1)S(1)} %constant_dynamic-update-slice_fusion.refs_5_.refs_11_) | copy-start | bytes 983044
  1.9 10.5 %collective-permute-start = (bf16[160,1024]{1,0:T(8,128)(2,1)S(1)}, bf16[160,1024]{1,0:T(8,128)(2,1)S(1)}, u32[]{:S(2)}, u32[]{:S(2)}) collective-permute-start(bf16[160,1024]{1,0:T(8,128)(2,1)S(1)} %constant_dynamic-update-slice_fusion.refs_5_.refs_11_), channel_id=1, source_target_pairs={{0,2},{1,3},{2,4},{3,5},{4,6},{5,7},{6,8},{7,9},{8,10},{9,11},{10,... | collective-permute-start | bytes 983048 | tf_op jit(solution)/shard_map/ppermute | solution.py:19
  5.1 37.1 %collective-permute-start.5 = (bf16[160,1024]{1,0:T(8,128)(2,1)S(1)}, bf16[160,1024]{1,0:T(8,128)(2,1)S(1)}, u32[]{:S(2)}, u32[]{:S(2)}) collective-permute-start(bf16[160,1024]{1,0:T(8,128)(2,1)S(1)} %constant_dynamic-update-slice_fusion.refs_5_.refs_11_), channel_id=1, source_target_pairs={{0,1},{2,3},{4,5},{6,7},{8,9},{10,11},{12,13},{14,15},{16,17},{18,... | collective-permute-start | bytes 983048 | tf_op jit(solution)/shard_map/ppermute | solution.py:19
  6.4 13.1 %collective-permute-start.2 = (bf16[160,1024]{1,0:T(8,128)(2,1)S(1)}, bf16[160,1024]{1,0:T(8,128)(2,1)S(1)}, u32[]{:S(2)}, u32[]{:S(2)}) collective-permute-start(bf16[160,1024]{1,0:T(8,128)(2,1)S(1)} %constant_dynamic-update-slice_fusion.refs_5_.refs_11_), channel_id=1, source_target_pairs={{188,192},{189,193},{380,384},{381,385},{572,576},{573,577}} | collective-permute-start | bytes 983048 | tf_op jit(solution)/shard_map/ppermute | solution.py:19
  12.4 29.9 %copy-start.3 = (bf16[160,1024]{1,0:T(8,128)(2,1)}, bf16[160,1024]{1,0:T(8,128)(2,1)S(1)}, u32[]{:S(2)}) copy-start(bf16[160,1024]{1,0:T(8,128)(2,1)S(1)} %collective-permute-done.refs_3_.refs_9_) | copy-start | bytes 983044
  12.4 23.1 %collective-permute-start.1 = (bf16[160,1024]{1,0:T(8,128)(2,1)S(1)}, bf16[160,1024]{1,0:T(8,128)(2,1)S(1)}, u32[]{:S(2)}, u32[]{:S(2)}) collective-permute-start(bf16[160,1024]{1,0:T(8,128)(2,1)S(1)} %collective-permute-done.refs_3_.refs_9_), channel_id=1, source_target_pairs={{0,2},{1,3},{2,4},{3,5},{4,6},{5,7},{6,8},{7,9},{8,10},{9,11},{10,... | collective-permute-start | bytes 983048 | tf_op jit(solution)/shard_map/ppermute | solution.py:19
  15.8 26.5 %collective-permute-start.4 = (bf16[160,1024]{1,0:T(8,128)(2,1)S(1)}, bf16[160,1024]{1,0:T(8,128)(2,1)S(1)}, u32[]{:S(2)}, u32[]{:S(2)}) collective-permute-start(bf16[160,1024]{1,0:T(8,128)(2,1)S(1)} %collective-permute-done.refs_3_.refs_9_), channel_id=1, source_target_pairs={{0,1},{2,3},{4,5},{6,7},{8,9},{10,11},{12,13},{14,15},{16,17},{18,... | collective-permute-start | bytes 983048 | tf_op jit(solution)/shard_map/ppermute | solution.py:19
  35.6 6.7 %copy-start = (bf16[160,1024]{1,0:T(8,128)(2,1)}, bf16[160,1024]{1,0:T(8,128)(2,1)S(1)}, u32[]{:S(2)}) copy-start(bf16[160,1024]{1,0:T(8,128)(2,1)S(1)} %add.24.refs_0_.refs_6_) | copy-start | bytes 983044
  35.6 6.7 %collective-permute-start.3 = (bf16[160,1024]{1,0:T(8,128)(2,1)S(1)}, bf16[160,1024]{1,0:T(8,128)(2,1)S(1)}, u32[]{:S(2)}, u32[]{:S(2)}) collective-permute-start(bf16[160,1024]{1,0:T(8,128)(2,1)S(1)} %add.24.refs_0_.refs_6_), channel_id=1, source_target_pairs={{1,0},{3,2},{5,4},{7,6},{9,8},{11,10},{13,12},{15,14},{17,16},{19,... | collective-permute-start | bytes 983048 | tf_op jit(solution)/shard_map/ppermute | solution.py:19
  42.2 0.7 copy-start.4
  42.2 0.9 copy-start.5
  43.1 0.7 copy-start.6

commit v9 on v6

--- a/solution.py
+++ b/solution.py
@@ -32,7 +32,7 @@
     return tuple(i for i in range(4, len(flat)) if hops(chips[i - 2], chips[i]) >= 3)
 
 
-def window_blocks(own, far):
+def window_blocks(own, far, early):
     count = lax.axis_size("ctx") * lax.axis_size("grp")
     ahead2 = [(i, i + 2) for i in range(count - 2)]
     to_odd = [(i, i + 1) for i in range(0, count - 1, 2)]
@@ -40,13 +40,14 @@
     swap = to_odd + to_even
     far_set = set(far)
     back2 = send(own, ahead2)
+    back2, early = lax.optimization_barrier((back2, early))
     from_even_own = send(own, to_odd)
     direct4 = send(own, [(i - 4, i) for i in far])
     forward2 = [(i, j) for i, j in ahead2 if j not in far_set]
     back4 = send(back2, forward2) + direct4 if far else send(back2, forward2)
     swapped2 = send(back2, swap)
     from_odd4 = send(back4, to_even)
-    return [back4, from_odd4, swapped2, back2, from_even_own, own]
+    return [back4, from_odd4, swapped2, back2, from_even_own, own], early
 
 
 def attend_kernel(qs_ref, scale_ref, ds_ref, q_ref, *refs):
@@ -127,12 +128,12 @@
     q_start = ctx_index * slab_rows + grp_index * tok_rows
     q_pos = q_start + jnp.arange(tok_rows, dtype=jnp.int32)
     own = jnp.concatenate([keys, values], axis=1)
-    blocks = window_blocks(own, far)
     totals = jnp.cumsum(lengths, dtype=jnp.int32)
     before = totals[None, :] <= q_pos[:, None]
-    doc_start = jnp.sum(jnp.where(before, lengths[None, :], 0), axis=1, dtype=jnp.int32)
+    doc_start = jnp.sum(jnp.where(before, lengths[None, :], 0), axis=1, keepdims=True, dtype=jnp.int32)
     where = jnp.stack([q_start, grp_index % 2]).astype(jnp.int32)
-    return attend(queries, blocks, where, ssmax_scale, doc_start[:, None])
+    blocks, (where, doc_start) = window_blocks(own, far, (where, doc_start))
+    return attend(queries, blocks, where, ssmax_scale, doc_start)
 
 
 def solution(mesh):

time: 58.6 us -> 62.3 us (1.063)
  waiting for transfers between devices: 20.1 us -> 23.8 us
  other arithmetic: 1.97 us -> 2.73 us
    ppermute x6, waiting for transfers between devices: 20.1 us -> 23.8 us  [send(): return lax.ppermute(x, AXES, pairs)]
    broadcast_in_dim x1 -> x0, local copies, waits for them, and re-layouts: 0.77 us -> none  [body(): return attend(queries, blocks, where, ssmax_scale, doc_start[:, None])]
    optimization_barrier x0 -> x1, local copies, waits for them, and re-layouts: none -> 0.76 us  [window_blocks(): back2, early = lax.optimization_barrier((back2, early))]
    reduce_sum x1, other arithmetic: 0.19 us -> 0.87 us  [body(): jnp.sum(jnp.where(before, lengths[None, :], 0), axis=1, keepdims=True, dt...]
    unnamed x15 -> x13, local copies, waits for them, and re-layouts: 2.52 us -> 2.04 us
  transfers between devices with their start and end apart: 6 -> 6, of which waited for: 2 -> 3; matrix products, arithmetic and copies ran while one was open for 5% -> 6% of each run, Pallas kernels for 0% -> 0%
where the time goes in v9:
time: 62.3 us; the launch traced here: 62 us
  waiting for transfers between devices  23.8 us (38%)
  starting transfers between devices  16.9 us (27%)
  Pallas kernels  14.5 us (23%)
  local copies, waits for them, and re-layouts  3.92 us (6%)
  other arithmetic  2.73 us (4%)
    ppermute x6, waiting for transfers between devices, send(): return lax.ppermute(x, AXES, pairs)  23.8 us
    ppermute x6, starting transfers between devices, send(): return lax.ppermute(x, AXES, pairs)  16.9 us
    pallas_call x1, Pallas kernels, attend(): pl.pallas_call(attend_kernel, grid=(HK,), in_specs=[pl.BlockSpec(memory_s...  14.5 us
    unnamed x13, local copies, waits for them, and re-layouts  2.04 us
  transfers between devices with their start and end apart: 6, of which 3 were waited for; matrix products, arithmetic and copies ran while one was open for 6% of the time, Pallas kernels for 0%

profile of v9, /device:TPU:15, one launch (start us, length us, event | category | flops | bytes accessed | tf_op | source)
XLA Modules:
  0.0 62.0 jit_solution(8972516119752002955)
XLA Ops:
  0.0 0.9 %constant_dynamic-update-slice_fusion.1 = bf16[160,1024]{1,0:T(8,128)(2,1)S(1)} fusion(bf16[160,512]{1,0:T(8,128)(2,1)} %param.6), kind=kLoop, calls=%fused_computation.2 | loop fusion | bytes 327680
  0.9 0.9 %constant_dynamic-update-slice_fusion.refs_5_.refs_11_ = bf16[160,1024]{1,0:T(8,128)(2,1)S(1)} fusion(bf16[160,1024]{1,0:T(8,128)(2,1)S(1)} %constant_dynamic-update-slice_fusion.1, bf16[160,512]{1,0:T(8,128)(2,1)} %param.7), kind=kLoop, calls=%fused_computation.1 | loop fusion | bytes 327680 | tf_op jit(solution)/shard_map/concatenate | solution.py:130
  1.9 0.0 copy-start.1
  1.9 0.7 %collective-permute-start.2 = (bf16[160,1024]{1,0:T(8,128)(2,1)S(1)}, bf16[160,1024]{1,0:T(8,128)(2,1)S(1)}, u32[]{:S(2)}, u32[]{:S(2)}) collective-permute-start(bf16[160,1024]{1,0:T(8,128)(2,1)S(1)} %constant_dynamic-update-slice_fusion.refs_5_.refs_11_), channel_id=1, source_target_pairs={{188,192},{189,193},{380,384},{381,385},{572,576},{573,577}} | collective-permute-start | bytes 983048 | tf_op jit(solution)/shard_map/ppermute | solution.py:18
  2.6 3.2 %collective-permute-start = (bf16[160,1024]{1,0:T(8,128)(2,1)S(1)}, bf16[160,1024]{1,0:T(8,128)(2,1)S(1)}, u32[]{:S(2)}, u32[]{:S(2)}) collective-permute-start(bf16[160,1024]{1,0:T(8,128)(2,1)S(1)} %constant_dynamic-update-slice_fusion.refs_5_.refs_11_), channel_id=1, source_target_pairs={{0,2},{1,3},{2,4},{3,5},{4,6},{5,7},{6,8},{7,9},{8,10},{9,11},{10,... | collective-permute-start | bytes 983048 | tf_op jit(solution)/shard_map/ppermute | solution.py:18
  5.8 1.0 %reduce-window.9 = s32[3,128]{1,0:T(4,128)S(1)} reduce-window(s32[3,128]{1,0:T(4,128)} %bitcast.6, s32[]{:T(128)} %constant.26.clone.1), window={size=1x128 pad=0_0x127_0}, to_apply=%region_0.0 | reduce-window | flops 48768 | bytes 3076 | tf_op jit(solution)/shard_map/reduce-window
  6.8 0.1 slice.7
  6.9 0.1 slice_reduce_fusion
  7.0 0.7 %pad_add_fusion.qs_ref = s32[2]{0:T(128)} fusion(s32[1]{0:T(128)} %bitcast.1, s32[1]{0:T(128)} %bitcast), kind=kLoop, calls=%fused_computation.6 | loop fusion | flops 2 | bytes 16 | tf_op jit(solution)/shard_map/stack | solution.py:134
  7.7 0.1 add_bitcast_fusion
  7.8 0.9 %select_reduce_fusion = s32[160]{0:T(256)S(1)} fusion(s32[384]{0:T(512)} %param.8, s32[384]{0:T(512)S(1)} %add_bitcast_fusion, s32[160]{0:T(256)S(1)} %iota_add_fusion), kind=kLoop, calls=%fused_computation | loop fusion | flops 184160 | bytes 4352 | tf_op jit(solution)/shard_map/reduce_sum | solution.py:133
  8.6 4.4 %collective-permute-done.refs_3_.refs_9_ = bf16[160,1024]{1,0:T(8,128)(2,1)S(1)} collective-permute-done((bf16[160,1024]{1,0:T(8,128)(2,1)S(1)}, bf16[160,1024]{1,0:T(8,128)(2,1)S(1)}, u32[]{:S(2)}, u32[]{:S(2)}) %collective-permute-start) | collective-permute-done | bytes 327712 | tf_op jit(solution)/shard_map/ppermute | solution.py:18
  13.0 3.2 %collective-permute-start.1 = (bf16[160,1024]{1,0:T(8,128)(2,1)S(1)}, bf16[160,1024]{1,0:T(8,128)(2,1)S(1)}, u32[]{:S(2)}, u32[]{:S(2)}) collective-permute-start(bf16[160,1024]{1,0:T(8,128)(2,1)S(1)} %collective-permute-done.refs_3_.refs_9_), channel_id=1, source_target_pairs={{0,2},{1,3},{2,4},{3,5},{4,6},{5,7},{6,8},{7,9},{8,10},{9,11},{10,... | collective-permute-start | bytes 983048 | tf_op jit(solution)/shard_map/ppermute | solution.py:18
  16.2 1.3 %collective-permute-start.5 = (bf16[160,1024]{1,0:T(8,128)(2,1)S(1)}, bf16[160,1024]{1,0:T(8,128)(2,1)S(1)}, u32[]{:S(2)}, u32[]{:S(2)}) collective-permute-start(bf16[160,1024]{1,0:T(8,128)(2,1)S(1)} %constant_dynamic-update-slice_fusion.refs_5_.refs_11_), channel_id=1, source_target_pairs={{0,1},{2,3},{4,5},{6,7},{8,9},{10,11},{12,13},{14,15},{16,17},{18,... | collective-permute-start | bytes 983048 | tf_op jit(solution)/shard_map/ppermute | solution.py:18
  17.5 3.8 %collective-permute-start.4 = (bf16[160,1024]{1,0:T(8,128)(2,1)S(1)}, bf16[160,1024]{1,0:T(8,128)(2,1)S(1)}, u32[]{:S(2)}, u32[]{:S(2)}) collective-permute-start(bf16[160,1024]{1,0:T(8,128)(2,1)S(1)} %collective-permute-done.refs_3_.refs_9_), channel_id=1, source_target_pairs={{0,1},{2,3},{4,5},{6,7},{8,9},{10,11},{12,13},{14,15},{16,17},{18,... | collective-permute-start | bytes 983048 | tf_op jit(solution)/shard_map/ppermute | solution.py:18
  21.3 0.0 collective-permute-done.2
  21.3 19.0 %collective-permute-done.1 = bf16[160,1024]{1,0:T(8,128)(2,1)S(1)} collective-permute-done((bf16[160,1024]{1,0:T(8,128)(2,1)S(1)}, bf16[160,1024]{1,0:T(8,128)(2,1)S(1)}, u32[]{:S(2)}, u32[]{:S(2)}) %collective-permute-start.1) | collective-permute-done | bytes 327712 | tf_op jit(solution)/shard_map/ppermute | solution.py:18
  40.3 0.1 add.24.refs_0_.refs_6_
  40.4 0.0 copy-start
  40.4 4.8 %collective-permute-start.3 = (bf16[160,1024]{1,0:T(8,128)(2,1)S(1)}, bf16[160,1024]{1,0:T(8,128)(2,1)S(1)}, u32[]{:S(2)}, u32[]{:S(2)}) collective-permute-start(bf16[160,1024]{1,0:T(8,128)(2,1)S(1)} %add.24.refs_0_.refs_6_), channel_id=1, source_target_pairs={{1,0},{3,2},{5,4},{7,6},{9,8},{11,10},{13,12},{15,14},{17,16},{19,... | collective-permute-start | bytes 983048 | tf_op jit(solution)/shard_map/ppermute | solution.py:18
  45.2 0.8 %copy.7.ds_ref = s32[160,1]{1,0:T(8,128)} copy(s32[160,1]{0,1:T(1,128)S(1)} %bitcast.7) | data formatting | bytes 1280 | tf_op jit(solution)/shard_map/optimization_barrier | solution.py:43
  45.9 0.0 collective-permute-done.5.refs_4_.refs_10_
  45.9 0.0 collective-permute-done.4.refs_2_.refs_8_
  45.9 0.0 copy-start.4
  46.0 0.4 collective-permute-done.3.refs_1_.refs_7_
  46.4 0.0 copy-done.1
  46.4 0.0 copy-done.2
  46.4 0.0 copy-done
  46.4 0.2 copy-done.3
  46.6 0.1 copy-done.4
  46.8 0.7 %copy-done.5 = bf16[160,1024]{1,0:T(8,128)(2,1)} copy-done((bf16[160,1024]{1,0:T(8,128)(2,1)}, bf16[160,1024]{1,0:T(8,128)(2,1)S(1)}, u32[]{:S(2)}) %copy-start.5) | copy-done | bytes 327704
  47.5 14.5 %shard_map.55 = bf16[160,4096]{1,0:T(8,128)(2,1)} custom-call(s32[2]{0:T(128)} %pad_add_fusion.qs_ref, f32[32]{0:T(128)} %scale_ref.1, s32[160,1]{1,0:T(8,128)} %copy.7.ds_ref, bf16[160,4096]{1,0:T(8,128)(2,1)} %q_ref.1, bf16[160,1024]{1,0:T(8,128)(2,1)} %copy-done, bf16[160,1024]{1,0:T(8,128)(2,1)} %copy-done.5, bf16[160,1024]{1,0:T(8,128)(2,1)} %copy-done.4, ...), custom_call_target="tpu_custom_call" | custom-call | flops 2097152000 | bytes 4259840 | tf_op jit(solution)/shard_map/pallas_call | solution.py:100
  (5 shorter events, 0.0 us)
Async XLA Ops:
  1.9 44.5 %copy-start.1 = (bf16[160,1024]{1,0:T(8,128)(2,1)}, bf16[160,1024]{1,0:T(8,128)(2,1)S(1)}, u32[]{:S(2)}) copy-start(bf16[160,1024]{1,0:T(8,128)(2,1)S(1)} %constant_dynamic-update-slice_fusion.refs_5_.refs_11_) | copy-start | bytes 983044
  1.9 19.4 %collective-permute-start.2 = (bf16[160,1024]{1,0:T(8,128)(2,1)S(1)}, bf16[160,1024]{1,0:T(8,128)(2,1)S(1)}, u32[]{:S(2)}, u32[]{:S(2)}) collective-permute-start(bf16[160,1024]{1,0:T(8,128)(2,1)S(1)} %constant_dynamic-update-slice_fusion.refs_5_.refs_11_), channel_id=1, source_target_pairs={{188,192},{189,193},{380,384},{381,385},{572,576},{573,577}} | collective-permute-start | bytes 983048 | tf_op jit(solution)/shard_map/ppermute | solution.py:18
  2.6 10.5 %collective-permute-start = (bf16[160,1024]{1,0:T(8,128)(2,1)S(1)}, bf16[160,1024]{1,0:T(8,128)(2,1)S(1)}, u32[]{:S(2)}, u32[]{:S(2)}) collective-permute-start(bf16[160,1024]{1,0:T(8,128)(2,1)S(1)} %constant_dynamic-update-slice_fusion.refs_5_.refs_11_), channel_id=1, source_target_pairs={{0,2},{1,3},{2,4},{3,5},{4,6},{5,7},{6,8},{7,9},{8,10},{9,11},{10,... | collective-permute-start | bytes 983048 | tf_op jit(solution)/shard_map/ppermute | solution.py:18
  13.0 33.4 %copy-start.2 = (bf16[160,1024]{1,0:T(8,128)(2,1)}, bf16[160,1024]{1,0:T(8,128)(2,1)S(1)}, u32[]{:S(2)}) copy-start(bf16[160,1024]{1,0:T(8,128)(2,1)S(1)} %collective-permute-done.refs_3_.refs_9_) | copy-start | bytes 983044
  13.0 27.2 %collective-permute-start.1 = (bf16[160,1024]{1,0:T(8,128)(2,1)S(1)}, bf16[160,1024]{1,0:T(8,128)(2,1)S(1)}, u32[]{:S(2)}, u32[]{:S(2)}) collective-permute-start(bf16[160,1024]{1,0:T(8,128)(2,1)S(1)} %collective-permute-done.refs_3_.refs_9_), channel_id=1, source_target_pairs={{0,2},{1,3},{2,4},{3,5},{4,6},{5,7},{6,8},{7,9},{8,10},{9,11},{10,... | collective-permute-start | bytes 983048 | tf_op jit(solution)/shard_map/ppermute | solution.py:18
  16.2 29.7 %collective-permute-start.5 = (bf16[160,1024]{1,0:T(8,128)(2,1)S(1)}, bf16[160,1024]{1,0:T(8,128)(2,1)S(1)}, u32[]{:S(2)}, u32[]{:S(2)}) collective-permute-start(bf16[160,1024]{1,0:T(8,128)(2,1)S(1)} %constant_dynamic-update-slice_fusion.refs_5_.refs_11_), channel_id=1, source_target_pairs={{0,1},{2,3},{4,5},{6,7},{8,9},{10,11},{12,13},{14,15},{16,17},{18,... | collective-permute-start | bytes 983048 | tf_op jit(solution)/shard_map/ppermute | solution.py:18
  17.5 28.4 %collective-permute-start.4 = (bf16[160,1024]{1,0:T(8,128)(2,1)S(1)}, bf16[160,1024]{1,0:T(8,128)(2,1)S(1)}, u32[]{:S(2)}, u32[]{:S(2)}) collective-permute-start(bf16[160,1024]{1,0:T(8,128)(2,1)S(1)} %collective-permute-done.refs_3_.refs_9_), channel_id=1, source_target_pairs={{0,1},{2,3},{4,5},{6,7},{8,9},{10,11},{12,13},{14,15},{16,17},{18,... | collective-permute-start | bytes 983048 | tf_op jit(solution)/shard_map/ppermute | solution.py:18
  40.4 6.0 %copy-start = (bf16[160,1024]{1,0:T(8,128)(2,1)}, bf16[160,1024]{1,0:T(8,128)(2,1)S(1)}, u32[]{:S(2)}) copy-start(bf16[160,1024]{1,0:T(8,128)(2,1)S(1)} %add.24.refs_0_.refs_6_) | copy-start | bytes 983044
  40.4 6.0 %collective-permute-start.3 = (bf16[160,1024]{1,0:T(8,128)(2,1)S(1)}, bf16[160,1024]{1,0:T(8,128)(2,1)S(1)}, u32[]{:S(2)}, u32[]{:S(2)}) collective-permute-start(bf16[160,1024]{1,0:T(8,128)(2,1)S(1)} %add.24.refs_0_.refs_6_), channel_id=1, source_target_pairs={{1,0},{3,2},{5,4},{7,6},{9,8},{11,10},{13,12},{15,14},{17,16},{19,... | collective-permute-start | bytes 983048 | tf_op jit(solution)/shard_map/ppermute | solution.py:18
  45.9 0.7 %copy-start.3 = (bf16[160,1024]{1,0:T(8,128)(2,1)}, bf16[160,1024]{1,0:T(8,128)(2,1)S(1)}, u32[]{:S(2)}) copy-start(bf16[160,1024]{1,0:T(8,128)(2,1)S(1)} %collective-permute-done.5.refs_4_.refs_10_) | copy-start | bytes 983044
  45.9 0.8 %copy-start.4 = (bf16[160,1024]{1,0:T(8,128)(2,1)}, bf16[160,1024]{1,0:T(8,128)(2,1)S(1)}, u32[]{:S(2)}) copy-start(bf16[160,1024]{1,0:T(8,128)(2,1)S(1)} %collective-permute-done.4.refs_2_.refs_8_) | copy-start | bytes 983044
  46.8 0.7 %copy-start.5 = (bf16[160,1024]{1,0:T(8,128)(2,1)}, bf16[160,1024]{1,0:T(8,128)(2,1)S(1)}, u32[]{:S(2)}) copy-start(bf16[160,1024]{1,0:T(8,128)(2,1)S(1)} %collective-permute-done.3.refs_1_.refs_7_) | copy-start | bytes 983044

commit v10 on v6

--- a/solution.py
+++ b/solution.py
@@ -43,25 +43,28 @@
     from_even_own = send(own, to_odd)
     direct4 = send(own, [(i - 4, i) for i in far])
     forward2 = [(i, j) for i, j in ahead2 if j not in far_set]
-    back4 = send(back2, forward2) + direct4 if far else send(back2, forward2)
+    forward4 = send(back2, forward2)
     swapped2 = send(back2, swap)
-    from_odd4 = send(back4, to_even)
-    return [back4, from_odd4, swapped2, back2, from_even_own, own]
+    odd_to_next = [(i, i + 1) for i in range(1, count - 1, 2) if i + 1 not in far_set]
+    from_prev_odd = send(back2, odd_to_next)
+    from_odd_direct = send(direct4, [(i, i - 1) for i in far if i % 2 == 1])
+    return [forward4, direct4, from_prev_odd, from_odd_direct, swapped2, back2, from_even_own, own]
 
 
 def attend_kernel(qs_ref, scale_ref, ds_ref, q_ref, *refs):
     kv_refs, o_ref = refs[:-1], refs[-1]
     half = len(kv_refs) // 2
     rows = q_ref.shape[0]
-    width = rows * (half - 1)
+    width = rows * (half - 3)
     doc_most = width - rows
     head = pl.program_id(0)
     q_start = qs_ref[0]
     even = qs_ref[1] == 0
 
     def ordered(r):
-        back4, odd4, swap2, back2, even_own, own = [x[...] for x in r]
-        back3 = jnp.where(even, odd4, swap2)
+        fwd4, direct4, prev_odd, odd_direct, swap2, back2, even_own, own = [x[...] for x in r]
+        back4 = fwd4 + direct4
+        back3 = jnp.where(even, prev_odd + odd_direct, swap2)
         back1 = jnp.where(even, swap2, even_own)
         return jnp.concatenate([back4, back3, back2, back1, own], axis=0)
 
@@ -91,7 +94,7 @@
 
 def attend(queries, blocks, where, scale, doc_start, interpret=False):
     rows = queries.shape[0]
-    width = rows * (len(blocks) - 1)
+    width = rows * (len(blocks) - 3)
     per_group = HQ // HK
     flops = 4 * HQ * rows * width * HD
     k_specs = [pl.BlockSpec((rows, HD), lambda h: (0, h)) for _ in blocks]

time: 58.6 us -> 67.1 us (1.15)
  waiting for transfers between devices: 20.1 us -> 29.3 us
  local copies, waits for them, and re-layouts: 4.41 us -> 3.57 us
  starting transfers between devices: 17.2 us -> 16.5 us
    ppermute x6 -> x7, waiting for transfers between devices: 20.1 us -> 29.3 us  [send(): return lax.ppermute(x, AXES, pairs)]
    unnamed x15 -> x17, local copies, waits for them, and re-layouts: 2.52 us -> 1.68 us
    ppermute x6 -> x7, starting transfers between devices: 17.2 us -> 16.5 us  [send(): return lax.ppermute(x, AXES, pairs)]
    reduce_sum x1, other arithmetic: 0.19 us -> 0.87 us  [body(): jnp.sum(jnp.where(before, lengths[None, :], 0), axis=1, dtype=jnp.int32)]
  transfers between devices with their start and end apart: 6 -> 7, of which waited for: 2 -> 2; matrix products, arithmetic and copies ran while one was open for 5% -> 5% of each run, Pallas kernels for 0% -> 0%
where the time goes in v10:
time: 67.1 us; the launch traced here: 66.8 us
  waiting for transfers between devices  29.3 us (44%)
  starting transfers between devices  16.5 us (25%)
  Pallas kernels  14.6 us (22%)
  local copies, waits for them, and re-layouts  3.57 us (5%)
  other arithmetic  2.56 us (4%)
    ppermute x7, waiting for transfers between devices, send(): return lax.ppermute(x, AXES, pairs)  29.3 us
    ppermute x7, starting transfers between devices, send(): return lax.ppermute(x, AXES, pairs)  16.5 us
    pallas_call x1, Pallas kernels, attend(): pl.pallas_call(attend_kernel, grid=(HK,), in_specs=[pl.BlockSpec(memory_s...  14.6 us
    unnamed x17, local copies, waits for them, and re-layouts  1.68 us
  transfers between devices with their start and end apart: 7, of which 2 were waited for; matrix products, arithmetic and copies ran while one was open for 5% of the time, Pallas kernels for 0%

profile of v10, /device:TPU:15, one launch (start us, length us, event | category | flops | bytes accessed | tf_op | source)
XLA Modules:
  0.0 66.8 jit_solution(3779481102258036647)
XLA Ops:
  0.0 0.9 %constant_dynamic-update-slice_fusion.1 = bf16[160,1024]{1,0:T(8,128)(2,1)S(1)} fusion(bf16[160,512]{1,0:T(8,128)(2,1)} %param.6), kind=kLoop, calls=%fused_computation.2 | loop fusion | bytes 327680
  0.9 0.9 %constant_dynamic-update-slice_fusion.refs_7_.refs_15_ = bf16[160,1024]{1,0:T(8,128)(2,1)S(1)} fusion(bf16[160,1024]{1,0:T(8,128)(2,1)S(1)} %constant_dynamic-update-slice_fusion.1, bf16[160,512]{1,0:T(8,128)(2,1)} %param.7), kind=kLoop, calls=%fused_computation.1 | loop fusion | bytes 327680 | tf_op jit(solution)/shard_map/concatenate | solution.py:132
  1.9 0.0 copy-start
  1.9 1.3 %collective-permute-start.6 = (bf16[160,1024]{1,0:T(8,128)(2,1)S(1)}, bf16[160,1024]{1,0:T(8,128)(2,1)S(1)}, u32[]{:S(2)}, u32[]{:S(2)}) collective-permute-start(bf16[160,1024]{1,0:T(8,128)(2,1)S(1)} %constant_dynamic-update-slice_fusion.refs_7_.refs_15_), channel_id=1, source_target_pairs={{0,1},{2,3},{4,5},{6,7},{8,9},{10,11},{12,13},{14,15},{16,17},{18,... | collective-permute-start | bytes 983048 | tf_op jit(solution)/shard_map/ppermute | solution.py:18
  3.2 0.7 %collective-permute-start.2 = (bf16[160,1024]{1,0:T(8,128)(2,1)S(1)}, bf16[160,1024]{1,0:T(8,128)(2,1)S(1)}, u32[]{:S(2)}, u32[]{:S(2)}) collective-permute-start(bf16[160,1024]{1,0:T(8,128)(2,1)S(1)} %constant_dynamic-update-slice_fusion.refs_7_.refs_15_), channel_id=1, source_target_pairs={{188,192},{189,193},{380,384},{381,385},{572,576},{573,577}} | collective-permute-start | bytes 983048 | tf_op jit(solution)/shard_map/ppermute | solution.py:18
  3.9 3.2 %collective-permute-start = (bf16[160,1024]{1,0:T(8,128)(2,1)S(1)}, bf16[160,1024]{1,0:T(8,128)(2,1)S(1)}, u32[]{:S(2)}, u32[]{:S(2)}) collective-permute-start(bf16[160,1024]{1,0:T(8,128)(2,1)S(1)} %constant_dynamic-update-slice_fusion.refs_7_.refs_15_), channel_id=1, source_target_pairs={{0,2},{1,3},{2,4},{3,5},{4,6},{5,7},{6,8},{7,9},{8,10},{9,11},{10,... | collective-permute-start | bytes 983048 | tf_op jit(solution)/shard_map/ppermute | solution.py:18
  7.1 1.0 %reduce-window.9 = s32[3,128]{1,0:T(4,128)S(1)} reduce-window(s32[3,128]{1,0:T(4,128)} %bitcast.6, s32[]{:T(128)} %constant.26.clone.1), window={size=1x128 pad=0_0x127_0}, to_apply=%region_0.0 | reduce-window | flops 48768 | bytes 3076 | tf_op jit(solution)/shard_map/reduce-window
  8.1 0.1 slice.7
  8.2 0.1 slice_reduce_fusion
  8.3 0.1 add_bitcast_fusion
  8.4 5.4 %collective-permute-done.refs_5_.refs_13_ = bf16[160,1024]{1,0:T(8,128)(2,1)S(1)} collective-permute-done((bf16[160,1024]{1,0:T(8,128)(2,1)S(1)}, bf16[160,1024]{1,0:T(8,128)(2,1)S(1)}, u32[]{:S(2)}, u32[]{:S(2)}) %collective-permute-start) | collective-permute-done | bytes 327712 | tf_op jit(solution)/shard_map/ppermute | solution.py:18
  13.8 4.0 %collective-permute-start.5 = (bf16[160,1024]{1,0:T(8,128)(2,1)S(1)}, bf16[160,1024]{1,0:T(8,128)(2,1)S(1)}, u32[]{:S(2)}, u32[]{:S(2)}) collective-permute-start(bf16[160,1024]{1,0:T(8,128)(2,1)S(1)} %collective-permute-done.refs_5_.refs_13_), channel_id=1, source_target_pairs={{0,1},{2,3},{4,5},{6,7},{8,9},{10,11},{12,13},{14,15},{16,17},{18,... | collective-permute-start | bytes 983048 | tf_op jit(solution)/shard_map/ppermute | solution.py:18
  17.8 3.1 %collective-permute-start.3 = (bf16[160,1024]{1,0:T(8,128)(2,1)S(1)}, bf16[160,1024]{1,0:T(8,128)(2,1)S(1)}, u32[]{:S(2)}, u32[]{:S(2)}) collective-permute-start(bf16[160,1024]{1,0:T(8,128)(2,1)S(1)} %collective-permute-done.refs_5_.refs_13_), channel_id=1, source_target_pairs={{1,2},{3,4},{5,6},{7,8},{9,10},{11,12},{13,14},{15,16},{17,18},{19... | collective-permute-start | bytes 983048 | tf_op jit(solution)/shard_map/ppermute | solution.py:18
  20.9 3.5 %collective-permute-start.1 = (bf16[160,1024]{1,0:T(8,128)(2,1)S(1)}, bf16[160,1024]{1,0:T(8,128)(2,1)S(1)}, u32[]{:S(2)}, u32[]{:S(2)}) collective-permute-start(bf16[160,1024]{1,0:T(8,128)(2,1)S(1)} %collective-permute-done.refs_5_.refs_13_), channel_id=1, source_target_pairs={{0,2},{1,3},{2,4},{3,5},{4,6},{5,7},{6,8},{7,9},{8,10},{9,11},{10,... | collective-permute-start | bytes 983048 | tf_op jit(solution)/shard_map/ppermute | solution.py:18
  24.4 0.0 collective-permute-done.2.refs_1_.refs_9_
  24.4 0.0 copy-start.2
  24.5 0.7 %collective-permute-start.4 = (bf16[160,1024]{1,0:T(8,128)(2,1)S(1)}, bf16[160,1024]{1,0:T(8,128)(2,1)S(1)}, u32[]{:S(2)}, u32[]{:S(2)}) collective-permute-start(bf16[160,1024]{1,0:T(8,128)(2,1)S(1)} %collective-permute-done.2.refs_1_.refs_9_), channel_id=1, source_target_pairs={{193,192},{385,384},{577,576}} | collective-permute-start | bytes 983048 | tf_op jit(solution)/shard_map/ppermute | solution.py:18
  25.2 0.9 %select_reduce_fusion = s32[160]{0:T(256)S(1)} fusion(s32[384]{0:T(512)} %param.8, s32[384]{0:T(512)S(1)} %add_bitcast_fusion, s32[160]{0:T(256)S(1)} %iota_add_fusion), kind=kLoop, calls=%fused_computation | loop fusion | flops 184160 | bytes 4352 | tf_op jit(solution)/shard_map/reduce_sum | solution.py:136
  26.0 0.8 %copy.7.ds_ref = s32[160,1]{1,0:T(8,128)} copy(s32[160,1]{0,1:T(1,128)S(1)} %bitcast.7) | data formatting | bytes 1280 | tf_op jit(solution)/shard_map/broadcast_in_dim | solution.py:138
  26.8 0.6 pad_add_fusion.qs_ref
  27.4 0.0 collective-permute-done.6.refs_6_.refs_14_
  27.4 0.0 collective-permute-done.4.refs_3_.refs_11_
  27.4 0.0 copy-start.7
  27.4 0.0 collective-permute-done.5.refs_4_.refs_12_
  27.4 0.0 copy-start.4
  27.4 0.0 collective-permute-done.3.refs_2_.refs_10_
  27.4 0.0 copy-start.5
  27.4 23.9 %collective-permute-done.1.refs_0_.refs_8_ = bf16[160,1024]{1,0:T(8,128)(2,1)S(1)} collective-permute-done((bf16[160,1024]{1,0:T(8,128)(2,1)S(1)}, bf16[160,1024]{1,0:T(8,128)(2,1)S(1)}, u32[]{:S(2)}, u32[]{:S(2)}) %collective-permute-start.1) | collective-permute-done | bytes 327712 | tf_op jit(solution)/shard_map/ppermute | solution.py:18
  51.3 0.0 copy-done
  51.3 0.0 copy-done.3
  51.4 0.7 %copy-done.6 = bf16[160,1024]{1,0:T(8,128)(2,1)} copy-done((bf16[160,1024]{1,0:T(8,128)(2,1)}, bf16[160,1024]{1,0:T(8,128)(2,1)S(1)}, u32[]{:S(2)}) %copy-start.6) | copy-done | bytes 327704
  52.1 14.6 %shard_map.55 = bf16[160,4096]{1,0:T(8,128)(2,1)} custom-call(s32[2]{0:T(128)} %pad_add_fusion.qs_ref, f32[32]{0:T(128)} %scale_ref.1, s32[160,1]{1,0:T(8,128)} %copy.7.ds_ref, bf16[160,4096]{1,0:T(8,128)(2,1)} %q_ref.1, bf16[160,1024]{1,0:T(8,128)(2,1)} %copy-done.6, bf16[160,1024]{1,0:T(8,128)(2,1)} %copy-done.2, bf16[160,1024]{1,0:T(8,128)(2,1)} %copy-done.5, ...), custom_call_target="tpu_custom_call" | custom-call | flops 2097152000 | bytes 4259840 | tf_op jit(solution)/shard_map/pallas_call | solution.py:102
  (10 shorter events, 0.1 us)
Async XLA Ops:
  1.9 49.5 %copy-start = (bf16[160,1024]{1,0:T(8,128)(2,1)}, bf16[160,1024]{1,0:T(8,128)(2,1)S(1)}, u32[]{:S(2)}) copy-start(bf16[160,1024]{1,0:T(8,128)(2,1)S(1)} %constant_dynamic-update-slice_fusion.refs_7_.refs_15_) | copy-start | bytes 983044
  1.9 25.5 %collective-permute-start.6 = (bf16[160,1024]{1,0:T(8,128)(2,1)S(1)}, bf16[160,1024]{1,0:T(8,128)(2,1)S(1)}, u32[]{:S(2)}, u32[]{:S(2)}) collective-permute-start(bf16[160,1024]{1,0:T(8,128)(2,1)S(1)} %constant_dynamic-update-slice_fusion.refs_7_.refs_15_), channel_id=1, source_target_pairs={{0,1},{2,3},{4,5},{6,7},{8,9},{10,11},{12,13},{14,15},{16,17},{18,... | collective-permute-start | bytes 983048 | tf_op jit(solution)/shard_map/ppermute | solution.py:18
  3.2 21.3 %collective-permute-start.2 = (bf16[160,1024]{1,0:T(8,128)(2,1)S(1)}, bf16[160,1024]{1,0:T(8,128)(2,1)S(1)}, u32[]{:S(2)}, u32[]{:S(2)}) collective-permute-start(bf16[160,1024]{1,0:T(8,128)(2,1)S(1)} %constant_dynamic-update-slice_fusion.refs_7_.refs_15_), channel_id=1, source_target_pairs={{188,192},{189,193},{380,384},{381,385},{572,576},{573,577}} | collective-permute-start | bytes 983048 | tf_op jit(solution)/shard_map/ppermute | solution.py:18
  3.9 10.0 %collective-permute-start = (bf16[160,1024]{1,0:T(8,128)(2,1)S(1)}, bf16[160,1024]{1,0:T(8,128)(2,1)S(1)}, u32[]{:S(2)}, u32[]{:S(2)}) collective-permute-start(bf16[160,1024]{1,0:T(8,128)(2,1)S(1)} %constant_dynamic-update-slice_fusion.refs_7_.refs_15_), channel_id=1, source_target_pairs={{0,2},{1,3},{2,4},{3,5},{4,6},{5,7},{6,8},{7,9},{8,10},{9,11},{10,... | collective-permute-start | bytes 983048 | tf_op jit(solution)/shard_map/ppermute | solution.py:18
  13.8 37.5 %copy-start.3 = (bf16[160,1024]{1,0:T(8,128)(2,1)}, bf16[160,1024]{1,0:T(8,128)(2,1)S(1)}, u32[]{:S(2)}) copy-start(bf16[160,1024]{1,0:T(8,128)(2,1)S(1)} %collective-permute-done.refs_5_.refs_13_) | copy-start | bytes 983044
  13.8 13.6 %collective-permute-start.5 = (bf16[160,1024]{1,0:T(8,128)(2,1)S(1)}, bf16[160,1024]{1,0:T(8,128)(2,1)S(1)}, u32[]{:S(2)}, u32[]{:S(2)}) collective-permute-start(bf16[160,1024]{1,0:T(8,128)(2,1)S(1)} %collective-permute-done.refs_5_.refs_13_), channel_id=1, source_target_pairs={{0,1},{2,3},{4,5},{6,7},{8,9},{10,11},{12,13},{14,15},{16,17},{18,... | collective-permute-start | bytes 983048 | tf_op jit(solution)/shard_map/ppermute | solution.py:18
  17.8 9.6 %collective-permute-start.3 = (bf16[160,1024]{1,0:T(8,128)(2,1)S(1)}, bf16[160,1024]{1,0:T(8,128)(2,1)S(1)}, u32[]{:S(2)}, u32[]{:S(2)}) collective-permute-start(bf16[160,1024]{1,0:T(8,128)(2,1)S(1)} %collective-permute-done.refs_5_.refs_13_), channel_id=1, source_target_pairs={{1,2},{3,4},{5,6},{7,8},{9,10},{11,12},{13,14},{15,16},{17,18},{19... | collective-permute-start | bytes 983048 | tf_op jit(solution)/shard_map/ppermute | solution.py:18
  20.9 30.4 %collective-permute-start.1 = (bf16[160,1024]{1,0:T(8,128)(2,1)S(1)}, bf16[160,1024]{1,0:T(8,128)(2,1)S(1)}, u32[]{:S(2)}, u32[]{:S(2)}) collective-permute-start(bf16[160,1024]{1,0:T(8,128)(2,1)S(1)} %collective-permute-done.refs_5_.refs_13_), channel_id=1, source_target_pairs={{0,2},{1,3},{2,4},{3,5},{4,6},{5,7},{6,8},{7,9},{8,10},{9,11},{10,... | collective-permute-start | bytes 983048 | tf_op jit(solution)/shard_map/ppermute | solution.py:18
  24.4 26.9 %copy-start.2 = (bf16[160,1024]{1,0:T(8,128)(2,1)}, bf16[160,1024]{1,0:T(8,128)(2,1)S(1)}, u32[]{:S(2)}) copy-start(bf16[160,1024]{1,0:T(8,128)(2,1)S(1)} %collective-permute-done.2.refs_1_.refs_9_) | copy-start | bytes 983044
  24.5 2.9 %collective-permute-start.4 = (bf16[160,1024]{1,0:T(8,128)(2,1)S(1)}, bf16[160,1024]{1,0:T(8,128)(2,1)S(1)}, u32[]{:S(2)}, u32[]{:S(2)}) collective-permute-start(bf16[160,1024]{1,0:T(8,128)(2,1)S(1)} %collective-permute-done.2.refs_1_.refs_9_), channel_id=1, source_target_pairs={{193,192},{385,384},{577,576}} | collective-permute-start | bytes 983048 | tf_op jit(solution)/shard_map/ppermute | solution.py:18
  27.4 24.0 %copy-start.1 = (bf16[160,1024]{1,0:T(8,128)(2,1)}, bf16[160,1024]{1,0:T(8,128)(2,1)S(1)}, u32[]{:S(2)}) copy-start(bf16[160,1024]{1,0:T(8,128)(2,1)S(1)} %collective-permute-done.6.refs_6_.refs_14_) | copy-start | bytes 983044
  27.4 24.0 %copy-start.7 = (bf16[160,1024]{1,0:T(8,128)(2,1)}, bf16[160,1024]{1,0:T(8,128)(2,1)S(1)}, u32[]{:S(2)}) copy-start(bf16[160,1024]{1,0:T(8,128)(2,1)S(1)} %collective-permute-done.4.refs_3_.refs_11_) | copy-start | bytes 983044
  27.4 23.9 %copy-start.4 = (bf16[160,1024]{1,0:T(8,128)(2,1)}, bf16[160,1024]{1,0:T(8,128)(2,1)S(1)}, u32[]{:S(2)}) copy-start(bf16[160,1024]{1,0:T(8,128)(2,1)S(1)} %collective-permute-done.5.refs_4_.refs_12_) | copy-start | bytes 983044
  27.4 23.9 %copy-start.5 = (bf16[160,1024]{1,0:T(8,128)(2,1)}, bf16[160,1024]{1,0:T(8,128)(2,1)S(1)}, u32[]{:S(2)}) copy-start(bf16[160,1024]{1,0:T(8,128)(2,1)S(1)} %collective-permute-done.3.refs_2_.refs_10_) | copy-start | bytes 983044
  51.4 0.7 %copy-start.6 = (bf16[160,1024]{1,0:T(8,128)(2,1)}, bf16[160,1024]{1,0:T(8,128)(2,1)S(1)}, u32[]{:S(2)}) copy-start(bf16[160,1024]{1,0:T(8,128)(2,1)S(1)} %collective-permute-done.1.refs_0_.refs_8_) | copy-start | bytes 983044

commit v11 on v6

--- a/solution.py
+++ b/solution.py
@@ -65,12 +65,9 @@
         back1 = jnp.where(even, swap2, even_own)
         return jnp.concatenate([back4, back3, back2, back1, own], axis=0)
 
-    col = lax.broadcasted_iota(jnp.int32, (rows, width), 1)
-    row = lax.broadcasted_iota(jnp.int32, (rows, width), 0)
     doc_start = ds_ref[...]
-    live = (col >= doc_start - (q_start - doc_most)) & (col <= row + doc_most)
-    k = ordered(kv_refs[:half])
-    v = ordered(kv_refs[half:])
+    k_all = ordered(kv_refs[:half])
+    v_all = ordered(kv_refs[half:])
     q_pos = q_start + lax.broadcasted_iota(jnp.int32, (rows, 1), 0)
     logv = jnp.log((q_pos - doc_start + 1).astype(jnp.float32))
     per_group = HQ // HK
@@ -78,16 +75,28 @@
         [scale_ref[head * per_group + g] * logv / jnp.sqrt(jnp.float32(HD)) for g in range(per_group)]
     )
     q = jnp.concatenate([q_ref[:, g * HD : (g + 1) * HD] for g in range(per_group)], axis=0)
-    s = lax.dot_general(q, k, (((1,), (1,)), ((), ())), preferred_element_type=jnp.float32)
-    s = jnp.where(live[None], s.reshape(per_group, rows, width) * coef, -jnp.inf)
-    m = jnp.max(s, axis=2, keepdims=True)
-    p = jnp.exp(s - m)
-    l = jnp.sum(p, axis=2, keepdims=True)
-    w = (p * (1.0 / l)).astype(jnp.bfloat16).reshape(per_group * rows, width)
-    o = jnp.dot(w, v, preferred_element_type=jnp.float32)
-    for g in range(per_group):
-        o_ref[:, g * HD : (g + 1) * HD] = o[g * rows : (g + 1) * rows].astype(o_ref.dtype)
+    lo = doc_start - (q_start - doc_most)
 
+    def compute(skip):
+        first = skip * rows
+        span = width - first
+        k = k_all[first:]
+        v = v_all[first:]
+        col = lax.broadcasted_iota(jnp.int32, (rows, span), 1) + first
+        row = lax.broadcasted_iota(jnp.int32, (rows, span), 0)
+        live = (col >= lo) & (col <= row + doc_most)
+        s = lax.dot_general(q, k, (((1,), (1,)), ((), ())), preferred_element_type=jnp.float32)
+        s = jnp.where(live[None], s.reshape(per_group, rows, span) * coef, -jnp.inf)
+        m = jnp.max(s, axis=2, keepdims=True)
+        p = jnp.exp(s - m)
+        l = jnp.sum(p, axis=2, keepdims=True)
+        w = (p * (1.0 / l)).astype(jnp.bfloat16).reshape(per_group * rows, span)
+        o = jnp.dot(w, v, preferred_element_type=jnp.float32)
+        for g in range(per_group):
+            o_ref[:, g * HD : (g + 1) * HD] = o[g * rows : (g + 1) * rows].astype(o_ref.dtype)
+
+    for skip in range(half - 1):
+        pl.when(qs_ref[2] == skip)(functools.partial(compute, skip))
 
 def attend(queries, blocks, where, scale, doc_start, interpret=False):
     rows = queries.shape[0]
@@ -131,7 +140,8 @@
     totals = jnp.cumsum(lengths, dtype=jnp.int32)
     before = totals[None, :] <= q_pos[:, None]
     doc_start = jnp.sum(jnp.where(before, lengths[None, :], 0), axis=1, dtype=jnp.int32)
-    where = jnp.stack([q_start, grp_index % 2]).astype(jnp.int32)
+    skip = jnp.clip((doc_start[0] - (q_start - doc_most)) // tok_rows, 0, WIN_DEV)
+    where = jnp.stack([q_start, grp_index % 2, skip]).astype(jnp.int32)
     return attend(queries, blocks, where, ssmax_scale, doc_start[:, None])
 
 

time: 58.6 us -> 58 us (0.990); the launches traced: 58.3 us -> 57 us
  Pallas kernels: 14.5 us -> 12 us
  between operations: 0.17 us -> 0.76 us
    pallas_call x1, Pallas kernels: 14.5 us -> 12 us  [attend(): pl.pallas_call(attend_kernel, grid=(HK,), in_specs=[pl.BlockSpec(memory_s...]
  transfers between devices with their start and end apart: 6 -> 6, of which waited for: 2 -> 2; matrix products, arithmetic and copies ran while one was open for 5% -> 6% of each run, Pallas kernels for 0% -> 0%
where the time goes in v11:
time: 58 us; the launch traced here: 57 us
  waiting for transfers between devices  20.1 us (35%)
  starting transfers between devices  17.2 us (30%)
  Pallas kernels  12 us (21%)
  local copies, waits for them, and re-layouts  4.92 us (8%)
  other arithmetic  1.97 us (3%)
  between operations  0.76 us (1%)
    ppermute x6, waiting for transfers between devices, send(): return lax.ppermute(x, AXES, pairs)  20.1 us
    ppermute x6, starting transfers between devices, send(): return lax.ppermute(x, AXES, pairs)  17.2 us
    pallas_call x1, Pallas kernels, attend(): pl.pallas_call(attend_kernel, grid=(HK,), in_specs=[pl.BlockSpec(memory_s...  12 us
    unnamed x15, local copies, waits for them, and re-layouts  2.52 us
  transfers between devices with their start and end apart: 6, of which 2 were waited for; matrix products, arithmetic and copies ran while one was open for 6% of the time, Pallas kernels for 0%

profile of v11, /device:TPU:15, one launch (start us, length us, event | category | flops | bytes accessed | tf_op | source)
XLA Modules:
  0.0 57.0 jit_solution(16693824711256591249)
XLA Ops:
  0.0 0.9 %constant_dynamic-update-slice_fusion.1 = bf16[160,1024]{1,0:T(8,128)(2,1)S(1)} fusion(bf16[160,512]{1,0:T(8,128)(2,1)} %param.6), kind=kLoop, calls=%fused_computation.2 | loop fusion | bytes 327680
  0.9 0.9 %constant_dynamic-update-slice_fusion.refs_5_.refs_11_ = bf16[160,1024]{1,0:T(8,128)(2,1)S(1)} fusion(bf16[160,1024]{1,0:T(8,128)(2,1)S(1)} %constant_dynamic-update-slice_fusion.1, bf16[160,512]{1,0:T(8,128)(2,1)} %param.7), kind=kLoop, calls=%fused_computation.1 | loop fusion | bytes 327680 | tf_op jit(solution)/shard_map/concatenate | solution.py:138
  1.9 0.0 copy-start.1
  1.9 3.2 %collective-permute-start = (bf16[160,1024]{1,0:T(8,128)(2,1)S(1)}, bf16[160,1024]{1,0:T(8,128)(2,1)S(1)}, u32[]{:S(2)}, u32[]{:S(2)}) collective-permute-start(bf16[160,1024]{1,0:T(8,128)(2,1)S(1)} %constant_dynamic-update-slice_fusion.refs_5_.refs_11_), channel_id=1, source_target_pairs={{0,2},{1,3},{2,4},{3,5},{4,6},{5,7},{6,8},{7,9},{8,10},{9,11},{10,... | collective-permute-start | bytes 983048 | tf_op jit(solution)/shard_map/ppermute | solution.py:18
  5.1 1.3 %collective-permute-start.5 = (bf16[160,1024]{1,0:T(8,128)(2,1)S(1)}, bf16[160,1024]{1,0:T(8,128)(2,1)S(1)}, u32[]{:S(2)}, u32[]{:S(2)}) collective-permute-start(bf16[160,1024]{1,0:T(8,128)(2,1)S(1)} %constant_dynamic-update-slice_fusion.refs_5_.refs_11_), channel_id=1, source_target_pairs={{0,1},{2,3},{4,5},{6,7},{8,9},{10,11},{12,13},{14,15},{16,17},{18,... | collective-permute-start | bytes 983048 | tf_op jit(solution)/shard_map/ppermute | solution.py:18
  6.4 0.7 %collective-permute-start.2 = (bf16[160,1024]{1,0:T(8,128)(2,1)S(1)}, bf16[160,1024]{1,0:T(8,128)(2,1)S(1)}, u32[]{:S(2)}, u32[]{:S(2)}) collective-permute-start(bf16[160,1024]{1,0:T(8,128)(2,1)S(1)} %constant_dynamic-update-slice_fusion.refs_5_.refs_11_), channel_id=1, source_target_pairs={{188,192},{189,193},{380,384},{381,385},{572,576},{573,577}} | collective-permute-start | bytes 983048 | tf_op jit(solution)/shard_map/ppermute | solution.py:18
  7.1 1.0 %reduce-window.9 = s32[3,128]{1,0:T(4,128)S(1)} reduce-window(s32[3,128]{1,0:T(4,128)} %bitcast.8, s32[]{:T(128)} %constant.35.clone.1), window={size=1x128 pad=0_0x127_0}, to_apply=%region_0.0 | reduce-window | flops 48768 | bytes 3076 | tf_op jit(solution)/shard_map/reduce-window
  8.1 0.1 slice.10
  8.2 4.2 %collective-permute-done.refs_3_.refs_9_ = bf16[160,1024]{1,0:T(8,128)(2,1)S(1)} collective-permute-done((bf16[160,1024]{1,0:T(8,128)(2,1)S(1)}, bf16[160,1024]{1,0:T(8,128)(2,1)S(1)}, u32[]{:S(2)}, u32[]{:S(2)}) %collective-permute-start) | collective-permute-done | bytes 327712 | tf_op jit(solution)/shard_map/ppermute | solution.py:18
  12.4 3.2 %collective-permute-start.1 = (bf16[160,1024]{1,0:T(8,128)(2,1)S(1)}, bf16[160,1024]{1,0:T(8,128)(2,1)S(1)}, u32[]{:S(2)}, u32[]{:S(2)}) collective-permute-start(bf16[160,1024]{1,0:T(8,128)(2,1)S(1)} %collective-permute-done.refs_3_.refs_9_), channel_id=1, source_target_pairs={{0,2},{1,3},{2,4},{3,5},{4,6},{5,7},{6,8},{7,9},{8,10},{9,11},{10,... | collective-permute-start | bytes 983048 | tf_op jit(solution)/shard_map/ppermute | solution.py:18
  15.6 0.1 slice_reduce_fusion
  15.7 0.1 add_bitcast_fusion
  15.8 3.7 %collective-permute-start.4 = (bf16[160,1024]{1,0:T(8,128)(2,1)S(1)}, bf16[160,1024]{1,0:T(8,128)(2,1)S(1)}, u32[]{:S(2)}, u32[]{:S(2)}) collective-permute-start(bf16[160,1024]{1,0:T(8,128)(2,1)S(1)} %collective-permute-done.refs_3_.refs_9_), channel_id=1, source_target_pairs={{0,1},{2,3},{4,5},{6,7},{8,9},{10,11},{12,13},{14,15},{16,17},{18,... | collective-permute-start | bytes 983048 | tf_op jit(solution)/shard_map/ppermute | solution.py:18
  19.5 0.0 collective-permute-done.2
  19.5 16.0 %collective-permute-done.1 = bf16[160,1024]{1,0:T(8,128)(2,1)S(1)} collective-permute-done((bf16[160,1024]{1,0:T(8,128)(2,1)S(1)}, bf16[160,1024]{1,0:T(8,128)(2,1)S(1)}, u32[]{:S(2)}, u32[]{:S(2)}) %collective-permute-start.1) | collective-permute-done | bytes 327712 | tf_op jit(solution)/shard_map/ppermute | solution.py:18
  35.5 0.1 add.26.refs_0_.refs_6_
  35.6 0.0 copy-start
  35.6 5.1 %collective-permute-start.3 = (bf16[160,1024]{1,0:T(8,128)(2,1)S(1)}, bf16[160,1024]{1,0:T(8,128)(2,1)S(1)}, u32[]{:S(2)}, u32[]{:S(2)}) collective-permute-start(bf16[160,1024]{1,0:T(8,128)(2,1)S(1)} %add.26.refs_0_.refs_6_), channel_id=1, source_target_pairs={{1,0},{3,2},{5,4},{7,6},{9,8},{11,10},{13,12},{15,14},{17,16},{19,... | collective-permute-start | bytes 983048 | tf_op jit(solution)/shard_map/ppermute | solution.py:18
  40.7 0.0 copy-done.2
  40.7 0.2 select_reduce_fusion
  40.9 0.5 slice.12
  42.0 0.8 %copy.7.ds_ref = s32[160,1]{1,0:T(8,128)} copy(s32[160,1]{0,1:T(1,128)S(1)} %bitcast.9) | data formatting | bytes 1280 | tf_op jit(solution)/shard_map/broadcast_in_dim | solution.py:145
  42.7 0.6 %pad_add_fusion.qs_ref = s32[3]{0:T(128)} fusion(s32[1]{0:T(128)} %bitcast.5, s32[1]{0:T(128)} %bitcast.1, s32[1]{0:T(128)} %bitcast), kind=kLoop, calls=%fused_computation.6 | loop fusion | flops 6 | bytes 24 | tf_op jit(solution)/shard_map/stack | solution.py:144
  43.3 0.0 collective-permute-done.5.refs_4_.refs_10_
  43.3 0.0 collective-permute-done.4.refs_2_.refs_8_
  43.3 0.0 copy-start.5
  43.3 0.0 collective-permute-done.3.refs_1_.refs_7_
  43.4 0.0 copy-done.1
  43.4 0.7 %copy-done.4 = bf16[160,1024]{1,0:T(8,128)(2,1)} copy-done((bf16[160,1024]{1,0:T(8,128)(2,1)}, bf16[160,1024]{1,0:T(8,128)(2,1)S(1)}, u32[]{:S(2)}) %copy-start.4) | copy-done | bytes 327704
  44.0 0.2 copy-done.5
  44.2 0.7 %copy-done.6 = bf16[160,1024]{1,0:T(8,128)(2,1)} copy-done((bf16[160,1024]{1,0:T(8,128)(2,1)}, bf16[160,1024]{1,0:T(8,128)(2,1)S(1)}, u32[]{:S(2)}) %copy-start.6) | copy-done | bytes 327704
  45.0 12.0 %shard_map.55 = bf16[160,4096]{1,0:T(8,128)(2,1)} custom-call(s32[3]{0:T(128)} %pad_add_fusion.qs_ref, f32[32]{0:T(128)} %scale_ref.1, s32[160,1]{1,0:T(8,128)} %copy.7.ds_ref, bf16[160,4096]{1,0:T(8,128)(2,1)} %q_ref.1, bf16[160,1024]{1,0:T(8,128)(2,1)} %copy-done, bf16[160,1024]{1,0:T(8,128)(2,1)} %copy-done.6, bf16[160,1024]{1,0:T(8,128)(2,1)} %copy-done.5, ...), custom_call_target="tpu_custom_call" | custom-call | flops 2097152000 | bytes 4259840 | tf_op jit(solution)/shard_map/pallas_call | solution.py:108
  (8 shorter events, 0.1 us)
Async XLA Ops:
  0.0 40.7 %copy-start.2 = (s32[384]{0:T(512)S(1)}, s32[384]{0:T(512)}, u32[]{:S(2)}) copy-start(s32[384]{0:T(512)} %param.8) | copy-start | bytes 4612
  1.9 41.5 %copy-start.1 = (bf16[160,1024]{1,0:T(8,128)(2,1)}, bf16[160,1024]{1,0:T(8,128)(2,1)S(1)}, u32[]{:S(2)}) copy-start(bf16[160,1024]{1,0:T(8,128)(2,1)S(1)} %constant_dynamic-update-slice_fusion.refs_5_.refs_11_) | copy-start | bytes 983044
  1.9 10.5 %collective-permute-start = (bf16[160,1024]{1,0:T(8,128)(2,1)S(1)}, bf16[160,1024]{1,0:T(8,128)(2,1)S(1)}, u32[]{:S(2)}, u32[]{:S(2)}) collective-permute-start(bf16[160,1024]{1,0:T(8,128)(2,1)S(1)} %constant_dynamic-update-slice_fusion.refs_5_.refs_11_), channel_id=1, source_target_pairs={{0,2},{1,3},{2,4},{3,5},{4,6},{5,7},{6,8},{7,9},{8,10},{9,11},{10,... | collective-permute-start | bytes 983048 | tf_op jit(solution)/shard_map/ppermute | solution.py:18
  5.1 38.2 %collective-permute-start.5 = (bf16[160,1024]{1,0:T(8,128)(2,1)S(1)}, bf16[160,1024]{1,0:T(8,128)(2,1)S(1)}, u32[]{:S(2)}, u32[]{:S(2)}) collective-permute-start(bf16[160,1024]{1,0:T(8,128)(2,1)S(1)} %constant_dynamic-update-slice_fusion.refs_5_.refs_11_), channel_id=1, source_target_pairs={{0,1},{2,3},{4,5},{6,7},{8,9},{10,11},{12,13},{14,15},{16,17},{18,... | collective-permute-start | bytes 983048 | tf_op jit(solution)/shard_map/ppermute | solution.py:18
  6.4 13.1 %collective-permute-start.2 = (bf16[160,1024]{1,0:T(8,128)(2,1)S(1)}, bf16[160,1024]{1,0:T(8,128)(2,1)S(1)}, u32[]{:S(2)}, u32[]{:S(2)}) collective-permute-start(bf16[160,1024]{1,0:T(8,128)(2,1)S(1)} %constant_dynamic-update-slice_fusion.refs_5_.refs_11_), channel_id=1, source_target_pairs={{188,192},{189,193},{380,384},{381,385},{572,576},{573,577}} | collective-permute-start | bytes 983048 | tf_op jit(solution)/shard_map/ppermute | solution.py:18
  12.4 31.0 %copy-start.3 = (bf16[160,1024]{1,0:T(8,128)(2,1)}, bf16[160,1024]{1,0:T(8,128)(2,1)S(1)}, u32[]{:S(2)}) copy-start(bf16[160,1024]{1,0:T(8,128)(2,1)S(1)} %collective-permute-done.refs_3_.refs_9_) | copy-start | bytes 983044
  12.4 23.1 %collective-permute-start.1 = (bf16[160,1024]{1,0:T(8,128)(2,1)S(1)}, bf16[160,1024]{1,0:T(8,128)(2,1)S(1)}, u32[]{:S(2)}, u32[]{:S(2)}) collective-permute-start(bf16[160,1024]{1,0:T(8,128)(2,1)S(1)} %collective-permute-done.refs_3_.refs_9_), channel_id=1, source_target_pairs={{0,2},{1,3},{2,4},{3,5},{4,6},{5,7},{6,8},{7,9},{8,10},{9,11},{10,... | collective-permute-start | bytes 983048 | tf_op jit(solution)/shard_map/ppermute | solution.py:18
  15.8 27.6 %collective-permute-start.4 = (bf16[160,1024]{1,0:T(8,128)(2,1)S(1)}, bf16[160,1024]{1,0:T(8,128)(2,1)S(1)}, u32[]{:S(2)}, u32[]{:S(2)}) collective-permute-start(bf16[160,1024]{1,0:T(8,128)(2,1)S(1)} %collective-permute-done.refs_3_.refs_9_), channel_id=1, source_target_pairs={{0,1},{2,3},{4,5},{6,7},{8,9},{10,11},{12,13},{14,15},{16,17},{18,... | collective-permute-start | bytes 983048 | tf_op jit(solution)/shard_map/ppermute | solution.py:18
  35.6 7.8 %copy-start = (bf16[160,1024]{1,0:T(8,128)(2,1)}, bf16[160,1024]{1,0:T(8,128)(2,1)S(1)}, u32[]{:S(2)}) copy-start(bf16[160,1024]{1,0:T(8,128)(2,1)S(1)} %add.26.refs_0_.refs_6_) | copy-start | bytes 983044
  35.6 7.8 %collective-permute-start.3 = (bf16[160,1024]{1,0:T(8,128)(2,1)S(1)}, bf16[160,1024]{1,0:T(8,128)(2,1)S(1)}, u32[]{:S(2)}, u32[]{:S(2)}) collective-permute-start(bf16[160,1024]{1,0:T(8,128)(2,1)S(1)} %add.26.refs_0_.refs_6_), channel_id=1, source_target_pairs={{1,0},{3,2},{5,4},{7,6},{9,8},{11,10},{13,12},{15,14},{17,16},{19,... | collective-permute-start | bytes 983048 | tf_op jit(solution)/shard_map/ppermute | solution.py:18
  43.3 0.7 %copy-start.4 = (bf16[160,1024]{1,0:T(8,128)(2,1)}, bf16[160,1024]{1,0:T(8,128)(2,1)S(1)}, u32[]{:S(2)}) copy-start(bf16[160,1024]{1,0:T(8,128)(2,1)S(1)} %collective-permute-done.5.refs_4_.refs_10_) | copy-start | bytes 983044
  43.3 0.9 %copy-start.5 = (bf16[160,1024]{1,0:T(8,128)(2,1)}, bf16[160,1024]{1,0:T(8,128)(2,1)S(1)}, u32[]{:S(2)}) copy-start(bf16[160,1024]{1,0:T(8,128)(2,1)S(1)} %collective-permute-done.4.refs_2_.refs_8_) | copy-start | bytes 983044
  44.2 0.7 %copy-start.6 = (bf16[160,1024]{1,0:T(8,128)(2,1)}, bf16[160,1024]{1,0:T(8,128)(2,1)S(1)}, u32[]{:S(2)}) copy-start(bf16[160,1024]{1,0:T(8,128)(2,1)S(1)} %collective-permute-done.3.refs_1_.refs_7_) | copy-start | bytes 983044

commit v12 on v7

--- a/solution.py
+++ b/solution.py
@@ -29,7 +29,7 @@
     def hops(a, b):
         return sum(min(abs(p - q), n - abs(p - q)) for p, q, n in zip(a, b, sizes))
 
-    return tuple(i for i in range(4, len(flat)) if hops(chips[i - 4], chips[i]) >= 3)
+    return tuple(i for i in range(4, len(flat)) if hops(chips[i - 4], chips[i]) >= 3 and chips[i - 4][0] != chips[i][0])
 
 
 def window_blocks(own, far):

time: 62 us -> 62 us (level)
  no operation moved by 1% of the time
where the time goes in v12:
time: 62 us; the launch traced here: 61.7 us
  waiting for transfers between devices  24.6 us (40%)
  starting transfers between devices  16.1 us (26%)
  Pallas kernels  14.5 us (23%)
  local copies, waits for them, and re-layouts  4.41 us (7%)
  other arithmetic  1.97 us (3%)
    ppermute x6, waiting for transfers between devices, send(): return lax.ppermute(x, AXES, pairs)  24.6 us
    ppermute x6, starting transfers between devices, send(): return lax.ppermute(x, AXES, pairs)  16.1 us
    pallas_call x1, Pallas kernels, attend(): pl.pallas_call(attend_kernel, grid=(HK,), in_specs=[pl.BlockSpec(memory_s...  14.5 us
    unnamed x15, local copies, waits for them, and re-layouts  2.52 us
  transfers between devices with their start and end apart: 6, of which 2 were waited for; matrix products, arithmetic and copies ran while one was open for 5% of the time, Pallas kernels for 0%

profile of v12, /device:TPU:15, one launch (start us, length us, event | category | flops | bytes accessed | tf_op | source)
XLA Modules:
  0.0 61.7 jit_solution(3124850739029588924)
XLA Ops:
  0.0 0.9 %constant_dynamic-update-slice_fusion.1 = bf16[160,1024]{1,0:T(8,128)(2,1)S(1)} fusion(bf16[160,512]{1,0:T(8,128)(2,1)} %param.6), kind=kLoop, calls=%fused_computation.2 | loop fusion | bytes 327680
  0.9 0.9 %constant_dynamic-update-slice_fusion.refs_5_.refs_11_ = bf16[160,1024]{1,0:T(8,128)(2,1)S(1)} fusion(bf16[160,1024]{1,0:T(8,128)(2,1)S(1)} %constant_dynamic-update-slice_fusion.1, bf16[160,512]{1,0:T(8,128)(2,1)} %param.7), kind=kLoop, calls=%fused_computation.1 | loop fusion | bytes 327680 | tf_op jit(solution)/shard_map/concatenate | solution.py:129
  1.9 0.0 copy-start.1
  1.9 3.2 %collective-permute-start = (bf16[160,1024]{1,0:T(8,128)(2,1)S(1)}, bf16[160,1024]{1,0:T(8,128)(2,1)S(1)}, u32[]{:S(2)}, u32[]{:S(2)}) collective-permute-start(bf16[160,1024]{1,0:T(8,128)(2,1)S(1)} %constant_dynamic-update-slice_fusion.refs_5_.refs_11_), channel_id=1, source_target_pairs={{0,2},{1,3},{2,4},{3,5},{4,6},{5,7},{6,8},{7,9},{8,10},{9,11},{10,... | collective-permute-start | bytes 983048 | tf_op jit(solution)/shard_map/ppermute | solution.py:18
  5.1 1.3 %collective-permute-start.5 = (bf16[160,1024]{1,0:T(8,128)(2,1)S(1)}, bf16[160,1024]{1,0:T(8,128)(2,1)S(1)}, u32[]{:S(2)}, u32[]{:S(2)}) collective-permute-start(bf16[160,1024]{1,0:T(8,128)(2,1)S(1)} %constant_dynamic-update-slice_fusion.refs_5_.refs_11_), channel_id=1, source_target_pairs={{0,1},{2,3},{4,5},{6,7},{8,9},{10,11},{12,13},{14,15},{16,17},{18,... | collective-permute-start | bytes 983048 | tf_op jit(solution)/shard_map/ppermute | solution.py:18
  6.4 1.3 %collective-permute-start.2 = (bf16[160,1024]{1,0:T(8,128)(2,1)S(1)}, bf16[160,1024]{1,0:T(8,128)(2,1)S(1)}, u32[]{:S(2)}, u32[]{:S(2)}) collective-permute-start(bf16[160,1024]{1,0:T(8,128)(2,1)S(1)} %constant_dynamic-update-slice_fusion.refs_5_.refs_11_), channel_id=1, source_target_pairs={{188,192},{189,193},{190,194},{191,195},{380,384},{381,385},{382,3... | collective-permute-start | bytes 983048 | tf_op jit(solution)/shard_map/ppermute | solution.py:18
  7.7 1.0 %reduce-window.9 = s32[3,128]{1,0:T(4,128)S(1)} reduce-window(s32[3,128]{1,0:T(4,128)} %bitcast.6, s32[]{:T(128)} %constant.26.clone.1), window={size=1x128 pad=0_0x127_0}, to_apply=%region_0.0 | reduce-window | flops 48768 | bytes 3076 | tf_op jit(solution)/shard_map/reduce-window
  8.7 0.1 slice.7
  8.8 3.5 %collective-permute-done.refs_3_.refs_9_ = bf16[160,1024]{1,0:T(8,128)(2,1)S(1)} collective-permute-done((bf16[160,1024]{1,0:T(8,128)(2,1)S(1)}, bf16[160,1024]{1,0:T(8,128)(2,1)S(1)}, u32[]{:S(2)}, u32[]{:S(2)}) %collective-permute-start) | collective-permute-done | bytes 327712 | tf_op jit(solution)/shard_map/ppermute | solution.py:18
  12.4 3.2 %collective-permute-start.1 = (bf16[160,1024]{1,0:T(8,128)(2,1)S(1)}, bf16[160,1024]{1,0:T(8,128)(2,1)S(1)}, u32[]{:S(2)}, u32[]{:S(2)}) collective-permute-start(bf16[160,1024]{1,0:T(8,128)(2,1)S(1)} %collective-permute-done.refs_3_.refs_9_), channel_id=1, source_target_pairs={{0,2},{1,3},{2,4},{3,5},{4,6},{5,7},{6,8},{7,9},{8,10},{9,11},{10,... | collective-permute-start | bytes 983048 | tf_op jit(solution)/shard_map/ppermute | solution.py:18
  15.6 0.1 slice_reduce_fusion
  15.7 0.1 add_bitcast_fusion
  15.8 3.7 %collective-permute-start.4 = (bf16[160,1024]{1,0:T(8,128)(2,1)S(1)}, bf16[160,1024]{1,0:T(8,128)(2,1)S(1)}, u32[]{:S(2)}, u32[]{:S(2)}) collective-permute-start(bf16[160,1024]{1,0:T(8,128)(2,1)S(1)} %collective-permute-done.refs_3_.refs_9_), channel_id=1, source_target_pairs={{0,1},{2,3},{4,5},{6,7},{8,9},{10,11},{12,13},{14,15},{16,17},{18,... | collective-permute-start | bytes 983048 | tf_op jit(solution)/shard_map/ppermute | solution.py:18
  19.5 21.0 %collective-permute-done.2 = bf16[160,1024]{1,0:T(8,128)(2,1)S(1)} collective-permute-done((bf16[160,1024]{1,0:T(8,128)(2,1)S(1)}, bf16[160,1024]{1,0:T(8,128)(2,1)S(1)}, u32[]{:S(2)}, u32[]{:S(2)}) %collective-permute-start.2) | collective-permute-done | bytes 327712 | tf_op jit(solution)/shard_map/ppermute | solution.py:18
  40.5 0.0 collective-permute-done.1
  40.5 0.1 add.24.refs_0_.refs_6_
  40.6 0.0 copy-start
  40.6 3.4 %collective-permute-start.3 = (bf16[160,1024]{1,0:T(8,128)(2,1)S(1)}, bf16[160,1024]{1,0:T(8,128)(2,1)S(1)}, u32[]{:S(2)}, u32[]{:S(2)}) collective-permute-start(bf16[160,1024]{1,0:T(8,128)(2,1)S(1)} %add.24.refs_0_.refs_6_), channel_id=1, source_target_pairs={{1,0},{3,2},{5,4},{7,6},{9,8},{11,10},{13,12},{15,14},{17,16},{19,... | collective-permute-start | bytes 983048 | tf_op jit(solution)/shard_map/ppermute | solution.py:18
  44.0 0.0 copy-done.2
  44.0 0.2 select_reduce_fusion
  44.2 0.8 %copy.7.ds_ref = s32[160,1]{1,0:T(8,128)} copy(s32[160,1]{0,1:T(1,128)S(1)} %bitcast.7) | data formatting | bytes 1280 | tf_op jit(solution)/shard_map/broadcast_in_dim | solution.py:135
  45.0 0.6 pad_add_fusion.qs_ref
  45.6 0.0 collective-permute-done.5.refs_4_.refs_10_
  45.6 0.0 collective-permute-done.4.refs_2_.refs_8_
  45.6 0.0 collective-permute-done.3.refs_1_.refs_7_
  45.6 0.0 copy-done.1
  45.6 0.0 copy-done.3
  45.6 0.0 copy-done
  45.6 0.7 %copy-done.4 = bf16[160,1024]{1,0:T(8,128)(2,1)} copy-done((bf16[160,1024]{1,0:T(8,128)(2,1)}, bf16[160,1024]{1,0:T(8,128)(2,1)S(1)}, u32[]{:S(2)}) %copy-start.4) | copy-done | bytes 327704
  46.3 0.2 copy-done.5
  46.4 0.7 %copy-done.6 = bf16[160,1024]{1,0:T(8,128)(2,1)} copy-done((bf16[160,1024]{1,0:T(8,128)(2,1)}, bf16[160,1024]{1,0:T(8,128)(2,1)S(1)}, u32[]{:S(2)}) %copy-start.6) | copy-done | bytes 327704
  47.2 14.5 %shard_map.55 = bf16[160,4096]{1,0:T(8,128)(2,1)} custom-call(s32[2]{0:T(128)} %pad_add_fusion.qs_ref, f32[32]{0:T(128)} %scale_ref.1, s32[160,1]{1,0:T(8,128)} %copy.7.ds_ref, bf16[160,4096]{1,0:T(8,128)(2,1)} %q_ref.1, bf16[160,1024]{1,0:T(8,128)(2,1)} %copy-done, bf16[160,1024]{1,0:T(8,128)(2,1)} %copy-done.6, bf16[160,1024]{1,0:T(8,128)(2,1)} %copy-done.5, ...), custom_call_target="tpu_custom_call" | custom-call | flops 2097152000 | bytes 4259840 | tf_op jit(solution)/shard_map/pallas_call | solution.py:99
  (7 shorter events, 0.1 us)
Async XLA Ops:
  0.0 44.0 %copy-start.2 = (s32[384]{0:T(512)S(1)}, s32[384]{0:T(512)}, u32[]{:S(2)}) copy-start(s32[384]{0:T(512)} %param.8) | copy-start | bytes 4612
  1.9 43.7 %copy-start.1 = (bf16[160,1024]{1,0:T(8,128)(2,1)}, bf16[160,1024]{1,0:T(8,128)(2,1)S(1)}, u32[]{:S(2)}) copy-start(bf16[160,1024]{1,0:T(8,128)(2,1)S(1)} %constant_dynamic-update-slice_fusion.refs_5_.refs_11_) | copy-start | bytes 983044
  1.9 10.5 %collective-permute-start = (bf16[160,1024]{1,0:T(8,128)(2,1)S(1)}, bf16[160,1024]{1,0:T(8,128)(2,1)S(1)}, u32[]{:S(2)}, u32[]{:S(2)}) collective-permute-start(bf16[160,1024]{1,0:T(8,128)(2,1)S(1)} %constant_dynamic-update-slice_fusion.refs_5_.refs_11_), channel_id=1, source_target_pairs={{0,2},{1,3},{2,4},{3,5},{4,6},{5,7},{6,8},{7,9},{8,10},{9,11},{10,... | collective-permute-start | bytes 983048 | tf_op jit(solution)/shard_map/ppermute | solution.py:18
  5.1 40.5 %collective-permute-start.5 = (bf16[160,1024]{1,0:T(8,128)(2,1)S(1)}, bf16[160,1024]{1,0:T(8,128)(2,1)S(1)}, u32[]{:S(2)}, u32[]{:S(2)}) collective-permute-start(bf16[160,1024]{1,0:T(8,128)(2,1)S(1)} %constant_dynamic-update-slice_fusion.refs_5_.refs_11_), channel_id=1, source_target_pairs={{0,1},{2,3},{4,5},{6,7},{8,9},{10,11},{12,13},{14,15},{16,17},{18,... | collective-permute-start | bytes 983048 | tf_op jit(solution)/shard_map/ppermute | solution.py:18
  6.4 34.1 %collective-permute-start.2 = (bf16[160,1024]{1,0:T(8,128)(2,1)S(1)}, bf16[160,1024]{1,0:T(8,128)(2,1)S(1)}, u32[]{:S(2)}, u32[]{:S(2)}) collective-permute-start(bf16[160,1024]{1,0:T(8,128)(2,1)S(1)} %constant_dynamic-update-slice_fusion.refs_5_.refs_11_), channel_id=1, source_target_pairs={{188,192},{189,193},{190,194},{191,195},{380,384},{381,385},{382,3... | collective-permute-start | bytes 983048 | tf_op jit(solution)/shard_map/ppermute | solution.py:18
  12.4 33.2 %copy-start.3 = (bf16[160,1024]{1,0:T(8,128)(2,1)}, bf16[160,1024]{1,0:T(8,128)(2,1)S(1)}, u32[]{:S(2)}) copy-start(bf16[160,1024]{1,0:T(8,128)(2,1)S(1)} %collective-permute-done.refs_3_.refs_9_) | copy-start | bytes 983044
  12.4 28.1 %collective-permute-start.1 = (bf16[160,1024]{1,0:T(8,128)(2,1)S(1)}, bf16[160,1024]{1,0:T(8,128)(2,1)S(1)}, u32[]{:S(2)}, u32[]{:S(2)}) collective-permute-start(bf16[160,1024]{1,0:T(8,128)(2,1)S(1)} %collective-permute-done.refs_3_.refs_9_), channel_id=1, source_target_pairs={{0,2},{1,3},{2,4},{3,5},{4,6},{5,7},{6,8},{7,9},{8,10},{9,11},{10,... | collective-permute-start | bytes 983048 | tf_op jit(solution)/shard_map/ppermute | solution.py:18
  15.8 29.8 %collective-permute-start.4 = (bf16[160,1024]{1,0:T(8,128)(2,1)S(1)}, bf16[160,1024]{1,0:T(8,128)(2,1)S(1)}, u32[]{:S(2)}, u32[]{:S(2)}) collective-permute-start(bf16[160,1024]{1,0:T(8,128)(2,1)S(1)} %collective-permute-done.refs_3_.refs_9_), channel_id=1, source_target_pairs={{0,1},{2,3},{4,5},{6,7},{8,9},{10,11},{12,13},{14,15},{16,17},{18,... | collective-permute-start | bytes 983048 | tf_op jit(solution)/shard_map/ppermute | solution.py:18
  40.6 5.0 %copy-start = (bf16[160,1024]{1,0:T(8,128)(2,1)}, bf16[160,1024]{1,0:T(8,128)(2,1)S(1)}, u32[]{:S(2)}) copy-start(bf16[160,1024]{1,0:T(8,128)(2,1)S(1)} %add.24.refs_0_.refs_6_) | copy-start | bytes 983044
  40.6 5.0 %collective-permute-start.3 = (bf16[160,1024]{1,0:T(8,128)(2,1)S(1)}, bf16[160,1024]{1,0:T(8,128)(2,1)S(1)}, u32[]{:S(2)}, u32[]{:S(2)}) collective-permute-start(bf16[160,1024]{1,0:T(8,128)(2,1)S(1)} %add.24.refs_0_.refs_6_), channel_id=1, source_target_pairs={{1,0},{3,2},{5,4},{7,6},{9,8},{11,10},{13,12},{15,14},{17,16},{19,... | collective-permute-start | bytes 983048 | tf_op jit(solution)/shard_map/ppermute | solution.py:18
  45.6 0.7 %copy-start.4 = (bf16[160,1024]{1,0:T(8,128)(2,1)}, bf16[160,1024]{1,0:T(8,128)(2,1)S(1)}, u32[]{:S(2)}) copy-start(bf16[160,1024]{1,0:T(8,128)(2,1)S(1)} %collective-permute-done.5.refs_4_.refs_10_) | copy-start | bytes 983044
  45.6 0.9 %copy-start.5 = (bf16[160,1024]{1,0:T(8,128)(2,1)}, bf16[160,1024]{1,0:T(8,128)(2,1)S(1)}, u32[]{:S(2)}) copy-start(bf16[160,1024]{1,0:T(8,128)(2,1)S(1)} %collective-permute-done.4.refs_2_.refs_8_) | copy-start | bytes 983044
  46.4 0.7 %copy-start.6 = (bf16[160,1024]{1,0:T(8,128)(2,1)}, bf16[160,1024]{1,0:T(8,128)(2,1)S(1)}, u32[]{:S(2)}) copy-start(bf16[160,1024]{1,0:T(8,128)(2,1)S(1)} %collective-permute-done.3.refs_1_.refs_7_) | copy-start | bytes 983044

commit v13 on v6

--- a/solution.py
+++ b/solution.py
@@ -69,6 +69,7 @@
     row = lax.broadcasted_iota(jnp.int32, (rows, width), 0)
     doc_start = ds_ref[...]
     live = (col >= doc_start - (q_start - doc_most)) & (col <= row + doc_most)
+    bias = jnp.where(live, jnp.float32(0), -jnp.inf)
     k = ordered(kv_refs[:half])
     v = ordered(kv_refs[half:])
     q_pos = q_start + lax.broadcasted_iota(jnp.int32, (rows, 1), 0)
@@ -79,7 +80,7 @@
     )
     q = jnp.concatenate([q_ref[:, g * HD : (g + 1) * HD] for g in range(per_group)], axis=0)
     s = lax.dot_general(q, k, (((1,), (1,)), ((), ())), preferred_element_type=jnp.float32)
-    s = jnp.where(live[None], s.reshape(per_group, rows, width) * coef, -jnp.inf)
+    s = s.reshape(per_group, rows, width) * coef + bias[None]
     m = jnp.max(s, axis=2, keepdims=True)
     p = jnp.exp(s - m)
     l = jnp.sum(p, axis=2, keepdims=True)

time: 58.6 us -> 58.6 us (level)
  no operation moved by 1% of the time
where the time goes in v13:
time: 58.6 us; the launch traced here: 58.3 us
  waiting for transfers between devices  20.1 us (34%)
  starting transfers between devices  17.2 us (29%)
  Pallas kernels  14.4 us (25%)
  local copies, waits for them, and re-layouts  4.41 us (8%)
  other arithmetic  1.97 us (3%)
    ppermute x6, waiting for transfers between devices, send(): return lax.ppermute(x, AXES, pairs)  20.1 us
    ppermute x6, starting transfers between devices, send(): return lax.ppermute(x, AXES, pairs)  17.2 us
    pallas_call x1, Pallas kernels, attend(): pl.pallas_call(attend_kernel, grid=(HK,), in_specs=[pl.BlockSpec(memory_s...  14.4 us
    unnamed x15, local copies, waits for them, and re-layouts  2.52 us
  transfers between devices with their start and end apart: 6, of which 2 were waited for; matrix products, arithmetic and copies ran while one was open for 5% of the time, Pallas kernels for 0%

profile of v13, /device:TPU:15, one launch (start us, length us, event | category | flops | bytes accessed | tf_op | source)
XLA Modules:
  0.0 58.3 jit_solution(12795050676092737782)
XLA Ops:
  0.0 0.9 %constant_dynamic-update-slice_fusion.1 = bf16[160,1024]{1,0:T(8,128)(2,1)S(1)} fusion(bf16[160,512]{1,0:T(8,128)(2,1)} %param.6), kind=kLoop, calls=%fused_computation.2 | loop fusion | bytes 327680
  0.9 0.9 %constant_dynamic-update-slice_fusion.refs_5_.refs_11_ = bf16[160,1024]{1,0:T(8,128)(2,1)S(1)} fusion(bf16[160,1024]{1,0:T(8,128)(2,1)S(1)} %constant_dynamic-update-slice_fusion.1, bf16[160,512]{1,0:T(8,128)(2,1)} %param.7), kind=kLoop, calls=%fused_computation.1 | loop fusion | bytes 327680 | tf_op jit(solution)/shard_map/concatenate | solution.py:130
  1.9 0.0 copy-start.1
  1.9 3.2 %collective-permute-start = (bf16[160,1024]{1,0:T(8,128)(2,1)S(1)}, bf16[160,1024]{1,0:T(8,128)(2,1)S(1)}, u32[]{:S(2)}, u32[]{:S(2)}) collective-permute-start(bf16[160,1024]{1,0:T(8,128)(2,1)S(1)} %constant_dynamic-update-slice_fusion.refs_5_.refs_11_), channel_id=1, source_target_pairs={{0,2},{1,3},{2,4},{3,5},{4,6},{5,7},{6,8},{7,9},{8,10},{9,11},{10,... | collective-permute-start | bytes 983048 | tf_op jit(solution)/shard_map/ppermute | solution.py:18
  5.1 1.3 %collective-permute-start.5 = (bf16[160,1024]{1,0:T(8,128)(2,1)S(1)}, bf16[160,1024]{1,0:T(8,128)(2,1)S(1)}, u32[]{:S(2)}, u32[]{:S(2)}) collective-permute-start(bf16[160,1024]{1,0:T(8,128)(2,1)S(1)} %constant_dynamic-update-slice_fusion.refs_5_.refs_11_), channel_id=1, source_target_pairs={{0,1},{2,3},{4,5},{6,7},{8,9},{10,11},{12,13},{14,15},{16,17},{18,... | collective-permute-start | bytes 983048 | tf_op jit(solution)/shard_map/ppermute | solution.py:18
  6.4 0.7 %collective-permute-start.2 = (bf16[160,1024]{1,0:T(8,128)(2,1)S(1)}, bf16[160,1024]{1,0:T(8,128)(2,1)S(1)}, u32[]{:S(2)}, u32[]{:S(2)}) collective-permute-start(bf16[160,1024]{1,0:T(8,128)(2,1)S(1)} %constant_dynamic-update-slice_fusion.refs_5_.refs_11_), channel_id=1, source_target_pairs={{188,192},{189,193},{380,384},{381,385},{572,576},{573,577}} | collective-permute-start | bytes 983048 | tf_op jit(solution)/shard_map/ppermute | solution.py:18
  7.1 1.0 %reduce-window.9 = s32[3,128]{1,0:T(4,128)S(1)} reduce-window(s32[3,128]{1,0:T(4,128)} %bitcast.6, s32[]{:T(128)} %constant.26.clone.1), window={size=1x128 pad=0_0x127_0}, to_apply=%region_0.0 | reduce-window | flops 48768 | bytes 3076 | tf_op jit(solution)/shard_map/reduce-window
  8.1 0.1 slice.7
  8.2 4.2 %collective-permute-done.refs_3_.refs_9_ = bf16[160,1024]{1,0:T(8,128)(2,1)S(1)} collective-permute-done((bf16[160,1024]{1,0:T(8,128)(2,1)S(1)}, bf16[160,1024]{1,0:T(8,128)(2,1)S(1)}, u32[]{:S(2)}, u32[]{:S(2)}) %collective-permute-start) | collective-permute-done | bytes 327712 | tf_op jit(solution)/shard_map/ppermute | solution.py:18
  12.4 3.2 %collective-permute-start.1 = (bf16[160,1024]{1,0:T(8,128)(2,1)S(1)}, bf16[160,1024]{1,0:T(8,128)(2,1)S(1)}, u32[]{:S(2)}, u32[]{:S(2)}) collective-permute-start(bf16[160,1024]{1,0:T(8,128)(2,1)S(1)} %collective-permute-done.refs_3_.refs_9_), channel_id=1, source_target_pairs={{0,2},{1,3},{2,4},{3,5},{4,6},{5,7},{6,8},{7,9},{8,10},{9,11},{10,... | collective-permute-start | bytes 983048 | tf_op jit(solution)/shard_map/ppermute | solution.py:18
  15.6 0.1 slice_reduce_fusion
  15.7 0.1 add_bitcast_fusion
  15.8 3.7 %collective-permute-start.4 = (bf16[160,1024]{1,0:T(8,128)(2,1)S(1)}, bf16[160,1024]{1,0:T(8,128)(2,1)S(1)}, u32[]{:S(2)}, u32[]{:S(2)}) collective-permute-start(bf16[160,1024]{1,0:T(8,128)(2,1)S(1)} %collective-permute-done.refs_3_.refs_9_), channel_id=1, source_target_pairs={{0,1},{2,3},{4,5},{6,7},{8,9},{10,11},{12,13},{14,15},{16,17},{18,... | collective-permute-start | bytes 983048 | tf_op jit(solution)/shard_map/ppermute | solution.py:18
  19.5 0.0 collective-permute-done.2
  19.5 16.0 %collective-permute-done.1 = bf16[160,1024]{1,0:T(8,128)(2,1)S(1)} collective-permute-done((bf16[160,1024]{1,0:T(8,128)(2,1)S(1)}, bf16[160,1024]{1,0:T(8,128)(2,1)S(1)}, u32[]{:S(2)}, u32[]{:S(2)}) %collective-permute-start.1) | collective-permute-done | bytes 327712 | tf_op jit(solution)/shard_map/ppermute | solution.py:18
  35.5 0.1 add.24.refs_0_.refs_6_
  35.6 0.0 copy-start
  35.6 5.1 %collective-permute-start.3 = (bf16[160,1024]{1,0:T(8,128)(2,1)S(1)}, bf16[160,1024]{1,0:T(8,128)(2,1)S(1)}, u32[]{:S(2)}, u32[]{:S(2)}) collective-permute-start(bf16[160,1024]{1,0:T(8,128)(2,1)S(1)} %add.24.refs_0_.refs_6_), channel_id=1, source_target_pairs={{1,0},{3,2},{5,4},{7,6},{9,8},{11,10},{13,12},{15,14},{17,16},{19,... | collective-permute-start | bytes 983048 | tf_op jit(solution)/shard_map/ppermute | solution.py:18
  40.7 0.0 copy-done.2
  40.7 0.2 select_reduce_fusion
  40.9 0.8 %copy.7.ds_ref = s32[160,1]{1,0:T(8,128)} copy(s32[160,1]{0,1:T(1,128)S(1)} %bitcast.7) | data formatting | bytes 1280 | tf_op jit(solution)/shard_map/broadcast_in_dim | solution.py:136
  41.6 0.6 pad_add_fusion.qs_ref
  42.2 0.0 collective-permute-done.5.refs_4_.refs_10_
  42.2 0.0 collective-permute-done.4.refs_2_.refs_8_
  42.2 0.0 copy-start.5
  42.2 0.0 collective-permute-done.3.refs_1_.refs_7_
  42.3 0.0 copy-done.1
  42.3 0.0 copy-done.3
  42.3 0.7 %copy-done.4 = bf16[160,1024]{1,0:T(8,128)(2,1)} copy-done((bf16[160,1024]{1,0:T(8,128)(2,1)}, bf16[160,1024]{1,0:T(8,128)(2,1)S(1)}, u32[]{:S(2)}) %copy-start.4) | copy-done | bytes 327704
  42.9 0.2 copy-done.5
  43.1 0.7 %copy-done.6 = bf16[160,1024]{1,0:T(8,128)(2,1)} copy-done((bf16[160,1024]{1,0:T(8,128)(2,1)}, bf16[160,1024]{1,0:T(8,128)(2,1)S(1)}, u32[]{:S(2)}) %copy-start.6) | copy-done | bytes 327704
  43.9 14.4 %shard_map.55 = bf16[160,4096]{1,0:T(8,128)(2,1)} custom-call(s32[2]{0:T(128)} %pad_add_fusion.qs_ref, f32[32]{0:T(128)} %scale_ref.1, s32[160,1]{1,0:T(8,128)} %copy.7.ds_ref, bf16[160,4096]{1,0:T(8,128)(2,1)} %q_ref.1, bf16[160,1024]{1,0:T(8,128)(2,1)} %copy-done, bf16[160,1024]{1,0:T(8,128)(2,1)} %copy-done.6, bf16[160,1024]{1,0:T(8,128)(2,1)} %copy-done.5, ...), custom_call_target="tpu_custom_call" | custom-call | flops 2097152000 | bytes 4259840 | tf_op jit(solution)/shard_map/pallas_call | solution.py:100
  (7 shorter events, 0.1 us)
Async XLA Ops:
  0.0 40.7 %copy-start.2 = (s32[384]{0:T(512)S(1)}, s32[384]{0:T(512)}, u32[]{:S(2)}) copy-start(s32[384]{0:T(512)} %param.8) | copy-start | bytes 4612
  1.9 40.4 %copy-start.1 = (bf16[160,1024]{1,0:T(8,128)(2,1)}, bf16[160,1024]{1,0:T(8,128)(2,1)S(1)}, u32[]{:S(2)}) copy-start(bf16[160,1024]{1,0:T(8,128)(2,1)S(1)} %constant_dynamic-update-slice_fusion.refs_5_.refs_11_) | copy-start | bytes 983044
  1.9 10.5 %collective-permute-start = (bf16[160,1024]{1,0:T(8,128)(2,1)S(1)}, bf16[160,1024]{1,0:T(8,128)(2,1)S(1)}, u32[]{:S(2)}, u32[]{:S(2)}) collective-permute-start(bf16[160,1024]{1,0:T(8,128)(2,1)S(1)} %constant_dynamic-update-slice_fusion.refs_5_.refs_11_), channel_id=1, source_target_pairs={{0,2},{1,3},{2,4},{3,5},{4,6},{5,7},{6,8},{7,9},{8,10},{9,11},{10,... | collective-permute-start | bytes 983048 | tf_op jit(solution)/shard_map/ppermute | solution.py:18
  5.1 37.1 %collective-permute-start.5 = (bf16[160,1024]{1,0:T(8,128)(2,1)S(1)}, bf16[160,1024]{1,0:T(8,128)(2,1)S(1)}, u32[]{:S(2)}, u32[]{:S(2)}) collective-permute-start(bf16[160,1024]{1,0:T(8,128)(2,1)S(1)} %constant_dynamic-update-slice_fusion.refs_5_.refs_11_), channel_id=1, source_target_pairs={{0,1},{2,3},{4,5},{6,7},{8,9},{10,11},{12,13},{14,15},{16,17},{18,... | collective-permute-start | bytes 983048 | tf_op jit(solution)/shard_map/ppermute | solution.py:18
  6.4 13.1 %collective-permute-start.2 = (bf16[160,1024]{1,0:T(8,128)(2,1)S(1)}, bf16[160,1024]{1,0:T(8,128)(2,1)S(1)}, u32[]{:S(2)}, u32[]{:S(2)}) collective-permute-start(bf16[160,1024]{1,0:T(8,128)(2,1)S(1)} %constant_dynamic-update-slice_fusion.refs_5_.refs_11_), channel_id=1, source_target_pairs={{188,192},{189,193},{380,384},{381,385},{572,576},{573,577}} | collective-permute-start | bytes 983048 | tf_op jit(solution)/shard_map/ppermute | solution.py:18
  12.4 29.9 %copy-start.3 = (bf16[160,1024]{1,0:T(8,128)(2,1)}, bf16[160,1024]{1,0:T(8,128)(2,1)S(1)}, u32[]{:S(2)}) copy-start(bf16[160,1024]{1,0:T(8,128)(2,1)S(1)} %collective-permute-done.refs_3_.refs_9_) | copy-start | bytes 983044
  12.4 23.1 %collective-permute-start.1 = (bf16[160,1024]{1,0:T(8,128)(2,1)S(1)}, bf16[160,1024]{1,0:T(8,128)(2,1)S(1)}, u32[]{:S(2)}, u32[]{:S(2)}) collective-permute-start(bf16[160,1024]{1,0:T(8,128)(2,1)S(1)} %collective-permute-done.refs_3_.refs_9_), channel_id=1, source_target_pairs={{0,2},{1,3},{2,4},{3,5},{4,6},{5,7},{6,8},{7,9},{8,10},{9,11},{10,... | collective-permute-start | bytes 983048 | tf_op jit(solution)/shard_map/ppermute | solution.py:18
  15.8 26.5 %collective-permute-start.4 = (bf16[160,1024]{1,0:T(8,128)(2,1)S(1)}, bf16[160,1024]{1,0:T(8,128)(2,1)S(1)}, u32[]{:S(2)}, u32[]{:S(2)}) collective-permute-start(bf16[160,1024]{1,0:T(8,128)(2,1)S(1)} %collective-permute-done.refs_3_.refs_9_), channel_id=1, source_target_pairs={{0,1},{2,3},{4,5},{6,7},{8,9},{10,11},{12,13},{14,15},{16,17},{18,... | collective-permute-start | bytes 983048 | tf_op jit(solution)/shard_map/ppermute | solution.py:18
  35.6 6.7 %copy-start = (bf16[160,1024]{1,0:T(8,128)(2,1)}, bf16[160,1024]{1,0:T(8,128)(2,1)S(1)}, u32[]{:S(2)}) copy-start(bf16[160,1024]{1,0:T(8,128)(2,1)S(1)} %add.24.refs_0_.refs_6_) | copy-start | bytes 983044
  35.6 6.7 %collective-permute-start.3 = (bf16[160,1024]{1,0:T(8,128)(2,1)S(1)}, bf16[160,1024]{1,0:T(8,128)(2,1)S(1)}, u32[]{:S(2)}, u32[]{:S(2)}) collective-permute-start(bf16[160,1024]{1,0:T(8,128)(2,1)S(1)} %add.24.refs_0_.refs_6_), channel_id=1, source_target_pairs={{1,0},{3,2},{5,4},{7,6},{9,8},{11,10},{13,12},{15,14},{17,16},{19,... | collective-permute-start | bytes 983048 | tf_op jit(solution)/shard_map/ppermute | solution.py:18
  42.2 0.7 %copy-start.4 = (bf16[160,1024]{1,0:T(8,128)(2,1)}, bf16[160,1024]{1,0:T(8,128)(2,1)S(1)}, u32[]{:S(2)}) copy-start(bf16[160,1024]{1,0:T(8,128)(2,1)S(1)} %collective-permute-done.5.refs_4_.refs_10_) | copy-start | bytes 983044
  42.2 0.9 %copy-start.5 = (bf16[160,1024]{1,0:T(8,128)(2,1)}, bf16[160,1024]{1,0:T(8,128)(2,1)S(1)}, u32[]{:S(2)}) copy-start(bf16[160,1024]{1,0:T(8,128)(2,1)S(1)} %collective-permute-done.4.refs_2_.refs_8_) | copy-start | bytes 983044
  43.1 0.7 %copy-start.6 = (bf16[160,1024]{1,0:T(8,128)(2,1)}, bf16[160,1024]{1,0:T(8,128)(2,1)S(1)}, u32[]{:S(2)}) copy-start(bf16[160,1024]{1,0:T(8,128)(2,1)S(1)} %collective-permute-done.3.refs_1_.refs_7_) | copy-start | bytes 983044

commit v14 on v6

--- a/solution.py
+++ b/solution.py
@@ -11,6 +11,7 @@
 HK = 4
 HD = 128
 WIN_DEV = 4
+SPLIT = 2
 AXES = ("ctx", "grp")
 
 
@@ -56,6 +57,7 @@
     width = rows * (half - 1)
     doc_most = width - rows
     head = pl.program_id(0)
+    part = pl.program_id(1)
     q_start = qs_ref[0]
     even = qs_ref[1] == 0
 
@@ -73,9 +75,9 @@
     v = ordered(kv_refs[half:])
     q_pos = q_start + lax.broadcasted_iota(jnp.int32, (rows, 1), 0)
     logv = jnp.log((q_pos - doc_start + 1).astype(jnp.float32))
-    per_group = HQ // HK
+    per_group = HQ // HK // SPLIT
     coef = jnp.stack(
-        [scale_ref[head * per_group + g] * logv / jnp.sqrt(jnp.float32(HD)) for g in range(per_group)]
+        [scale_ref[(head * SPLIT + part) * per_group + g] * logv / jnp.sqrt(jnp.float32(HD)) for g in range(per_group)]
     )
     q = jnp.concatenate([q_ref[:, g * HD : (g + 1) * HD] for g in range(per_group)], axis=0)
     s = lax.dot_general(q, k, (((1,), (1,)), ((), ())), preferred_element_type=jnp.float32)
@@ -92,22 +94,22 @@
 def attend(queries, blocks, where, scale, doc_start, interpret=False):
     rows = queries.shape[0]
     width = rows * (len(blocks) - 1)
-    per_group = HQ // HK
+    per_group = HQ // HK // SPLIT
     flops = 4 * HQ * rows * width * HD
-    k_specs = [pl.BlockSpec((rows, HD), lambda h: (0, h)) for _ in blocks]
-    v_specs = [pl.BlockSpec((rows, HD), lambda h: (0, h + HK)) for _ in blocks]
+    k_specs = [pl.BlockSpec((rows, HD), lambda h, j: (0, h)) for _ in blocks]
+    v_specs = [pl.BlockSpec((rows, HD), lambda h, j: (0, h + HK)) for _ in blocks]
     return pl.pallas_call(
         attend_kernel,
-        grid=(HK,),
+        grid=(HK, SPLIT),
         in_specs=[
             pl.BlockSpec(memory_space=pltpu.SMEM),
             pl.BlockSpec(memory_space=pltpu.SMEM),
-            pl.BlockSpec((rows, 1), lambda h: (0, 0)),
-            pl.BlockSpec((rows, per_group * HD), lambda h: (0, h)),
+            pl.BlockSpec((rows, 1), lambda h, j: (0, 0)),
+            pl.BlockSpec((rows, per_group * HD), lambda h, j: (0, h * SPLIT + j)),
         ]
         + k_specs
         + v_specs,
-        out_specs=pl.BlockSpec((rows, per_group * HD), lambda h: (0, h)),
+        out_specs=pl.BlockSpec((rows, per_group * HD), lambda h, j: (0, h * SPLIT + j)),
         out_shape=jax.ShapeDtypeStruct((rows, HQ * HD), jnp.bfloat16),
         cost_estimate=pl.CostEstimate(
             flops=flops,

time: 58.6 us -> 60.6 us (1.034)
  Pallas kernels: 14.5 us -> 16.5 us
    pallas_call x1, Pallas kernels: 14.5 us -> 16.5 us  [attend(): pl.pallas_call(attend_kernel, grid=(HK, SPLIT), in_specs=[pl.BlockSpec(me...]
where the time goes in v14:
time: 60.6 us; the launch traced here: 60.3 us
  waiting for transfers between devices  20.1 us (33%)
  starting transfers between devices  17.2 us (28%)
  Pallas kernels  16.5 us (27%)
  local copies, waits for them, and re-layouts  4.41 us (7%)
  other arithmetic  1.97 us (3%)
    ppermute x6, waiting for transfers between devices, send(): return lax.ppermute(x, AXES, pairs)  20.1 us
    ppermute x6, starting transfers between devices, send(): return lax.ppermute(x, AXES, pairs)  17.2 us
    pallas_call x1, Pallas kernels, attend(): pl.pallas_call(attend_kernel, grid=(HK, SPLIT), in_specs=[pl.BlockSpec(me...  16.5 us
    unnamed x15, local copies, waits for them, and re-layouts  2.52 us
  transfers between devices with their start and end apart: 6, of which 2 were waited for; matrix products, arithmetic and copies ran while one was open for 5% of the time, Pallas kernels for 0%

profile of v14, /device:TPU:15, one launch (start us, length us, event | category | flops | bytes accessed | tf_op | source)
XLA Modules:
  0.0 60.3 jit_solution(10737755457167047736)
XLA Ops:
  0.0 0.9 %constant_dynamic-update-slice_fusion.1 = bf16[160,1024]{1,0:T(8,128)(2,1)S(1)} fusion(bf16[160,512]{1,0:T(8,128)(2,1)} %param.6), kind=kLoop, calls=%fused_computation.2 | loop fusion | bytes 327680
  0.9 0.9 %constant_dynamic-update-slice_fusion.refs_5_.refs_11_ = bf16[160,1024]{1,0:T(8,128)(2,1)S(1)} fusion(bf16[160,1024]{1,0:T(8,128)(2,1)S(1)} %constant_dynamic-update-slice_fusion.1, bf16[160,512]{1,0:T(8,128)(2,1)} %param.7), kind=kLoop, calls=%fused_computation.1 | loop fusion | bytes 327680 | tf_op jit(solution)/shard_map/concatenate | solution.py:131
  1.9 0.0 copy-start.1
  1.9 3.2 %collective-permute-start = (bf16[160,1024]{1,0:T(8,128)(2,1)S(1)}, bf16[160,1024]{1,0:T(8,128)(2,1)S(1)}, u32[]{:S(2)}, u32[]{:S(2)}) collective-permute-start(bf16[160,1024]{1,0:T(8,128)(2,1)S(1)} %constant_dynamic-update-slice_fusion.refs_5_.refs_11_), channel_id=1, source_target_pairs={{0,2},{1,3},{2,4},{3,5},{4,6},{5,7},{6,8},{7,9},{8,10},{9,11},{10,... | collective-permute-start | bytes 983048 | tf_op jit(solution)/shard_map/ppermute | solution.py:19
  5.1 1.3 %collective-permute-start.5 = (bf16[160,1024]{1,0:T(8,128)(2,1)S(1)}, bf16[160,1024]{1,0:T(8,128)(2,1)S(1)}, u32[]{:S(2)}, u32[]{:S(2)}) collective-permute-start(bf16[160,1024]{1,0:T(8,128)(2,1)S(1)} %constant_dynamic-update-slice_fusion.refs_5_.refs_11_), channel_id=1, source_target_pairs={{0,1},{2,3},{4,5},{6,7},{8,9},{10,11},{12,13},{14,15},{16,17},{18,... | collective-permute-start | bytes 983048 | tf_op jit(solution)/shard_map/ppermute | solution.py:19
  6.4 0.7 %collective-permute-start.2 = (bf16[160,1024]{1,0:T(8,128)(2,1)S(1)}, bf16[160,1024]{1,0:T(8,128)(2,1)S(1)}, u32[]{:S(2)}, u32[]{:S(2)}) collective-permute-start(bf16[160,1024]{1,0:T(8,128)(2,1)S(1)} %constant_dynamic-update-slice_fusion.refs_5_.refs_11_), channel_id=1, source_target_pairs={{188,192},{189,193},{380,384},{381,385},{572,576},{573,577}} | collective-permute-start | bytes 983048 | tf_op jit(solution)/shard_map/ppermute | solution.py:19
  7.1 1.0 %reduce-window.9 = s32[3,128]{1,0:T(4,128)S(1)} reduce-window(s32[3,128]{1,0:T(4,128)} %bitcast.6, s32[]{:T(128)} %constant.26.clone.1), window={size=1x128 pad=0_0x127_0}, to_apply=%region_0.0 | reduce-window | flops 48768 | bytes 3076 | tf_op jit(solution)/shard_map/reduce-window
  8.1 0.1 slice.7
  8.2 4.2 %collective-permute-done.refs_3_.refs_9_ = bf16[160,1024]{1,0:T(8,128)(2,1)S(1)} collective-permute-done((bf16[160,1024]{1,0:T(8,128)(2,1)S(1)}, bf16[160,1024]{1,0:T(8,128)(2,1)S(1)}, u32[]{:S(2)}, u32[]{:S(2)}) %collective-permute-start) | collective-permute-done | bytes 327712 | tf_op jit(solution)/shard_map/ppermute | solution.py:19
  12.4 3.2 %collective-permute-start.1 = (bf16[160,1024]{1,0:T(8,128)(2,1)S(1)}, bf16[160,1024]{1,0:T(8,128)(2,1)S(1)}, u32[]{:S(2)}, u32[]{:S(2)}) collective-permute-start(bf16[160,1024]{1,0:T(8,128)(2,1)S(1)} %collective-permute-done.refs_3_.refs_9_), channel_id=1, source_target_pairs={{0,2},{1,3},{2,4},{3,5},{4,6},{5,7},{6,8},{7,9},{8,10},{9,11},{10,... | collective-permute-start | bytes 983048 | tf_op jit(solution)/shard_map/ppermute | solution.py:19
  15.6 0.1 slice_reduce_fusion
  15.7 0.1 add_bitcast_fusion
  15.8 3.7 %collective-permute-start.4 = (bf16[160,1024]{1,0:T(8,128)(2,1)S(1)}, bf16[160,1024]{1,0:T(8,128)(2,1)S(1)}, u32[]{:S(2)}, u32[]{:S(2)}) collective-permute-start(bf16[160,1024]{1,0:T(8,128)(2,1)S(1)} %collective-permute-done.refs_3_.refs_9_), channel_id=1, source_target_pairs={{0,1},{2,3},{4,5},{6,7},{8,9},{10,11},{12,13},{14,15},{16,17},{18,... | collective-permute-start | bytes 983048 | tf_op jit(solution)/shard_map/ppermute | solution.py:19
  19.5 0.0 collective-permute-done.2
  19.5 16.0 %collective-permute-done.1 = bf16[160,1024]{1,0:T(8,128)(2,1)S(1)} collective-permute-done((bf16[160,1024]{1,0:T(8,128)(2,1)S(1)}, bf16[160,1024]{1,0:T(8,128)(2,1)S(1)}, u32[]{:S(2)}, u32[]{:S(2)}) %collective-permute-start.1) | collective-permute-done | bytes 327712 | tf_op jit(solution)/shard_map/ppermute | solution.py:19
  35.5 0.1 add.24.refs_0_.refs_6_
  35.6 0.0 copy-start
  35.6 5.1 %collective-permute-start.3 = (bf16[160,1024]{1,0:T(8,128)(2,1)S(1)}, bf16[160,1024]{1,0:T(8,128)(2,1)S(1)}, u32[]{:S(2)}, u32[]{:S(2)}) collective-permute-start(bf16[160,1024]{1,0:T(8,128)(2,1)S(1)} %add.24.refs_0_.refs_6_), channel_id=1, source_target_pairs={{1,0},{3,2},{5,4},{7,6},{9,8},{11,10},{13,12},{15,14},{17,16},{19,... | collective-permute-start | bytes 983048 | tf_op jit(solution)/shard_map/ppermute | solution.py:19
  40.7 0.0 copy-done.2
  40.7 0.2 select_reduce_fusion
  40.9 0.8 %copy.7.ds_ref = s32[160,1]{1,0:T(8,128)} copy(s32[160,1]{0,1:T(1,128)S(1)} %bitcast.7) | data formatting | bytes 1280 | tf_op jit(solution)/shard_map/broadcast_in_dim | solution.py:137
  41.6 0.6 pad_add_fusion.qs_ref
  42.2 0.0 collective-permute-done.5.refs_4_.refs_10_
  42.2 0.0 collective-permute-done.4.refs_2_.refs_8_
  42.2 0.0 collective-permute-done.3.refs_1_.refs_7_
  42.3 0.0 copy-done.1
  42.3 0.0 copy-done.3
  42.3 0.0 copy-done
  42.3 0.7 %copy-done.4 = bf16[160,1024]{1,0:T(8,128)(2,1)} copy-done((bf16[160,1024]{1,0:T(8,128)(2,1)}, bf16[160,1024]{1,0:T(8,128)(2,1)S(1)}, u32[]{:S(2)}) %copy-start.4) | copy-done | bytes 327704
  42.9 0.2 copy-done.5
  43.1 0.7 %copy-done.6 = bf16[160,1024]{1,0:T(8,128)(2,1)} copy-done((bf16[160,1024]{1,0:T(8,128)(2,1)}, bf16[160,1024]{1,0:T(8,128)(2,1)S(1)}, u32[]{:S(2)}) %copy-start.6) | copy-done | bytes 327704
  43.9 16.5 %shard_map.55 = bf16[160,4096]{1,0:T(8,128)(2,1)} custom-call(s32[2]{0:T(128)} %pad_add_fusion.qs_ref, f32[32]{0:T(128)} %scale_ref.1, s32[160,1]{1,0:T(8,128)} %copy.7.ds_ref, bf16[160,4096]{1,0:T(8,128)(2,1)} %q_ref.1, bf16[160,1024]{1,0:T(8,128)(2,1)} %copy-done, bf16[160,1024]{1,0:T(8,128)(2,1)} %copy-done.6, bf16[160,1024]{1,0:T(8,128)(2,1)} %copy-done.5, ...), custom_call_target="tpu_custom_call" | custom-call | flops 2097152000 | bytes 4259840 | tf_op jit(solution)/shard_map/pallas_call | solution.py:101
  (7 shorter events, 0.1 us)
Async XLA Ops:
  0.0 40.7 %copy-start.2 = (s32[384]{0:T(512)S(1)}, s32[384]{0:T(512)}, u32[]{:S(2)}) copy-start(s32[384]{0:T(512)} %param.8) | copy-start | bytes 4612
  1.9 40.4 %copy-start.1 = (bf16[160,1024]{1,0:T(8,128)(2,1)}, bf16[160,1024]{1,0:T(8,128)(2,1)S(1)}, u32[]{:S(2)}) copy-start(bf16[160,1024]{1,0:T(8,128)(2,1)S(1)} %constant_dynamic-update-slice_fusion.refs_5_.refs_11_) | copy-start | bytes 983044
  1.9 10.5 %collective-permute-start = (bf16[160,1024]{1,0:T(8,128)(2,1)S(1)}, bf16[160,1024]{1,0:T(8,128)(2,1)S(1)}, u32[]{:S(2)}, u32[]{:S(2)}) collective-permute-start(bf16[160,1024]{1,0:T(8,128)(2,1)S(1)} %constant_dynamic-update-slice_fusion.refs_5_.refs_11_), channel_id=1, source_target_pairs={{0,2},{1,3},{2,4},{3,5},{4,6},{5,7},{6,8},{7,9},{8,10},{9,11},{10,... | collective-permute-start | bytes 983048 | tf_op jit(solution)/shard_map/ppermute | solution.py:19
  5.1 37.1 %collective-permute-start.5 = (bf16[160,1024]{1,0:T(8,128)(2,1)S(1)}, bf16[160,1024]{1,0:T(8,128)(2,1)S(1)}, u32[]{:S(2)}, u32[]{:S(2)}) collective-permute-start(bf16[160,1024]{1,0:T(8,128)(2,1)S(1)} %constant_dynamic-update-slice_fusion.refs_5_.refs_11_), channel_id=1, source_target_pairs={{0,1},{2,3},{4,5},{6,7},{8,9},{10,11},{12,13},{14,15},{16,17},{18,... | collective-permute-start | bytes 983048 | tf_op jit(solution)/shard_map/ppermute | solution.py:19
  6.4 13.1 %collective-permute-start.2 = (bf16[160,1024]{1,0:T(8,128)(2,1)S(1)}, bf16[160,1024]{1,0:T(8,128)(2,1)S(1)}, u32[]{:S(2)}, u32[]{:S(2)}) collective-permute-start(bf16[160,1024]{1,0:T(8,128)(2,1)S(1)} %constant_dynamic-update-slice_fusion.refs_5_.refs_11_), channel_id=1, source_target_pairs={{188,192},{189,193},{380,384},{381,385},{572,576},{573,577}} | collective-permute-start | bytes 983048 | tf_op jit(solution)/shard_map/ppermute | solution.py:19
  12.4 29.9 %copy-start.3 = (bf16[160,1024]{1,0:T(8,128)(2,1)}, bf16[160,1024]{1,0:T(8,128)(2,1)S(1)}, u32[]{:S(2)}) copy-start(bf16[160,1024]{1,0:T(8,128)(2,1)S(1)} %collective-permute-done.refs_3_.refs_9_) | copy-start | bytes 983044
  12.4 23.1 %collective-permute-start.1 = (bf16[160,1024]{1,0:T(8,128)(2,1)S(1)}, bf16[160,1024]{1,0:T(8,128)(2,1)S(1)}, u32[]{:S(2)}, u32[]{:S(2)}) collective-permute-start(bf16[160,1024]{1,0:T(8,128)(2,1)S(1)} %collective-permute-done.refs_3_.refs_9_), channel_id=1, source_target_pairs={{0,2},{1,3},{2,4},{3,5},{4,6},{5,7},{6,8},{7,9},{8,10},{9,11},{10,... | collective-permute-start | bytes 983048 | tf_op jit(solution)/shard_map/ppermute | solution.py:19
  15.8 26.5 %collective-permute-start.4 = (bf16[160,1024]{1,0:T(8,128)(2,1)S(1)}, bf16[160,1024]{1,0:T(8,128)(2,1)S(1)}, u32[]{:S(2)}, u32[]{:S(2)}) collective-permute-start(bf16[160,1024]{1,0:T(8,128)(2,1)S(1)} %collective-permute-done.refs_3_.refs_9_), channel_id=1, source_target_pairs={{0,1},{2,3},{4,5},{6,7},{8,9},{10,11},{12,13},{14,15},{16,17},{18,... | collective-permute-start | bytes 983048 | tf_op jit(solution)/shard_map/ppermute | solution.py:19
  35.6 6.7 %copy-start = (bf16[160,1024]{1,0:T(8,128)(2,1)}, bf16[160,1024]{1,0:T(8,128)(2,1)S(1)}, u32[]{:S(2)}) copy-start(bf16[160,1024]{1,0:T(8,128)(2,1)S(1)} %add.24.refs_0_.refs_6_) | copy-start | bytes 983044
  35.6 6.7 %collective-permute-start.3 = (bf16[160,1024]{1,0:T(8,128)(2,1)S(1)}, bf16[160,1024]{1,0:T(8,128)(2,1)S(1)}, u32[]{:S(2)}, u32[]{:S(2)}) collective-permute-start(bf16[160,1024]{1,0:T(8,128)(2,1)S(1)} %add.24.refs_0_.refs_6_), channel_id=1, source_target_pairs={{1,0},{3,2},{5,4},{7,6},{9,8},{11,10},{13,12},{15,14},{17,16},{19,... | collective-permute-start | bytes 983048 | tf_op jit(solution)/shard_map/ppermute | solution.py:19
  42.2 0.7 %copy-start.4 = (bf16[160,1024]{1,0:T(8,128)(2,1)}, bf16[160,1024]{1,0:T(8,128)(2,1)S(1)}, u32[]{:S(2)}) copy-start(bf16[160,1024]{1,0:T(8,128)(2,1)S(1)} %collective-permute-done.5.refs_4_.refs_10_) | copy-start | bytes 983044
  42.2 0.9 %copy-start.5 = (bf16[160,1024]{1,0:T(8,128)(2,1)}, bf16[160,1024]{1,0:T(8,128)(2,1)S(1)}, u32[]{:S(2)}) copy-start(bf16[160,1024]{1,0:T(8,128)(2,1)S(1)} %collective-permute-done.4.refs_2_.refs_8_) | copy-start | bytes 983044
  43.1 0.7 %copy-start.6 = (bf16[160,1024]{1,0:T(8,128)(2,1)}, bf16[160,1024]{1,0:T(8,128)(2,1)S(1)}, u32[]{:S(2)}) copy-start(bf16[160,1024]{1,0:T(8,128)(2,1)S(1)} %collective-permute-done.3.refs_1_.refs_7_) | copy-start | bytes 983044
